TPU v7x, 256 devices: a whole 4x4x8 slice. The times are simulated.
256 devices in a mesh: gx: 32 (over z, y_lo, core), gy: 8 (over y_hi, x).
Axes of the slice: x: 4, y: 4 (y_hi: 2, y_lo: 2; y = y_hi * 2 + y_lo), z: 8, core: 2. Of those that a mesh axis runs over, the one named last changes fastest.
Arguments:
- state: bfloat16 [4, 2, 4096, 4096], P(None, None, 'gx', 'gy'), may hold values from -6 to 6
- heights: int32 [4096, 4096], P('gx', 'gy'), may hold values from 0 to 1
- surface_flag: int32 [4096, 4096], P('gx', 'gy'), may hold values 0 or 1
Outputs:
- tendency: bfloat16 [4, 2, 4096, 4096], P(None, None, 'gx', 'gy')
- spectrum: float32 [2, 2, 4096, 4096], P(None, None, ('gx', 'gy'))
All inputs are finite; a program needn't handle non-finite values. No bound on the sum of `surface_flag` on one device may be relied on, other than what follows from the above.
Results may differ from a plain program's by a relative error of at most 0.002.
Values may be sent and summed in bfloat16 or wider, within the bound.
No kernel may reach another device: no remote copies, remote signals or barrier semaphores. Data moves between devices by JAX's collectives and lax.ppermute only.
A program may use at most 64 MiB of HBM per device.

v0:
```python
import math

import numpy as np
import jax
import jax.numpy as jnp
from jax import lax
from jax.sharding import PartitionSpec as P

NU = 0.1
BETA = 0.5
HEAT = 1.0
DT = 0.5
PREC = lax.Precision.HIGH


def ring(count):
    up = [(i, (i + 1) % count) for i in range(count)]
    down = [(j, i) for i, j in up]
    return up, down


def raised(field):
    zero = jnp.zeros_like(field[:1])
    return jnp.concatenate([field[1:], zero], axis=0)


def lowered(field):
    zero = jnp.zeros_like(field[:1])
    return jnp.concatenate([zero, field[:-1]], axis=0)


def tendency_one(component, field, pick, center, fluid, surface):
    slope_x = (
        45.0 * (pick(1, 0) - pick(-1, 0))
        - 9.0 * (pick(2, 0) - pick(-2, 0))
        + (pick(3, 0) - pick(-3, 0))
    ) / 60.0
    slope_y = (
        45.0 * (pick(0, 1) - pick(0, -1))
        - 9.0 * (pick(0, 2) - pick(0, -2))
        + (pick(0, 3) - pick(0, -3))
    ) / 60.0
    above = raised(field)
    below = lowered(field)
    slope_z = (above - below) * 0.5
    advect = center[0] * slope_x + center[1] * slope_y + center[2] * slope_z
    spread = (
        pick(1, 0)
        + pick(-1, 0)
        + pick(0, 1)
        + pick(0, -1)
        - 4.0 * field
        + (above + below - 2.0 * field)
    )
    result = NU * spread - advect
    if component == 2:
        result = result + BETA * center[3]
    if component == 3:
        result = result + HEAT * surface
    return fluid * result


def cos_sin(rows, cols, length, scale=1.0):
    product = (np.arange(rows)[:, None] * np.arange(cols)[None, :]) % length
    angle = product * (2.0 * math.pi / length)
    return np.cos(angle) * scale, np.sin(angle) * scale


def const(array):
    return jnp.asarray(np.asarray(array, dtype=np.float32))


def y_tables(n_p, n_q):
    c1, s1 = cos_sin(n_p, n_p, n_p)
    w1 = np.concatenate([c1, -s1], axis=0)
    t_c, t_s = cos_sin(n_p, n_q, n_p * n_q)
    c2, s2 = cos_sin(n_q, n_q, n_q)
    w2 = np.zeros((n_q, 2, 2, n_q))
    w2[:, 0, 0] = c2
    w2[:, 0, 1] = s2
    w2[:, 1, 0] = -s2
    w2[:, 1, 1] = c2
    return w1, t_c, t_s, w2.reshape(2 * n_q, 2 * n_q)


def x_tables(n_s, n_i, scale):
    c2, s2 = cos_sin(n_s, n_s, n_s)
    wa = np.zeros((n_s, 2, 2, n_s))
    wa[:, 0, 0] = c2
    wa[:, 1, 0] = s2
    wa[:, 0, 1] = -s2
    wa[:, 1, 1] = c2
    t_c, t_s = cos_sin(n_i, n_s, n_s * n_i)
    cb, sb = cos_sin(n_i, n_i, n_i, scale)
    wb = np.zeros((2, n_i, 2, n_i))
    wb[0, :, 0] = cb
    wb[0, :, 1] = sb
    wb[1, :, 0] = -sb
    wb[1, :, 1] = cb
    return wa.reshape(2 * n_s, 2 * n_s), t_c, t_s, wb.reshape(2 * n_i, 2 * n_i)


def body(state, heights, surface_flag):
    levels = state.shape[1]
    rows_x = state.shape[2]
    rows_y = state.shape[3]
    count_x = lax.axis_size("gx")
    count_y = lax.axis_size("gy")
    up_x, down_x = ring(count_x)
    up_y, down_y = ring(count_y)

    level = lax.broadcasted_iota(jnp.int32, state.shape[1:], 0)
    fluid = (level >= heights[None]).astype(jnp.float32)
    surface = (level == heights[None]).astype(jnp.float32) * surface_flag[None].astype(jnp.float32)
    masked = state * fluid.astype(jnp.bfloat16)[None]

    x_before = lax.ppermute(masked[:, :, rows_x - 3 :, :], "gx", up_x)
    x_after = lax.ppermute(masked[:, :, :3, :], "gx", down_x)
    y_before = lax.ppermute(masked[:, :, :, rows_y - 3 :], "gy", up_y)
    y_after = lax.ppermute(masked[:, :, :, :3], "gy", down_y)
    pad_x = jnp.concatenate([x_before, masked, x_after], axis=2).astype(jnp.float32)
    pad_y = jnp.concatenate([y_before, masked, y_after], axis=3).astype(jnp.float32)
    center = masked.astype(jnp.float32)

    pieces = []
    for component in range(4):

        def pick(step_x, step_y, component=component):
            if step_y == 0:
                return pad_x[component, :, 3 + step_x : 3 + step_x + rows_x, :]
            return pad_y[component, :, :, 3 + step_y : 3 + step_y + rows_y]

        pieces.append(
            tendency_one(component, center[component], pick, center, fluid, surface).astype(
                jnp.bfloat16
            )
        )
    tendency = jnp.stack(pieces)

    star = center[:3] + DT * tendency[:3].astype(jnp.float32)
    flow_u, flow_v, flow_w = star[0], star[1], star[2]
    u_before = lax.ppermute(flow_u[:, rows_x - 1 :, :], "gx", up_x)
    u_after = lax.ppermute(flow_u[:, :1, :], "gx", down_x)
    v_before = lax.ppermute(flow_v[:, :, rows_y - 1 :], "gy", up_y)
    v_after = lax.ppermute(flow_v[:, :, :1], "gy", down_y)
    u_next = jnp.concatenate([flow_u[:, 1:, :], u_after], axis=1)
    u_prev = jnp.concatenate([u_before, flow_u[:, :-1, :]], axis=1)
    v_next = jnp.concatenate([flow_v[:, :, 1:], v_after], axis=2)
    v_prev = jnp.concatenate([v_before, flow_v[:, :, :-1]], axis=2)
    diverge = ((u_next - u_prev) + (v_next - v_prev) + (raised(flow_w) - lowered(flow_w))) * 0.5

    total_y = rows_y * count_y
    n_q = 256
    n_p = total_y // n_q
    split_y = rows_y // n_q
    piece_x = rows_x // count_y
    sent = diverge.reshape(levels, rows_x, split_y, n_q).transpose(0, 2, 1, 3)
    columns = lax.all_to_all(sent, "gy", split_axis=2, concat_axis=1, tiled=True)
    w1, t1c, t1s, w2 = y_tables(n_p, n_q)
    w1b = jnp.broadcast_to(const(w1)[None], (levels,) + w1.shape)
    stage1 = lax.dot_general(
        w1b, columns, (((2,), (1,)), ((0,), (0,))), precision=PREC
    )
    real1 = stage1[:, :n_p]
    imag1 = stage1[:, n_p:]
    tc = const(t1c)[None, :, None, :]
    ts = const(t1s)[None, :, None, :]
    real_t = real1 * tc + imag1 * ts
    imag_t = imag1 * tc - real1 * ts
    rows_m = levels * n_p * piece_x
    joined = jnp.concatenate(
        [real_t.reshape(rows_m, n_q), imag_t.reshape(rows_m, n_q)], axis=1
    )
    spectrum_y = lax.dot_general(
        const(w2), joined, (((1,), (1,)), ((), ())), precision=PREC
    )
    devices = count_x * count_y
    spectrum_y = spectrum_y.reshape(devices, 2, rows_m)
    moved = lax.all_to_all(spectrum_y, ("gx", "gy"), split_axis=0, concat_axis=0, tiled=True)

    total_x = rows_x * count_x
    n_s = devices
    n_i = piece_x
    scale = 1.0 / math.sqrt(total_x * total_y)
    wa, t2c, t2s, wb = x_tables(n_s, n_i, scale)
    stage_a = lax.dot_general(
        moved.reshape(2 * n_s, rows_m), const(wa), (((0,), (0,)), ((), ())), precision=PREC
    )
    batch = levels * n_p
    stage_a = stage_a.reshape(batch, n_i, 2 * n_s)
    real_a = stage_a[:, :, :n_s]
    imag_a = stage_a[:, :, n_s:]
    uc = const(t2c)[None]
    us = const(t2s)[None]
    real_b = real_a * uc + imag_a * us
    imag_b = imag_a * uc - real_a * us
    joined_x = jnp.concatenate([real_b, imag_b], axis=1)
    wbb = jnp.broadcast_to(const(wb)[None], (batch,) + wb.shape)
    result = lax.dot_general(
        wbb, joined_x, (((2,), (1,)), ((0,), (0,))), precision=PREC
    )
    result = result.reshape(levels, n_p, 2, n_i, n_s).transpose(2, 0, 1, 3, 4)
    spectrum = result.reshape(2, levels, n_p, total_x)
    return (tendency, spectrum)


def solution(mesh):
    return jax.shard_map(
        body,
        mesh=mesh,
        in_specs=(P(None, None, "gx", "gy"), P("gx", "gy"), P("gx", "gy")),
        out_specs=(P(None, None, "gx", "gy"), P(None, None, ("gx", "gy"), None)),
        check_vma=False,
    )
```

profile of v0, /device:TPU:1, one launch (start us, length us, event | category | flops | bytes accessed | tf_op | source)
XLA Modules:
  0.0 116.2 jit_solution(16217143777396639404)
XLA Ops:
  0.6 2.3 %copy.31 = bf16[4,2,128,512]{2,3,1,0:T(8,128)(2,1)} copy(bf16[4,2,128,512]{3,2,1,0:T(8,128)(2,1)} %param.11) | data formatting | bytes 2097152 | tf_op args[0]
  2.9 0.1 copy.30
  3.1 0.1 convert_convert_fusion
  3.2 1.4 %fusion.117 = (f32[4,2,128,512]{2,3,1,0:T(8,128)S(1)}, bf16[4,2,128,512]{2,3,1,0:T(8,128)(2,1)S(1)}) fusion(bf16[4,2,128,512]{2,3,1,0:T(8,128)(2,1)} %copy.31, bf16[2,128,512]{1,2,0:T(8,128)(2,1)S(1)} %convert_convert_fusion), kind=kLoop, calls=%fused_computation.184 | loop fusion | flops 1048576 | bytes 4456448 | tf_op jit(solution)/shard_map/convert_element_type | solution.py:123
  4.6 6.0 %collective-permute-start.3 = (bf16[4,2,128,3]{2,3,1,0:T(4,128)(2,1)S(1)}, bf16[4,2,128,3]{2,3,1,0:T(4,128)(2,1)S(1)}, u32[]{:S(2)}, u32[]{:S(2)}) collective-permute-start(bf16[4,2,128,3]{2,3,1,0:T(4,128)(2,1)S(1)} %get-tuple-element.27), channel_id=1, source_target_pairs={{1,0},{2,1},{3,2},{4,3},{5,4},{6,5},{7,6},{0,7},{9,8},{10,9},{11,1... | collective-permute-start | bytes 18440 | tf_op jit(solution)/shard_map/ppermute | solution.py:120
  10.6 1.7 %fusion.118 = (bf16[4,2,3,512]{2,3,1,0:T(8,128)(2,1)}, bf16[4,2,3,512]{2,3,1,0:T(8,128)(2,1)}) fusion(bf16[4,2,128,512]{2,3,1,0:T(8,128)(2,1)S(1)} %get-tuple-element.7), kind=kLoop, calls=%fused_computation.185 | loop fusion | bytes 98304 | tf_op jit(solution)/shard_map/slice | solution.py:117
  12.3 1.6 %copy.33 = bf16[4,2,3,512]{3,0,2,1:T(4,128)(2,1)S(1)} copy(bf16[4,2,3,512]{2,3,1,0:T(8,128)(2,1)} %get-tuple-element.25) | data formatting | bytes 49152 | tf_op jit(solution)/shard_map/slice | solution.py:118
  13.9 1.0 collective-permute-start.1
  15.0 1.6 %copy.32 = bf16[4,2,3,512]{3,0,2,1:T(4,128)(2,1)S(1)} copy(bf16[4,2,3,512]{2,3,1,0:T(8,128)(2,1)} %get-tuple-element.24) | data formatting | bytes 49152 | tf_op jit(solution)/shard_map/slice | solution.py:117
  16.6 0.9 collective-permute-start
  17.4 1.4 %slice_bitcast_fusion.21 = (f32[1,128,512]{1,2,0:T(8,128)}, f32[1,128,512]{1,2,0:T(8,128)}, f32[1,128,512]{1,2,0:T(8,128)}, f32[1,128,512]{1,2,0:T(8,128)}, f32[...) fusion(f32[4,2,128,512]{2,3,1,0:T(8,128)S(1)} %get-tuple-element.6), kind=kLoop, calls=%fused_computation.174 | loop fusion | bytes 4194304 | tf_op jit(solution)/shard_map/slice | solution.py:24
  18.9 0.2 maximum_convert_fusion.1
  19.1 1.4 %copy.35 = bf16[4,2,3,512]{2,3,1,0:T(8,128)(2,1)} copy(bf16[4,2,3,512]{3,0,2,1:T(4,128)(2,1)S(1)} %collective-permute-done.1) | data formatting | bytes 49152 | tf_op jit(solution)/shard_map/ppermute | solution.py:118
  20.5 1.9 %collective-permute-done = bf16[4,2,3,512]{3,0,2,1:T(4,128)(2,1)S(1)} collective-permute-done((bf16[4,2,3,512]{3,0,2,1:T(4,128)(2,1)S(1)}, bf16[4,2,3,512]{3,0,2,1:T(4,128)(2,1)S(1)}, u32[]{:S(2)}, u32[]{:S(2)}) %collective-permute-start) | collective-permute-done | bytes 24608 | tf_op jit(solution)/shard_map/ppermute | solution.py:117
  22.5 1.4 %copy.34 = bf16[4,2,3,512]{2,3,1,0:T(8,128)(2,1)} copy(bf16[4,2,3,512]{3,0,2,1:T(4,128)(2,1)S(1)} %collective-permute-done) | data formatting | bytes 49152 | tf_op jit(solution)/shard_map/ppermute | solution.py:117
  23.8 2.8 %maximum_convert_fusion = f32[4,2,134,512]{2,3,1,0:T(8,128)S(1)} fusion(bf16[4,2,3,512]{2,3,1,0:T(8,128)(2,1)} %copy.35, bf16[4,2,128,512]{2,3,1,0:T(8,128)(2,1)S(1)} %get-tuple-element.7, bf16[4,2,3,512]{2,3,1,0:T(8,128)(2,1)} %copy.34), kind=kLoop, calls=%fused_computation | loop fusion | flops 3293184 | bytes 3293184 | tf_op jit(solution)/shard_map/convert_element_type | solution.py:121
  26.7 1.0 fusion.111
  27.7 0.2 copy-done.11
  27.9 0.3 copy-done.12
  28.1 0.9 fusion.109
  29.1 0.2 copy-done.9
  29.3 0.1 copy-done.10
  29.4 0.9 fusion.110
  30.3 0.2 slice_add_fusion
  30.5 0.1 slice_bitcast_fusion
  30.6 0.5 copy-done.7
  31.0 0.2 fusion.122
  31.2 0.2 fusion.123
  31.5 0.1 fusion.121
  31.5 4.7 %collective-permute-start.4 = (f32[2,1,512]{1,2,0:T(8,128)S(1)}, f32[2,1,512]{1,2,0:T(8,128)S(1)}, u32[]{:S(2)}, u32[]{:S(2)}) collective-permute-start(f32[2,1,512]{1,2,0:T(8,128)S(1)} %get-tuple-element.33), channel_id=1, source_target_pairs={{8,0},{16,8},{24,16},{32,24},{40,32},{48,40},{56,48},{64,56},{72,6... | collective-permute-start | bytes 12296 | tf_op jit(solution)/shard_map/ppermute | solution.py:143
  36.3 5.7 %collective-permute-start.6 = (f32[2,128,1]{1,2,0:T(1,128)S(1)}, f32[2,128,1]{1,2,0:T(1,128)S(1)}, u32[]{:S(2)}, u32[]{:S(2)}) collective-permute-start(f32[2,128,1]{1,2,0:T(1,128)S(1)} %get-tuple-element.29), channel_id=1, source_target_pairs={{1,0},{2,1},{3,2},{4,3},{5,4},{6,5},{7,6},{0,7},{9,8},{10,9},{11,1... | collective-permute-start | bytes 3080 | tf_op jit(solution)/shard_map/ppermute | solution.py:145
  42.0 0.7 collective-permute-done.6
  42.7 5.3 %collective-permute-done.7 = f32[2,128,1]{1,2,0:T(1,128)S(1)} collective-permute-done((f32[2,128,1]{1,2,0:T(1,128)S(1)}, f32[2,128,1]{1,2,0:T(1,128)S(1)}, u32[]{:S(2)}, u32[]{:S(2)}) %collective-permute-start.7) | collective-permute-done | bytes 1056 | tf_op jit(solution)/shard_map/ppermute | solution.py:144
  48.0 0.3 fusion.101
  48.4 0.3 copy.37
  48.6 0.0 copy-start.21
  48.6 12.3 %all_to_all.23 = f32[2,2,128,256]{3,1,0,2:T(2,128)S(1)} all-to-all(f32[2,2,128,256]{3,1,0,2:T(2,128)S(1)} %copy.37), channel_id=1, replica_groups=mesh['gx'=32,'gy'=8] {'gy'}, dimensions={2} | all-to-all | bytes 1048576 | tf_op jit(solution)/shard_map/all_to_all | solution.py:158
  60.9 0.1 copy.38
  61.1 0.4 copy.39
  61.5 0.4 all_to_all.19
  61.8 0.6 fusion.113
  62.5 0.0 copy-start.16
  62.5 0.2 multiply_subtract_fusion.1
  62.7 0.0 copy-start.15
  62.7 0.3 copy.40
  63.0 0.3 copy.41
  63.3 0.2 copy-done.16
  63.5 0.6 fusion.124
  64.2 0.6 fusion
  64.8 1.6 %reshape.117 = f32[256,2,512]{2,1,0:T(2,128)} reshape(f32[512,512]{1,0:T(8,128)S(1)} %fusion) | data formatting | bytes 2097152 | tf_op jit(solution)/shard_map/reshape | solution.py:178
  66.4 12.7 %all-to-all-start.1 = ((f32[256,2,512]{2,1,0:T(2,128)}), f32[256,2,512]{2,1,0:T(2,128)S(1)}, u32[]{:S(2)}, u32[]{:S(2)}) async-start(f32[256,2,512]{2,1,0:T(2,128)} %reshape.117), calls=%async_computation.1 | async-start | bytes 2097152 | tf_op jit(solution)/shard_map/all_to_all | solution.py:179
  79.0 1.7 %convert_element_type.51 = f32[128,512]{1,0:T(8,128)} convert(s32[128,512]{1,0:T(8,128)} %param.13) | non-fusion elementwise | flops 65536 | bytes 524288 | tf_op jit(solution)/shard_map/convert_element_type | solution.py:114
  80.7 1.8 %copy.36 = f32[128,512]{0,1:T(8,128)} copy(f32[128,512]{1,0:T(8,128)} %convert_element_type.51) | data formatting | bytes 524288 | tf_op jit(solution)/shard_map/convert_element_type | solution.py:114
  82.5 4.8 %fusion.112 = bf16[1,2,128,512]{2,3,1,0:T(8,128)(2,1)S(1)} fusion(f32[128,512]{0,1:T(8,128)} %copy.36, f32[4,2,128,512]{2,3,1,0:T(8,128)} %copy-done, f32[4,2,128,518]{2,3,1,0:T(8,128)S(1)} %maximum_convert_fusion.1, f32[4,2,134,512]{2,3,1,0:T(8,128)} %copy-done.2, f32[1,128,512]{1,2,0:T(8,128)} %get-tuple-element.9, f32[1,128,512]{1,2,0:T(8,128)} %get-tuple-element.10, ...), kind=kLoop, calls=%fused_computation.179 | loop fusion | flops 5242880 | bytes 9699328 | tf_op jit(solution)/shard_map/stack | solution.py:138
  87.3 0.1 pad_maximum_fusion
  87.4 1.3 %copy.44 = bf16[4,2,128,512]{3,2,1,0:T(8,128)(2,1)} copy(bf16[4,2,128,512]{2,3,1,0:T(8,128)(2,1)S(1)} %pad_maximum_fusion) | data formatting | bytes 2097152
  88.7 21.1 %all-to-all-done.1 = f32[256,2,512]{2,1,0:T(2,128)S(1)} async-done(((f32[256,2,512]{2,1,0:T(2,128)}), f32[256,2,512]{2,1,0:T(2,128)S(1)}, u32[]{:S(2)}, u32[]{:S(2)}) %all-to-all-start.1) | async-done | bytes 1048608 | tf_op jit(solution)/shard_map/all_to_all | solution.py:179
  109.8 0.7 reshape.118
  110.6 0.3 copy.42
  110.9 2.2 %fusion.125 = f32[32,16,512]{2,1,0:T(8,128)S(1)} fusion(f32[32,16,512]{2,1,0:T(8,128)S(1)} %bitcast.321, f32[512,512,1]{1,0,2:T(8,128)} %constant.70), kind=kOutput, calls=%fused_computation.192 | convolution fusion | flops 805306368 | bytes 3145728 | tf_op jit(solution)/shard_map/dot_general | solution.py:186
  113.2 0.2 multiply_add_fusion
  113.3 0.6 fusion.1
  113.9 0.7 reshape.139
  114.6 1.6 %copy.46 = f32[2,2,16,4096]{3,2,1,0:T(8,128)} copy(f32[2,2,16,4096]{3,0,2,1:T(2,128)S(1)} %reshape.139) | data formatting | bytes 2097152 | tf_op jit(solution)/shard_map/reshape | solution.py:203
  (46 shorter events, 0.1 us)
Async XLA Ops:
  0.6 2.3 %copy-start.17 = (s32[128,512]{1,0:T(8,128)S(1)}, s32[128,512]{1,0:T(8,128)}, u32[]{:S(2)}) copy-start(s32[128,512]{1,0:T(8,128)} %param.12) | copy-start | bytes 786436
  4.6 12.8 %copy-start = (f32[4,2,128,512]{2,3,1,0:T(8,128)}, f32[4,2,128,512]{2,3,1,0:T(8,128)S(1)}, u32[]{:S(2)}) copy-start(f32[4,2,128,512]{2,3,1,0:T(8,128)S(1)} %get-tuple-element.6) | copy-start | bytes 6291460
  4.6 14.2 %collective-permute-start.3 = (bf16[4,2,128,3]{2,3,1,0:T(4,128)(2,1)S(1)}, bf16[4,2,128,3]{2,3,1,0:T(4,128)(2,1)S(1)}, u32[]{:S(2)}, u32[]{:S(2)}) collective-permute-start(bf16[4,2,128,3]{2,3,1,0:T(4,128)(2,1)S(1)} %get-tuple-element.27), channel_id=1, source_target_pairs={{1,0},{2,1},{3,2},{4,3},{5,4},{6,5},{7,6},{0,7},{9,8},{10,9},{11,1... | collective-permute-start | bytes 18440 | tf_op jit(solution)/shard_map/ppermute | solution.py:120
  10.6 8.2 %collective-permute-start.2 = (bf16[4,2,128,3]{2,3,1,0:T(4,128)(2,1)S(1)}, bf16[4,2,128,3]{2,3,1,0:T(4,128)(2,1)S(1)}, u32[]{:S(2)}, u32[]{:S(2)}) collective-permute-start(bf16[4,2,128,3]{2,3,1,0:T(4,128)(2,1)S(1)} %get-tuple-element.26), channel_id=1, source_target_pairs={{0,1},{1,2},{2,3},{3,4},{4,5},{5,6},{6,7},{7,0},{8,9},{9,10},{10,1... | collective-permute-start | bytes 18440 | tf_op jit(solution)/shard_map/ppermute | solution.py:119
  13.9 5.2 %collective-permute-start.1 = (bf16[4,2,3,512]{3,0,2,1:T(4,128)(2,1)S(1)}, bf16[4,2,3,512]{3,0,2,1:T(4,128)(2,1)S(1)}, u32[]{:S(2)}, u32[]{:S(2)}) collective-permute-start(bf16[4,2,3,512]{3,0,2,1:T(4,128)(2,1)S(1)} %copy.33), channel_id=1, source_target_pairs={{8,0},{16,8},{24,16},{32,24},{40,32},{48,40},{56,48},{64,56},{72,6... | collective-permute-start | bytes 73736 | tf_op jit(solution)/shard_map/ppermute | solution.py:118
  16.6 5.9 %collective-permute-start = (bf16[4,2,3,512]{3,0,2,1:T(4,128)(2,1)S(1)}, bf16[4,2,3,512]{3,0,2,1:T(4,128)(2,1)S(1)}, u32[]{:S(2)}, u32[]{:S(2)}) collective-permute-start(bf16[4,2,3,512]{3,0,2,1:T(4,128)(2,1)S(1)} %copy.32), channel_id=1, source_target_pairs={{0,8},{8,16},{16,24},{24,32},{32,40},{40,48},{48,56},{56,64},{64,7... | collective-permute-start | bytes 73736 | tf_op jit(solution)/shard_map/ppermute | solution.py:117
  23.8 2.8 %copy-start.1 = (f32[4,2,128,512]{2,3,1,0:T(8,128)S(1)}, f32[4,2,128,512]{2,3,1,0:T(8,128)}, u32[]{:S(2)}) copy-start(f32[4,2,128,512]{2,3,1,0:T(8,128)} %copy-done) | copy-start | bytes 6291460
  23.8 2.8 %copy-start.13 = (f32[1,128,512]{1,2,0:T(8,128)S(1)}, f32[1,128,512]{1,2,0:T(8,128)}, u32[]{:S(2)}) copy-start(f32[1,128,512]{1,2,0:T(8,128)} %get-tuple-element.11) | copy-start | bytes 786436
  23.8 2.9 %copy-start.14 = (f32[1,128,512]{1,2,0:T(8,128)S(1)}, f32[1,128,512]{1,2,0:T(8,128)}, u32[]{:S(2)}) copy-start(f32[1,128,512]{1,2,0:T(8,128)} %get-tuple-element.12) | copy-start | bytes 786436
  26.7 2.4 %copy-start.2 = (f32[4,2,134,512]{2,3,1,0:T(8,128)}, f32[4,2,134,512]{2,3,1,0:T(8,128)S(1)}, u32[]{:S(2)}) copy-start(f32[4,2,134,512]{2,3,1,0:T(8,128)S(1)} %maximum_convert_fusion) | copy-start | bytes 6586372
  26.7 1.1 copy-start.11
  26.7 1.4 %copy-start.12 = (f32[1,128,512]{1,2,0:T(8,128)S(1)}, f32[1,128,512]{1,2,0:T(8,128)}, u32[]{:S(2)}) copy-start(f32[1,128,512]{1,2,0:T(8,128)} %get-tuple-element.14) | copy-start | bytes 786436
  27.7 2.6 %copy-start.3 = (bf16[1,2,128,512]{2,3,1,0:T(8,128)(2,1)}, bf16[1,2,128,512]{2,3,1,0:T(8,128)(2,1)S(1)}, u32[]{:S(2)}) copy-start(bf16[1,2,128,512]{2,3,1,0:T(8,128)(2,1)S(1)} %fusion.111) | copy-start | bytes 786436
  28.1 1.2 copy-start.9
  28.1 1.3 %copy-start.10 = (f32[1,128,512]{1,2,0:T(8,128)S(1)}, f32[1,128,512]{1,2,0:T(8,128)}, u32[]{:S(2)}) copy-start(f32[1,128,512]{1,2,0:T(8,128)} %get-tuple-element.15) | copy-start | bytes 786436
  29.0 1.3 %copy-start.5 = (bf16[1,2,128,512]{2,3,1,0:T(8,128)(2,1)}, bf16[1,2,128,512]{2,3,1,0:T(8,128)(2,1)S(1)}, u32[]{:S(2)}) copy-start(bf16[1,2,128,512]{2,3,1,0:T(8,128)(2,1)S(1)} %fusion.109) | copy-start | bytes 786436
  30.3 0.7 copy-start.7
  31.5 16.5 %collective-permute-start.4 = (f32[2,1,512]{1,2,0:T(8,128)S(1)}, f32[2,1,512]{1,2,0:T(8,128)S(1)}, u32[]{:S(2)}, u32[]{:S(2)}) collective-permute-start(f32[2,1,512]{1,2,0:T(8,128)S(1)} %get-tuple-element.33), channel_id=1, source_target_pairs={{8,0},{16,8},{24,16},{32,24},{40,32},{48,40},{56,48},{64,56},{72,6... | collective-permute-start | bytes 12296 | tf_op jit(solution)/shard_map/ppermute | solution.py:143
  36.3 11.7 %collective-permute-start.5 = (f32[2,1,512]{1,2,0:T(8,128)S(1)}, f32[2,1,512]{1,2,0:T(8,128)S(1)}, u32[]{:S(2)}, u32[]{:S(2)}) collective-permute-start(f32[2,1,512]{1,2,0:T(8,128)S(1)} %get-tuple-element.32), channel_id=1, source_target_pairs={{0,8},{8,16},{16,24},{24,32},{32,40},{40,48},{48,56},{56,64},{64,7... | collective-permute-start | bytes 12296 | tf_op jit(solution)/shard_map/ppermute | solution.py:142
  36.3 6.4 %collective-permute-start.6 = (f32[2,128,1]{1,2,0:T(1,128)S(1)}, f32[2,128,1]{1,2,0:T(1,128)S(1)}, u32[]{:S(2)}, u32[]{:S(2)}) collective-permute-start(f32[2,128,1]{1,2,0:T(1,128)S(1)} %get-tuple-element.29), channel_id=1, source_target_pairs={{1,0},{2,1},{3,2},{4,3},{5,4},{6,5},{7,6},{0,7},{9,8},{10,9},{11,1... | collective-permute-start | bytes 3080 | tf_op jit(solution)/shard_map/ppermute | solution.py:145
  42.0 6.0 %collective-permute-start.7 = (f32[2,128,1]{1,2,0:T(1,128)S(1)}, f32[2,128,1]{1,2,0:T(1,128)S(1)}, u32[]{:S(2)}, u32[]{:S(2)}) collective-permute-start(f32[2,128,1]{1,2,0:T(1,128)S(1)} %get-tuple-element.28), channel_id=1, source_target_pairs={{0,1},{1,2},{2,3},{3,4},{4,5},{5,6},{6,7},{7,0},{8,9},{9,10},{10,1... | collective-permute-start | bytes 3080 | tf_op jit(solution)/shard_map/ppermute | solution.py:144
  48.6 13.2 %copy-start.21 = (f32[32,16]{0,1:T(8,128)S(1)}, f32[32,16]{0,1:T(8,128)}, u32[]{:S(2)}) copy-start(f32[32,16]{0,1:T(8,128)} %constant.42.clone) | copy-start | bytes 6148
  60.9 1.5 %copy-start.18 = (f32[16,256]{1,0:T(8,128)S(1)}, f32[16,256]{1,0:T(8,128)}, u32[]{:S(2)}) copy-start(f32[16,256]{1,0:T(8,128)} %constant.44.clone) | copy-start | bytes 49156
  60.9 1.5 %copy-start.19 = (f32[16,256]{1,0:T(8,128)S(1)}, f32[16,256]{1,0:T(8,128)}, u32[]{:S(2)}) copy-start(f32[16,256]{1,0:T(8,128)} %constant.43.clone) | copy-start | bytes 49156
  62.5 1.0 copy-start.16
  62.7 1.5 %copy-start.15 = (f32[512,256]{1,0:T(8,128)S(1)}, f32[512,256]{1,0:T(8,128)}, u32[]{:S(2)}) copy-start(f32[512,256]{1,0:T(8,128)} %constant.69) | copy-start | bytes 1572868
  66.4 43.5 %all-to-all-start.1 = ((f32[256,2,512]{2,1,0:T(2,128)}), f32[256,2,512]{2,1,0:T(2,128)S(1)}, u32[]{:S(2)}, u32[]{:S(2)}) async-start(f32[256,2,512]{2,1,0:T(2,128)} %reshape.117), calls=%async_computation.1 | async-start | bytes 2097152 | tf_op jit(solution)/shard_map/all_to_all | solution.py:179
  82.5 4.8 %copy-start.4 = (bf16[1,2,128,512]{2,3,1,0:T(8,128)(2,1)S(1)}, bf16[1,2,128,512]{2,3,1,0:T(8,128)(2,1)}, u32[]{:S(2)}) copy-start(bf16[1,2,128,512]{2,3,1,0:T(8,128)(2,1)} %copy-done.3) | copy-start | bytes 786436
  82.5 4.8 %copy-start.6 = (bf16[1,2,128,512]{2,3,1,0:T(8,128)(2,1)S(1)}, bf16[1,2,128,512]{2,3,1,0:T(8,128)(2,1)}, u32[]{:S(2)}) copy-start(bf16[1,2,128,512]{2,3,1,0:T(8,128)(2,1)} %copy-done.5) | copy-start | bytes 786436
  82.5 4.8 %copy-start.8 = (bf16[1,2,128,512]{2,3,1,0:T(8,128)(2,1)S(1)}, bf16[1,2,128,512]{2,3,1,0:T(8,128)(2,1)}, u32[]{:S(2)}) copy-start(bf16[1,2,128,512]{2,3,1,0:T(8,128)(2,1)} %copy-done.7) | copy-start | bytes 786436
  110.9 2.4 %copy-start.20 = (f32[32,32]{1,0:T(8,128)S(1)}, f32[32,32]{1,0:T(8,128)}, u32[]{:S(2)}) copy-start(f32[32,32]{1,0:T(8,128)} %constant.47.clone) | copy-start | bytes 12292
where the time goes:
time: 117 us; the launch traced here: 116 us
  starting transfers between devices  31 us (26%)
  waiting for transfers between devices  29.1 us (25%)
  local copies, waits for them, and re-layouts  23.4 us (20%)
  other arithmetic  14.7 us (13%)
  blocking collectives  12.3 us (11%)
  matrix products  4.62 us (4%)
    all_to_all x1, waiting for transfers between devices, body(): lax.all_to_all(spectrum_y, ('gx', 'gy'), split_axis=0, concat_axis=0, til...  21.1 us
    all_to_all x1, starting transfers between devices, body(): lax.all_to_all(spectrum_y, ('gx', 'gy'), split_axis=0, concat_axis=0, til...  12.7 us
    all_to_all x1, blocking collectives, body(): lax.all_to_all(sent, 'gy', split_axis=2, concat_axis=1, tiled=True)  12.3 us
    another operation x5, other arithmetic, body(): tendency = jnp.stack(pieces)  7.68 us
    ppermute x1, starting transfers between devices, body(): y_after = lax.ppermute(masked[:, :, :, :3], 'gy', down_y)  6 us
    ppermute x1, starting transfers between devices, body(): v_after = lax.ppermute(flow_v[:, :, :1], 'gy', down_y)  5.68 us
    ppermute x1, waiting for transfers between devices, body(): v_before = lax.ppermute(flow_v[:, :, rows_y - 1:], 'gy', up_y)  5.31 us
    unnamed x47, local copies, waits for them, and re-layouts  5.25 us
  transfers between devices with their start and end apart: 9, of which 4 were waited for; matrix products, arithmetic and copies ran while one was open for 15% of the time, Pallas kernels for 0%

commit v1 on v0

--- a/solution.py
+++ b/solution.py
@@ -154,28 +154,28 @@
     n_p = total_y // n_q
     split_y = rows_y // n_q
     piece_x = rows_x // count_y
-    sent = diverge.reshape(levels, rows_x, split_y, n_q).transpose(0, 2, 1, 3)
-    columns = lax.all_to_all(sent, "gy", split_axis=2, concat_axis=1, tiled=True)
+    sent = diverge.reshape(levels, count_y, piece_x, split_y, n_q).transpose(1, 3, 0, 2, 4)
+    sent = sent.reshape(count_y, split_y * levels * piece_x, n_q)
+    columns = lax.all_to_all(sent, "gy", split_axis=0, concat_axis=0, tiled=True)
+    columns = columns.reshape(n_p, levels, piece_x, n_q)
     w1, t1c, t1s, w2 = y_tables(n_p, n_q)
-    w1b = jnp.broadcast_to(const(w1)[None], (levels,) + w1.shape)
     stage1 = lax.dot_general(
-        w1b, columns, (((2,), (1,)), ((0,), (0,))), precision=PREC
-    )
-    real1 = stage1[:, :n_p]
-    imag1 = stage1[:, n_p:]
-    tc = const(t1c)[None, :, None, :]
-    ts = const(t1s)[None, :, None, :]
+        const(w1), columns, (((1,), (0,)), ((), ())), precision=PREC
+    )
+    real1 = stage1[:n_p]
+    imag1 = stage1[n_p:]
+    tc = const(t1c)[:, None, None, :]
+    ts = const(t1s)[:, None, None, :]
     real_t = real1 * tc + imag1 * ts
     imag_t = imag1 * tc - real1 * ts
     rows_m = levels * n_p * piece_x
     joined = jnp.concatenate(
         [real_t.reshape(rows_m, n_q), imag_t.reshape(rows_m, n_q)], axis=1
     )
+    devices = count_x * count_y
     spectrum_y = lax.dot_general(
-        const(w2), joined, (((1,), (1,)), ((), ())), precision=PREC
-    )
-    devices = count_x * count_y
-    spectrum_y = spectrum_y.reshape(devices, 2, rows_m)
+        const(w2.reshape(devices, 2, 2 * n_q)), joined, (((2,), (1,)), ((), ())), precision=PREC
+    )
     moved = lax.all_to_all(spectrum_y, ("gx", "gy"), split_axis=0, concat_axis=0, tiled=True)
 
     total_x = rows_x * count_x
@@ -199,7 +199,7 @@
     result = lax.dot_general(
         wbb, joined_x, (((2,), (1,)), ((0,), (0,))), precision=PREC
     )
-    result = result.reshape(levels, n_p, 2, n_i, n_s).transpose(2, 0, 1, 3, 4)
+    result = result.reshape(n_p, levels, 2, n_i, n_s).transpose(2, 1, 0, 3, 4)
     spectrum = result.reshape(2, levels, n_p, total_x)
     return (tendency, spectrum)
 

time: 117 us -> 108 us (0.923)
  local copies, waits for them, and re-layouts: 23.4 us -> 9.34 us
  blocking collectives: 12.3 us -> 15.2 us
  starting transfers between devices: 31 us -> 33.4 us
  other arithmetic: 14.7 us -> 13.5 us
    ppermute x1, starting transfers between devices: 0.01 us -> 4.3 us  [body(): u_before = lax.ppermute(flow_u[:, rows_x - 1:, :], 'gx', up_x)]
    unnamed x47 -> x28, local copies, waits for them, and re-layouts: 5.25 us -> 1.57 us
    ppermute x1, starting transfers between devices: 4.75 us -> 1.28 us  [body(): u_after = lax.ppermute(flow_u[:, :1, :], 'gx', down_x)]
    all_to_all x1, waiting for transfers between devices: 21.1 us -> 24.4 us  [body(): lax.all_to_all(spectrum_y, ('gx', 'gy'), split_axis=0, concat_axis=0, til...]
    slice x2 -> x1, local copies, waits for them, and re-layouts: 3.3 us -> 0.03 us  [body(): x_before = lax.ppermute(masked[:, :, rows_x - 3:, :], 'gx', up_x)]
    ppermute x1, waiting for transfers between devices: 0.01 us -> 3.13 us  [body(): y_before = lax.ppermute(masked[:, :, :, rows_y - 3:], 'gy', up_y)]
    ppermute x1, waiting for transfers between devices: 5.31 us -> 2.31 us  [body(): v_before = lax.ppermute(flow_v[:, :, rows_y - 1:], 'gy', up_y)]
    all_to_all x1, blocking collectives: 12.3 us -> 15.2 us  [body(): lax.all_to_all(sent, 'gy', split_axis=0, concat_axis=0, tiled=True)]
  transfers between devices with their start and end apart: 9 -> 9, of which waited for: 4 -> 3; matrix products, arithmetic and copies ran while one was open for 15% -> 8% of each run, Pallas kernels for 0% -> 0%
where the time goes in v1:
time: 108 us
  starting transfers between devices  33.4 us (31%)
  waiting for transfers between devices  29.9 us (28%)
  blocking collectives  15.2 us (14%)
  other arithmetic  13.5 us (12%)
  local copies, waits for them, and re-layouts  9.34 us (9%)
  matrix products  5.26 us (5%)
    all_to_all x1, waiting for transfers between devices, body(): lax.all_to_all(spectrum_y, ('gx', 'gy'), split_axis=0, concat_axis=0, til...  24.4 us
    all_to_all x1, blocking collectives, body(): lax.all_to_all(sent, 'gy', split_axis=0, concat_axis=0, tiled=True)  15.2 us
    all_to_all x1, starting transfers between devices, body(): lax.all_to_all(spectrum_y, ('gx', 'gy'), split_axis=0, concat_axis=0, til...  14 us
    another operation x5, other arithmetic, body(): tendency = jnp.stack(pieces)  8.12 us
    ppermute x1, starting transfers between devices, body(): v_after = lax.ppermute(flow_v[:, :, :1], 'gy', down_y)  5.36 us
    ppermute x1, starting transfers between devices, body(): y_after = lax.ppermute(masked[:, :, :, :3], 'gy', down_y)  4.48 us
    ppermute x1, starting transfers between devices, body(): u_before = lax.ppermute(flow_u[:, rows_x - 1:, :], 'gx', up_x)  4.3 us
    ppermute x1, waiting for transfers between devices, body(): y_before = lax.ppermute(masked[:, :, :, rows_y - 3:], 'gy', up_y)  3.13 us
  transfers between devices with their start and end apart: 9, of which 3 were waited for; matrix products, arithmetic and copies ran while one was open for 8% of the time, Pallas kernels for 0%

profile of v1, /device:TPU:1, one launch (start us, length us, event | category | flops | bytes accessed | tf_op | source)
XLA Modules:
  0.0 107.6 jit_solution(3807674278950986516)
XLA Ops:
  0.6 1.0 convert_convert_fusion
  1.6 1.4 %fusion.119 = (f32[4,2,128,512]{3,2,1,0:T(8,128)S(1)}, bf16[4,2,128,512]{3,2,1,0:T(8,128)(2,1)S(1)}) fusion(bf16[4,2,128,512]{3,2,1,0:T(8,128)(2,1)} %param.11, bf16[2,128,512]{2,1,0:T(8,128)(2,1)S(1)} %convert_convert_fusion), kind=kLoop, calls=%fused_computation.186 | loop fusion | flops 1048576 | bytes 4456448 | tf_op jit(solution)/shard_map/convert_element_type | solution.py:123
  3.1 2.8 %collective-permute-start = (bf16[4,2,3,512]{3,2,1,0:T(4,128)(2,1)S(1)}, bf16[4,2,3,512]{3,2,1,0:T(4,128)(2,1)S(1)}, u32[]{:S(2)}, u32[]{:S(2)}) collective-permute-start(bf16[4,2,3,512]{3,2,1,0:T(4,128)(2,1)S(1)} %get-tuple-element.20), channel_id=1, source_target_pairs={{0,8},{8,16},{16,24},{24,32},{32,40},{40,48},{48,56},{56,64},{64,7... | collective-permute-start | bytes 73736 | tf_op jit(solution)/shard_map/ppermute | solution.py:117
  5.9 0.6 collective-permute-start.1
  6.5 0.1 fusion.121
  6.6 0.7 collective-permute-start.2
  7.3 4.5 %collective-permute-start.3 = (bf16[4,2,128,3]{3,2,1,0:T(8,128)(2,1)S(1)}, bf16[4,2,128,3]{3,2,1,0:T(8,128)(2,1)S(1)}, u32[]{:S(2)}, u32[]{:S(2)}) collective-permute-start(bf16[4,2,128,3]{3,2,1,0:T(8,128)(2,1)S(1)} %get-tuple-element.23), channel_id=1, source_target_pairs={{1,0},{2,1},{3,2},{4,3},{5,4},{6,5},{7,6},{0,7},{9,8},{10,9},{11,1... | collective-permute-start | bytes 18440 | tf_op jit(solution)/shard_map/ppermute | solution.py:120
  11.8 1.0 slice_bitcast_fusion.21
  12.8 3.1 %collective-permute-done.2 = bf16[4,2,128,3]{3,2,1,0:T(8,128)(2,1)S(1)} collective-permute-done((bf16[4,2,128,3]{3,2,1,0:T(8,128)(2,1)S(1)}, bf16[4,2,128,3]{3,2,1,0:T(8,128)(2,1)S(1)}, u32[]{:S(2)}, u32[]{:S(2)}) %collective-permute-start.2) | collective-permute-done | bytes 6176 | tf_op jit(solution)/shard_map/ppermute | solution.py:119
  15.9 0.0 collective-permute-done.3
  15.9 0.7 maximum_convert_fusion
  16.6 0.0 copy-start.2
  16.6 0.0 collective-permute-done
  16.6 0.0 collective-permute-done.1
  16.6 0.4 maximum_convert_fusion.1
  17.0 0.7 copy-done.2
  17.7 0.9 fusion.114
  18.6 0.9 fusion.115
  19.6 0.9 fusion.113
  20.5 0.3 slice_add_fusion
  20.8 0.1 slice_bitcast_fusion
  20.9 0.3 copy-done.7
  21.2 0.1 fusion.122
  21.3 0.2 fusion.123
  21.6 0.1 fusion.125
  21.7 4.3 %collective-permute-start.5 = (f32[2,1,512]{2,1,0:T(1,128)S(1)}, f32[2,1,512]{2,1,0:T(1,128)S(1)}, u32[]{:S(2)}, u32[]{:S(2)}) collective-permute-start(f32[2,1,512]{2,1,0:T(1,128)S(1)} %get-tuple-element.28), channel_id=1, source_target_pairs={{0,8},{8,16},{16,24},{24,32},{32,40},{40,48},{48,56},{56,64},{64,7... | collective-permute-start | bytes 12296 | tf_op jit(solution)/shard_map/ppermute | solution.py:142
  26.0 1.3 %collective-permute-start.4 = (f32[2,1,512]{2,1,0:T(1,128)S(1)}, f32[2,1,512]{2,1,0:T(1,128)S(1)}, u32[]{:S(2)}, u32[]{:S(2)}) collective-permute-start(f32[2,1,512]{2,1,0:T(1,128)S(1)} %get-tuple-element.29), channel_id=1, source_target_pairs={{8,0},{16,8},{24,16},{32,24},{40,32},{48,40},{56,48},{64,56},{72,6... | collective-permute-start | bytes 12296 | tf_op jit(solution)/shard_map/ppermute | solution.py:143
  27.3 0.0 collective-permute-start.7
  27.3 5.4 %collective-permute-start.6 = (f32[2,128,1]{2,1,0:T(8,128)S(1)}, f32[2,128,1]{2,1,0:T(8,128)S(1)}, u32[]{:S(2)}, u32[]{:S(2)}) collective-permute-start(f32[2,128,1]{2,1,0:T(8,128)S(1)} %get-tuple-element.25), channel_id=1, source_target_pairs={{1,0},{2,1},{3,2},{4,3},{5,4},{6,5},{7,6},{0,7},{9,8},{10,9},{11,1... | collective-permute-start | bytes 3080 | tf_op jit(solution)/shard_map/ppermute | solution.py:145
  32.7 2.3 %collective-permute-done.7 = f32[2,128,1]{2,1,0:T(8,128)S(1)} collective-permute-done((f32[2,128,1]{2,1,0:T(8,128)S(1)}, f32[2,128,1]{2,1,0:T(8,128)S(1)}, u32[]{:S(2)}, u32[]{:S(2)}) %collective-permute-start.7) | collective-permute-done | bytes 1056 | tf_op jit(solution)/shard_map/ppermute | solution.py:144
  35.0 0.0 collective-permute-done.6
  35.0 0.0 collective-permute-done.5
  35.0 0.0 collective-permute-done.4
  35.0 0.3 fusion.103
  35.3 0.0 copy-start.10
  35.3 0.3 reshape.116
  35.7 0.0 copy-start.11
  35.7 0.1 copy.27
  35.8 15.2 %all_to_all.10 = f32[8,64,256]{2,1,0:T(8,128)S(1)} all-to-all(f32[8,64,256]{2,1,0:T(8,128)S(1)} %bitcast.318), channel_id=1, replica_groups=mesh['gx'=32,'gy'=8] {'gy'}, dimensions={0} | all-to-all | bytes 1048576 | tf_op jit(solution)/shard_map/all_to_all | solution.py:159
  51.0 1.4 %fusion.110 = f32[32,2,16,256]{3,0,2,1:T(8,128)S(1)} fusion(f32[32,16,1,1]{0,1,3,2:T(8,128)} %constant.68, f32[16,2,16,256]{3,2,1,0:T(8,128)S(1)} %bitcast.316), kind=kOutput, calls=%fused_computation.159 | convolution fusion | flops 25165824 | bytes 1574912 | tf_op jit(solution)/shard_map/dot_general | solution.py:162
  52.4 0.0 copy-start.9
  52.4 0.2 multiply_add_fusion.1
  52.6 0.3 copy.29
  52.9 0.3 copy.30
  53.2 0.4 copy-done.9
  53.7 1.0 fusion
  54.7 1.8 %copy.31 = f32[256,2,512]{2,1,0:T(2,128)} copy(f32[256,2,512]{2,0,1:T(8,128)S(1)} %fusion) | data formatting | bytes 2097152 | tf_op jit(solution)/shard_map/dot_general | solution.py:176
  56.5 14.0 %all-to-all-start.1 = ((f32[256,2,512]{2,1,0:T(2,128)}), f32[256,2,512]{2,1,0:T(2,128)S(1)}, u32[]{:S(2)}, u32[]{:S(2)}) async-start(f32[256,2,512]{2,1,0:T(2,128)} %copy.31), calls=%async_computation.1 | async-start | bytes 2097152 | tf_op jit(solution)/shard_map/all_to_all | solution.py:179
  70.5 1.0 convert_element_type.51
  71.5 4.3 %fusion.116 = bf16[1,2,128,512]{3,2,1,0:T(8,128)(2,1)S(1)} fusion(f32[128,512]{1,0:T(8,128)S(1)} %convert_element_type.51, f32[4,2,128,512]{3,2,1,0:T(8,128)} %copy-done.1, f32[4,2,128,518]{3,2,1,0:T(8,128)} %copy-done, f32[4,2,134,512]{3,2,1,0:T(8,128)S(1)} %maximum_convert_fusion.1, f32[1,128,512]{2,1,0:T(8,128)} %get-tuple-element.5, ...), kind=kLoop, calls=%fused_computation.183 | loop fusion | flops 5242880 | bytes 9699328 | tf_op jit(solution)/shard_map/stack | solution.py:138
  75.8 0.0 copy-done.4
  75.8 0.0 copy-done.6
  75.8 0.0 copy-done.8
  75.8 1.1 %pad_maximum_fusion = bf16[4,2,128,512]{3,2,1,0:T(8,128)(2,1)} fusion(bf16[1,2,128,512]{3,2,1,0:T(8,128)(2,1)S(1)} %fusion.116, bf16[1,2,128,512]{3,2,1,0:T(8,128)(2,1)S(1)} %copy-done.6, bf16[1,2,128,512]{3,2,1,0:T(8,128)(2,1)S(1)} %copy-done.8, bf16[1,2,128,512]{3,2,1,0:T(8,128)(2,1)S(1)} %copy-done.4), kind=kLoop, calls=%fused_computation.3 | loop fusion | flops 1572864 | bytes 2097152 | tf_op jit(solution)/shard_map/stack | solution.py:138
  76.9 24.4 %all-to-all-done.1 = f32[256,2,512]{2,1,0:T(2,128)S(1)} async-done(((f32[256,2,512]{2,1,0:T(2,128)}), f32[256,2,512]{2,1,0:T(2,128)S(1)}, u32[]{:S(2)}, u32[]{:S(2)}) %all-to-all-start.1) | async-done | bytes 1048608 | tf_op jit(solution)/shard_map/all_to_all | solution.py:179
  101.3 0.7 reshape.121
  102.0 0.0 copy-start.12
  102.0 0.3 copy.32
  102.4 0.0 copy-start.13
  102.4 2.2 %fusion.126 = f32[32,16,512]{2,1,0:T(8,128)S(1)} fusion(f32[32,16,512]{2,1,0:T(8,128)S(1)} %bitcast.313, f32[512,512,1]{1,0,2:T(8,128)} %constant.69), kind=kOutput, calls=%fused_computation.193 | convolution fusion | flops 805306368 | bytes 3145728 | tf_op jit(solution)/shard_map/dot_general | solution.py:186
  104.6 0.2 multiply_add_fusion
  104.8 0.6 fusion.3
  105.4 0.7 reshape.143
  106.1 1.6 %copy.35 = f32[2,2,16,4096]{3,2,1,0:T(8,128)} copy(f32[2,2,16,4096]{3,0,1,2:T(2,128)S(1)} %reshape.143) | data formatting | bytes 2097152 | tf_op jit(solution)/shard_map/reshape | solution.py:203
  (19 shorter events, 0.1 us)
Async XLA Ops:
  3.1 17.4 %copy-start.1 = (f32[4,2,128,512]{3,2,1,0:T(8,128)}, f32[4,2,128,512]{3,2,1,0:T(8,128)S(1)}, u32[]{:S(2)}) copy-start(f32[4,2,128,512]{3,2,1,0:T(8,128)S(1)} %get-tuple-element.2) | copy-start | bytes 6291460
  3.1 13.5 %collective-permute-start = (bf16[4,2,3,512]{3,2,1,0:T(4,128)(2,1)S(1)}, bf16[4,2,3,512]{3,2,1,0:T(4,128)(2,1)S(1)}, u32[]{:S(2)}, u32[]{:S(2)}) collective-permute-start(bf16[4,2,3,512]{3,2,1,0:T(4,128)(2,1)S(1)} %get-tuple-element.20), channel_id=1, source_target_pairs={{0,8},{8,16},{16,24},{24,32},{32,40},{40,48},{48,56},{56,64},{64,7... | collective-permute-start | bytes 73736 | tf_op jit(solution)/shard_map/ppermute | solution.py:117
  5.9 10.7 %collective-permute-start.1 = (bf16[4,2,3,512]{3,2,1,0:T(4,128)(2,1)S(1)}, bf16[4,2,3,512]{3,2,1,0:T(4,128)(2,1)S(1)}, u32[]{:S(2)}, u32[]{:S(2)}) collective-permute-start(bf16[4,2,3,512]{3,2,1,0:T(4,128)(2,1)S(1)} %get-tuple-element.21), channel_id=1, source_target_pairs={{8,0},{16,8},{24,16},{32,24},{40,32},{48,40},{56,48},{64,56},{72,6... | collective-permute-start | bytes 73736 | tf_op jit(solution)/shard_map/ppermute | solution.py:118
  6.6 9.3 %collective-permute-start.2 = (bf16[4,2,128,3]{3,2,1,0:T(8,128)(2,1)S(1)}, bf16[4,2,128,3]{3,2,1,0:T(8,128)(2,1)S(1)}, u32[]{:S(2)}, u32[]{:S(2)}) collective-permute-start(bf16[4,2,128,3]{3,2,1,0:T(8,128)(2,1)S(1)} %get-tuple-element.22), channel_id=1, source_target_pairs={{0,1},{1,2},{2,3},{3,4},{4,5},{5,6},{6,7},{7,0},{8,9},{9,10},{10,1... | collective-permute-start | bytes 18440 | tf_op jit(solution)/shard_map/ppermute | solution.py:119
  7.3 8.6 %collective-permute-start.3 = (bf16[4,2,128,3]{3,2,1,0:T(8,128)(2,1)S(1)}, bf16[4,2,128,3]{3,2,1,0:T(8,128)(2,1)S(1)}, u32[]{:S(2)}, u32[]{:S(2)}) collective-permute-start(bf16[4,2,128,3]{3,2,1,0:T(8,128)(2,1)S(1)} %get-tuple-element.23), channel_id=1, source_target_pairs={{1,0},{2,1},{3,2},{4,3},{5,4},{6,5},{7,6},{0,7},{9,8},{10,9},{11,1... | collective-permute-start | bytes 18440 | tf_op jit(solution)/shard_map/ppermute | solution.py:120
  16.5 3.0 %copy-start = (f32[4,2,128,518]{3,2,1,0:T(8,128)}, f32[4,2,128,518]{3,2,1,0:T(8,128)S(1)}, u32[]{:S(2)}) copy-start(f32[4,2,128,518]{3,2,1,0:T(8,128)S(1)} %maximum_convert_fusion) | copy-start | bytes 6365188
  16.6 1.1 %copy-start.2 = (s32[128,512]{1,0:T(8,128)S(1)}, s32[128,512]{1,0:T(8,128)}, u32[]{:S(2)}) copy-start(s32[128,512]{1,0:T(8,128)} %param.12) | copy-start | bytes 786436
  18.6 1.9 %copy-start.3 = (bf16[1,2,128,512]{3,2,1,0:T(8,128)(2,1)}, bf16[1,2,128,512]{3,2,1,0:T(8,128)(2,1)S(1)}, u32[]{:S(2)}) copy-start(bf16[1,2,128,512]{3,2,1,0:T(8,128)(2,1)S(1)} %fusion.114) | copy-start | bytes 786436
  19.5 0.9 copy-start.5
  20.5 0.8 copy-start.7
  21.7 13.3 %collective-permute-start.5 = (f32[2,1,512]{2,1,0:T(1,128)S(1)}, f32[2,1,512]{2,1,0:T(1,128)S(1)}, u32[]{:S(2)}, u32[]{:S(2)}) collective-permute-start(f32[2,1,512]{2,1,0:T(1,128)S(1)} %get-tuple-element.28), channel_id=1, source_target_pairs={{0,8},{8,16},{16,24},{24,32},{32,40},{40,48},{48,56},{56,64},{64,7... | collective-permute-start | bytes 12296 | tf_op jit(solution)/shard_map/ppermute | solution.py:142
  26.0 9.0 %collective-permute-start.4 = (f32[2,1,512]{2,1,0:T(1,128)S(1)}, f32[2,1,512]{2,1,0:T(1,128)S(1)}, u32[]{:S(2)}, u32[]{:S(2)}) collective-permute-start(f32[2,1,512]{2,1,0:T(1,128)S(1)} %get-tuple-element.29), channel_id=1, source_target_pairs={{8,0},{16,8},{24,16},{32,24},{40,32},{48,40},{56,48},{64,56},{72,6... | collective-permute-start | bytes 12296 | tf_op jit(solution)/shard_map/ppermute | solution.py:143
  27.3 7.7 %collective-permute-start.7 = (f32[2,128,1]{2,1,0:T(8,128)S(1)}, f32[2,128,1]{2,1,0:T(8,128)S(1)}, u32[]{:S(2)}, u32[]{:S(2)}) collective-permute-start(f32[2,128,1]{2,1,0:T(8,128)S(1)} %get-tuple-element.24), channel_id=1, source_target_pairs={{0,1},{1,2},{2,3},{3,4},{4,5},{5,6},{6,7},{7,0},{8,9},{9,10},{10,1... | collective-permute-start | bytes 3080 | tf_op jit(solution)/shard_map/ppermute | solution.py:144
  27.3 7.7 %collective-permute-start.6 = (f32[2,128,1]{2,1,0:T(8,128)S(1)}, f32[2,128,1]{2,1,0:T(8,128)S(1)}, u32[]{:S(2)}, u32[]{:S(2)}) collective-permute-start(f32[2,128,1]{2,1,0:T(8,128)S(1)} %get-tuple-element.25), channel_id=1, source_target_pairs={{1,0},{2,1},{3,2},{4,3},{5,4},{6,5},{7,6},{0,7},{9,8},{10,9},{11,1... | collective-permute-start | bytes 3080 | tf_op jit(solution)/shard_map/ppermute | solution.py:145
  35.3 17.1 %copy-start.10 = (f32[16,256]{1,0:T(8,128)S(1)}, f32[16,256]{1,0:T(8,128)}, u32[]{:S(2)}) copy-start(f32[16,256]{1,0:T(8,128)} %constant.44.clone) | copy-start | bytes 49156
  35.7 16.7 %copy-start.11 = (f32[16,256]{1,0:T(8,128)S(1)}, f32[16,256]{1,0:T(8,128)}, u32[]{:S(2)}) copy-start(f32[16,256]{1,0:T(8,128)} %constant.43.clone) | copy-start | bytes 49156
  52.4 1.2 %copy-start.9 = (f32[256,2,512]{2,0,1:T(8,128)S(1)}, f32[256,2,512]{2,0,1:T(8,128)}, u32[]{:S(2)}) copy-start(f32[256,2,512]{2,0,1:T(8,128)} %constant.45.clone) | copy-start | bytes 3145732
  56.5 44.8 %all-to-all-start.1 = ((f32[256,2,512]{2,1,0:T(2,128)}), f32[256,2,512]{2,1,0:T(2,128)S(1)}, u32[]{:S(2)}, u32[]{:S(2)}) async-start(f32[256,2,512]{2,1,0:T(2,128)} %copy.31), calls=%async_computation.1 | async-start | bytes 2097152 | tf_op jit(solution)/shard_map/all_to_all | solution.py:179
  71.4 4.3 %copy-start.4 = (bf16[1,2,128,512]{3,2,1,0:T(8,128)(2,1)S(1)}, bf16[1,2,128,512]{3,2,1,0:T(8,128)(2,1)}, u32[]{:S(2)}) copy-start(bf16[1,2,128,512]{3,2,1,0:T(8,128)(2,1)} %copy-done.3) | copy-start | bytes 786436
  71.4 4.3 %copy-start.6 = (bf16[1,2,128,512]{3,2,1,0:T(8,128)(2,1)S(1)}, bf16[1,2,128,512]{3,2,1,0:T(8,128)(2,1)}, u32[]{:S(2)}) copy-start(bf16[1,2,128,512]{3,2,1,0:T(8,128)(2,1)} %copy-done.5) | copy-start | bytes 786436
  71.5 4.3 %copy-start.8 = (bf16[1,2,128,512]{3,2,1,0:T(8,128)(2,1)S(1)}, bf16[1,2,128,512]{3,2,1,0:T(8,128)(2,1)}, u32[]{:S(2)}) copy-start(bf16[1,2,128,512]{3,2,1,0:T(8,128)(2,1)} %copy-done.7) | copy-start | bytes 786436
  102.0 2.6 %copy-start.12 = (f32[16,256]{1,0:T(8,128)S(1)}, f32[16,256]{1,0:T(8,128)}, u32[]{:S(2)}) copy-start(f32[16,256]{1,0:T(8,128)} %constant.43.clone) | copy-start | bytes 49156
  102.4 2.4 %copy-start.13 = (f32[32,32]{1,0:T(8,128)S(1)}, f32[32,32]{1,0:T(8,128)}, u32[]{:S(2)}) copy-start(f32[32,32]{1,0:T(8,128)} %constant.47.clone) | copy-start | bytes 12292

commit v2 on v1

--- a/solution.py
+++ b/solution.py
@@ -114,39 +114,71 @@
     surface = (level == heights[None]).astype(jnp.float32) * surface_flag[None].astype(jnp.float32)
     masked = state * fluid.astype(jnp.bfloat16)[None]
 
-    x_before = lax.ppermute(masked[:, :, rows_x - 3 :, :], "gx", up_x)
-    x_after = lax.ppermute(masked[:, :, :3, :], "gx", down_x)
-    y_before = lax.ppermute(masked[:, :, :, rows_y - 3 :], "gy", up_y)
-    y_after = lax.ppermute(masked[:, :, :, :3], "gy", down_y)
-    pad_x = jnp.concatenate([x_before, masked, x_after], axis=2).astype(jnp.float32)
-    pad_y = jnp.concatenate([y_before, masked, y_after], axis=3).astype(jnp.float32)
-    center = masked.astype(jnp.float32)
-
-    pieces = []
-    for component in range(4):
-
-        def pick(step_x, step_y, component=component):
-            if step_y == 0:
-                return pad_x[component, :, 3 + step_x : 3 + step_x + rows_x, :]
-            return pad_y[component, :, :, 3 + step_y : 3 + step_y + rows_y]
-
-        pieces.append(
-            tendency_one(component, center[component], pick, center, fluid, surface).astype(
-                jnp.bfloat16
-            )
-        )
-    tendency = jnp.stack(pieces)
-
-    star = center[:3] + DT * tendency[:3].astype(jnp.float32)
-    flow_u, flow_v, flow_w = star[0], star[1], star[2]
-    u_before = lax.ppermute(flow_u[:, rows_x - 1 :, :], "gx", up_x)
-    u_after = lax.ppermute(flow_u[:, :1, :], "gx", down_x)
-    v_before = lax.ppermute(flow_v[:, :, rows_y - 1 :], "gy", up_y)
-    v_after = lax.ppermute(flow_v[:, :, :1], "gy", down_y)
-    u_next = jnp.concatenate([flow_u[:, 1:, :], u_after], axis=1)
-    u_prev = jnp.concatenate([u_before, flow_u[:, :-1, :]], axis=1)
-    v_next = jnp.concatenate([flow_v[:, :, 1:], v_after], axis=2)
-    v_prev = jnp.concatenate([v_before, flow_v[:, :, :-1]], axis=2)
+    halo = 4
+    held = jnp.concatenate([masked, fluid.astype(jnp.bfloat16)[None]], axis=0)
+    lo_x, hi_x = slice(0, halo), slice(rows_x - halo, rows_x)
+    lo_y, hi_y = slice(0, halo), slice(rows_y - halo, rows_y)
+    x_before = lax.ppermute(held[:, :, hi_x, :], "gx", up_x)
+    x_after = lax.ppermute(held[:, :, lo_x, :], "gx", down_x)
+    y_before = lax.ppermute(held[:, :, :, hi_y], "gy", up_y)
+    y_after = lax.ppermute(held[:, :, :, lo_y], "gy", down_y)
+
+    def diagonal(step_x, step_y):
+        return [
+            (a * count_y + b, ((a + step_x) % count_x) * count_y + (b + step_y) % count_y)
+            for a in range(count_x)
+            for b in range(count_y)
+        ]
+
+    both = ("gx", "gy")
+    corner_mm = lax.ppermute(held[:, :, hi_x, hi_y], both, diagonal(1, 1))
+    corner_mp = lax.ppermute(held[:, :, hi_x, lo_y], both, diagonal(1, -1))
+    corner_pm = lax.ppermute(held[:, :, lo_x, hi_y], both, diagonal(-1, 1))
+    corner_pp = lax.ppermute(held[:, :, lo_x, lo_y], both, diagonal(-1, -1))
+    top = jnp.concatenate([corner_mm, x_before, corner_mp], axis=3)
+    middle = jnp.concatenate([y_before, held, y_after], axis=3)
+    bottom = jnp.concatenate([corner_pm, x_after, corner_pp], axis=3)
+    padded = jnp.concatenate([top, middle, bottom], axis=2).astype(jnp.float32)
+
+    def region(grow):
+        span_x = rows_x + 2 * grow
+        span_y = rows_y + 2 * grow
+        base = halo - grow
+        center = padded[:4, :, base : base + span_x, base : base + span_y]
+        fluid_r = padded[4, :, base : base + span_x, base : base + span_y]
+
+        def picker(component):
+            def pick(step_x, step_y):
+                return padded[
+                    component,
+                    :,
+                    base + step_x : base + step_x + span_x,
+                    base + step_y : base + step_y + span_y,
+                ]
+
+            return pick
+
+        return center, fluid_r, picker
+
+    center_g, fluid_g, picker_g = region(1)
+    center_0, fluid_0, picker_0 = region(0)
+    grown = [
+        tendency_one(c, center_g[c], picker_g(c), center_g, fluid_g, None).astype(jnp.bfloat16)
+        for c in range(2)
+    ]
+    inner = [
+        tendency_one(c, center_0[c], picker_0(c), center_0, fluid_0, surface).astype(jnp.bfloat16)
+        for c in range(2, 4)
+    ]
+    tendency = jnp.stack([g[:, 1:-1, 1:-1] for g in grown] + inner)
+
+    star_u = center_g[0] + DT * grown[0].astype(jnp.float32)
+    star_v = center_g[1] + DT * grown[1].astype(jnp.float32)
+    flow_w = center_0[2] + DT * inner[0].astype(jnp.float32)
+    u_next = star_u[:, 2:, 1:-1]
+    u_prev = star_u[:, :-2, 1:-1]
+    v_next = star_v[:, 1:-1, 2:]
+    v_prev = star_v[:, 1:-1, :-2]
     diverge = ((u_next - u_prev) + (v_next - v_prev) + (raised(flow_w) - lowered(flow_w))) * 0.5
 
     total_y = rows_y * count_y

time: 108 us -> 128 us (1.19)
  waiting for transfers between devices: 29.9 us -> 42 us
  other arithmetic: 13.5 us -> 24.3 us
  starting transfers between devices: 33.4 us -> 25.2 us
  local copies, waits for them, and re-layouts: 9.34 us -> 13.4 us
  blocking collectives: 15.2 us -> 17.9 us
  matrix products: 5.26 us -> 3.34 us
    ppermute x8, waiting for transfers between devices: 5.46 us -> 19.4 us  [the longest x1 9.74 us: body(): corner_mm = lax.ppermute(held[:, :, hi_x, hi_y], both, diagonal(1, 1))]
    add x1 -> x3, other arithmetic: 0.31 us -> 10.7 us  [the longest x1 3.75 us: body(): star_v = center_g[1] + DT * grown[1].astype(jnp.float32)]
    ppermute x8, starting transfers between devices: 19.5 us -> 13.7 us  [the longest x1 4.48 us: body(): y_after = lax.ppermute(held[:, :, :, lo_y], 'gy', down_y)]
    another operation x5 -> x2, other arithmetic: 8.12 us -> 4.88 us  [body(): tendency = jnp.stack([g[:, 1:-1, 1:-1] for g in grown] + inner)]
    all_to_all x1, blocking collectives: 15.2 us -> 17.9 us  [body(): lax.all_to_all(sent, 'gy', split_axis=0, concat_axis=0, tiled=True)]
    all_to_all x1, starting transfers between devices: 14 us -> 11.5 us  [body(): lax.all_to_all(spectrum_y, ('gx', 'gy'), split_axis=0, concat_axis=0, til...]
    reshape x1, local copies, waits for them, and re-layouts: 0.34 us -> 2.16 us  [body(): diverge.reshape(levels, count_y, piece_x, split_y, n_q)]
    all_to_all x1, waiting for transfers between devices: 24.4 us -> 22.6 us  [body(): lax.all_to_all(spectrum_y, ('gx', 'gy'), split_axis=0, concat_axis=0, til...]
  transfers between devices with their start and end apart: 9 -> 9, of which waited for: 3 -> 5; matrix products, arithmetic and copies ran while one was open for 8% -> 6% of each run, Pallas kernels for 0% -> 0%
where the time goes in v2:
time: 128 us; the launch traced here: 127 us
  waiting for transfers between devices  42 us (33%)
  starting transfers between devices  25.2 us (20%)
  other arithmetic  24.3 us (19%)
  blocking collectives  17.9 us (14%)
  local copies, waits for them, and re-layouts  13.4 us (10%)
  matrix products  3.34 us (3%)
    all_to_all x1, waiting for transfers between devices, body(): lax.all_to_all(spectrum_y, ('gx', 'gy'), split_axis=0, concat_axis=0, til...  22.6 us
    all_to_all x1, blocking collectives, body(): lax.all_to_all(sent, 'gy', split_axis=0, concat_axis=0, tiled=True)  17.9 us
    all_to_all x1, starting transfers between devices, body(): lax.all_to_all(spectrum_y, ('gx', 'gy'), split_axis=0, concat_axis=0, til...  11.5 us
    ppermute x1, waiting for transfers between devices, body(): corner_mm = lax.ppermute(held[:, :, hi_x, hi_y], both, diagonal(1, 1))  9.74 us
    ppermute x1, waiting for transfers between devices, body(): corner_pm = lax.ppermute(held[:, :, lo_x, hi_y], both, diagonal(-1, 1))  6.42 us
    another operation x2, other arithmetic, body(): tendency = jnp.stack([g[:, 1:-1, 1:-1] for g in grown] + inner)  4.88 us
    ppermute x1, starting transfers between devices, body(): y_after = lax.ppermute(held[:, :, :, lo_y], 'gy', down_y)  4.48 us
    add x1, other arithmetic, body(): star_v = center_g[1] + DT * grown[1].astype(jnp.float32)  3.75 us
  transfers between devices with their start and end apart: 9, of which 5 were waited for; matrix products, arithmetic and copies ran while one was open for 6% of the time, Pallas kernels for 0%

profile of v2, /device:TPU:1, one launch (start us, length us, event | category | flops | bytes accessed | tf_op | source)
XLA Modules:
  0.0 127.1 jit_solution(9207224826888684199)
XLA Ops:
  0.6 1.0 convert_convert_fusion
  1.6 1.0 convert_convert_fusion.1
  2.6 1.3 %broadcast_multiply_fusion = bf16[4,2,128,512]{3,2,1,0:T(8,128)(2,1)S(1)} fusion(bf16[4,2,128,512]{3,2,1,0:T(8,128)(2,1)} %param.11, bf16[2,128,512]{2,1,0:T(8,128)(2,1)S(1)} %convert_convert_fusion.1), kind=kLoop, calls=%fused_computation.180 | loop fusion | flops 524288 | bytes 2359296 | tf_op jit(solution)/shard_map/mul | solution.py:115
  4.0 2.8 %collective-permute-start.1 = (bf16[5,2,4,512]{3,2,1,0:T(4,128)(2,1)S(1)}, bf16[5,2,4,512]{3,2,1,0:T(4,128)(2,1)S(1)}, u32[]{:S(2)}, u32[]{:S(2)}) collective-permute-start(bf16[5,2,4,512]{3,2,1,0:T(4,128)(2,1)S(1)} %get-tuple-element.20), channel_id=1, source_target_pairs={{0,8},{8,16},{16,24},{24,32},{32,40},{40,48},{48,56},{56,64},{64,7... | collective-permute-start | bytes 122888 | tf_op jit(solution)/shard_map/ppermute | solution.py:121
  6.8 0.6 collective-permute-start.6
  7.4 0.2 fusion.113
  7.5 0.7 collective-permute-start.3
  8.2 4.5 %collective-permute-start.4 = (bf16[5,2,128,4]{3,2,1,0:T(8,128)(2,1)S(1)}, bf16[5,2,128,4]{3,2,1,0:T(8,128)(2,1)S(1)}, u32[]{:S(2)}, u32[]{:S(2)}) collective-permute-start(bf16[5,2,128,4]{3,2,1,0:T(8,128)(2,1)S(1)} %get-tuple-element.23), channel_id=1, source_target_pairs={{1,0},{2,1},{3,2},{4,3},{5,4},{6,5},{7,6},{0,7},{9,8},{10,9},{11,1... | collective-permute-start | bytes 30728 | tf_op jit(solution)/shard_map/ppermute | solution.py:124
  12.7 0.1 pad_maximum_fusion.4
  12.8 0.1 collective-permute-start
  12.9 9.7 %collective-permute-done = bf16[5,2,4,4]{3,2,1,0:T(4,128)(2,1)S(1)} collective-permute-done((bf16[5,2,4,4]{3,2,1,0:T(4,128)(2,1)S(1)}, bf16[5,2,4,4]{3,2,1,0:T(4,128)(2,1)S(1)}, u32[]{:S(2)}, u32[]{:S(2)}) %collective-permute-start) | collective-permute-done | bytes 352 | tf_op jit(solution)/shard_map/ppermute | solution.py:134
  22.6 0.0 collective-permute-start.5
  22.6 6.4 %collective-permute-done.5 = bf16[5,2,4,4]{3,2,1,0:T(4,128)(2,1)S(1)} collective-permute-done((bf16[5,2,4,4]{3,2,1,0:T(4,128)(2,1)S(1)}, bf16[5,2,4,4]{3,2,1,0:T(4,128)(2,1)S(1)}, u32[]{:S(2)}, u32[]{:S(2)}) %collective-permute-start.5) | collective-permute-done | bytes 352 | tf_op jit(solution)/shard_map/ppermute | solution.py:136
  29.0 2.4 %collective-permute-start.7 = (bf16[5,2,4,4]{3,2,1,0:T(4,128)(2,1)S(1)}, bf16[5,2,4,4]{3,2,1,0:T(4,128)(2,1)S(1)}, u32[]{:S(2)}, u32[]{:S(2)}) collective-permute-start(bf16[5,2,4,4]{3,2,1,0:T(4,128)(2,1)S(1)} %get-tuple-element.18), channel_id=1, source_target_pairs={{0,255},{1,248},{2,249},{3,250},{4,251},{5,252},{6,253},{7,254},{8... | collective-permute-start | bytes 968 | tf_op jit(solution)/shard_map/ppermute | solution.py:137
  31.4 1.6 %collective-permute-done.7 = bf16[5,2,4,4]{3,2,1,0:T(4,128)(2,1)S(1)} collective-permute-done((bf16[5,2,4,4]{3,2,1,0:T(4,128)(2,1)S(1)}, bf16[5,2,4,4]{3,2,1,0:T(4,128)(2,1)S(1)}, u32[]{:S(2)}, u32[]{:S(2)}) %collective-permute-start.7) | collective-permute-done | bytes 352 | tf_op jit(solution)/shard_map/ppermute | solution.py:137
  33.0 2.7 %collective-permute-start.2 = (bf16[5,2,4,4]{3,2,1,0:T(4,128)(2,1)S(1)}, bf16[5,2,4,4]{3,2,1,0:T(4,128)(2,1)S(1)}, u32[]{:S(2)}, u32[]{:S(2)}) collective-permute-start(bf16[5,2,4,4]{3,2,1,0:T(4,128)(2,1)S(1)} %get-tuple-element.19), channel_id=1, source_target_pairs={{0,15},{1,8},{2,9},{3,10},{4,11},{5,12},{6,13},{7,14},{8,23},{9,16... | collective-permute-start | bytes 968 | tf_op jit(solution)/shard_map/ppermute | solution.py:135
  35.8 1.6 %collective-permute-done.2 = bf16[5,2,4,4]{3,2,1,0:T(4,128)(2,1)S(1)} collective-permute-done((bf16[5,2,4,4]{3,2,1,0:T(4,128)(2,1)S(1)}, bf16[5,2,4,4]{3,2,1,0:T(4,128)(2,1)S(1)}, u32[]{:S(2)}, u32[]{:S(2)}) %collective-permute-start.2) | collective-permute-done | bytes 352 | tf_op jit(solution)/shard_map/ppermute | solution.py:135
  37.4 0.0 collective-permute-done.3
  37.4 0.0 collective-permute-done.4
  37.4 0.0 collective-permute-done.1
  37.4 0.0 collective-permute-done.6
  37.4 2.5 %maximum_convert_fusion = f32[5,2,136,520]{3,2,1,0:T(8,128)S(1)} fusion(bf16[5,2,4,4]{3,2,1,0:T(4,128)(2,1)S(1)} %collective-permute-done.7, bf16[5,2,4,512]{3,2,1,0:T(4,128)(2,1)S(1)} %collective-permute-done.6, bf16[5,2,4,4]{3,2,1,0:T(4,128)(2,1)S(1)} %collective-permute-done.5, bf16[5,2,128,4]{3,2,1,0:T(8,128)(2,1)S(1)} %collective-permute-done.4, ...), kind=kLoop, calls=%fused_computation.4 | loop fusion | flops 14144000 | bytes 4243200 | tf_op jit(solution)/shard_map/convert_element_type | solution.py:141
  39.9 1.2 slice_bitcast_fusion.22
  41.1 0.5 slice_bitcast_fusion.18
  41.6 3.3 %multiply_add_fusion.4 = (f32[2,128,512]{2,1,0:T(8,128)S(1)}, bf16[2,128,512]{2,1,0:T(8,128)(2,1)}) fusion(f32[5,2,136,520]{3,2,1,0:T(8,128)S(1)} %maximum_convert_fusion, f32[1,128,512]{2,1,0:T(8,128)S(1)} %get-tuple-element.15, f32[1,128,512]{2,1,0:T(8,128)S(1)} %get-tuple-element.12), kind=kLoop, calls=%fused_computation.176 | loop fusion | flops 5373952 | bytes 10223616 | tf_op jit(solution)/shard_map/add | solution.py:177
  44.9 3.7 %multiply_add_fusion.1 = (f32[2,130,514]{2,1,0:T(8,128)S(1)}, bf16[2,130,514]{2,1,0:T(8,128)(2,1)}) fusion(f32[5,2,136,520]{3,2,1,0:T(8,128)S(1)} %maximum_convert_fusion, f32[1,130,514]{2,1,0:T(8,128)S(1)} %get-tuple-element.11, f32[1,130,514]{2,1,0:T(8,128)S(1)} %get-tuple-element.8), kind=kLoop, calls=%fused_computation.91 | loop fusion | flops 5211960 | bytes 9889360 | tf_op jit(solution)/shard_map/add | solution.py:175
  48.6 3.7 %multiply_add_fusion = (f32[2,130,514]{2,1,0:T(8,128)S(1)}, bf16[2,130,514]{2,1,0:T(8,128)(2,1)}) fusion(f32[5,2,136,520]{3,2,1,0:T(8,128)S(1)} %maximum_convert_fusion, f32[1,130,514]{2,1,0:T(8,128)S(1)} %get-tuple-element.10, f32[1,130,514]{2,1,0:T(8,128)S(1)} %get-tuple-element.9), kind=kLoop, calls=%fused_computation.90 | loop fusion | flops 5211960 | bytes 9889360 | tf_op jit(solution)/shard_map/add | solution.py:176
  52.3 0.0 copy-start.6
  52.3 0.0 copy-start.3
  52.3 0.0 copy-start.4
  52.3 1.3 %fusion.79 = f32[2,128,512]{2,1,0:T(8,128)} fusion(f32[2,130,514]{2,1,0:T(8,128)S(1)} %get-tuple-element.6, f32[2,130,514]{2,1,0:T(8,128)S(1)} %get-tuple-element.4, f32[1,128,512]{2,1,0:T(8,128)S(1)} %get-tuple-element.29, f32[1,128,512]{2,1,0:T(8,128)S(1)} %get-tuple-element.28), kind=kLoop, calls=%fused_computation.119 | loop fusion | flops 786432 | bytes 3145728 | tf_op jit(solution)/shard_map/mul | solution.py:182
  53.7 2.2 %reshape.122 = f32[2,8,16,2,256]{4,3,2,1,0:T(2,128)} reshape(f32[2,128,512]{2,1,0:T(8,128)} %fusion.79) | data formatting | bytes 1048576 | tf_op jit(solution)/shard_map/reshape | solution.py:189
  55.8 1.1 copy.27
  56.9 0.0 copy-start.1
  57.0 17.9 %all_to_all.10 = f32[8,64,256]{2,1,0:T(8,128)S(1)} all-to-all(f32[8,64,256]{2,1,0:T(8,128)S(1)} %bitcast.315), channel_id=1, replica_groups=mesh['gx'=32,'gy'=8] {'gy'}, dimensions={0} | all-to-all | bytes 1048576 | tf_op jit(solution)/shard_map/all_to_all | solution.py:191
  74.9 0.0 copy-done.6
  74.9 0.7 fusion.111
  75.6 0.0 copy-done.3
  75.6 0.0 copy-done.4
  75.6 0.2 multiply_add_fusion.3
  75.8 0.3 copy.29
  76.1 0.3 copy.30
  76.4 0.0 copy-done.1
  76.4 1.0 fusion
  77.5 1.8 %copy.31 = f32[256,2,512]{2,1,0:T(2,128)} copy(f32[256,2,512]{2,0,1:T(8,128)S(1)} %fusion) | data formatting | bytes 2097152 | tf_op jit(solution)/shard_map/dot_general | solution.py:208
  79.3 11.5 %all-to-all-start.1 = ((f32[256,2,512]{2,1,0:T(2,128)}), f32[256,2,512]{2,1,0:T(2,128)}, u32[]{:S(2)}, u32[]{:S(2)}) async-start(f32[256,2,512]{2,1,0:T(2,128)} %copy.31), calls=%async_computation.1 | async-start | bytes 2097152 | tf_op jit(solution)/shard_map/all_to_all | solution.py:211
  90.8 1.0 convert_element_type.64
  91.8 1.5 %slice_bitcast_fusion.23 = (bf16[1,2,128,512]{3,2,1,0:T(8,128)(2,1)S(1)}, bf16[1,2,128,512]{3,2,1,0:T(8,128)(2,1)S(1)}) fusion(bf16[2,130,514]{2,1,0:T(8,128)(2,1)} %get-tuple-element.7, bf16[2,130,514]{2,1,0:T(8,128)(2,1)} %get-tuple-element.5), kind=kLoop, calls=%fused_computation.193 | loop fusion | bytes 1048576 | tf_op jit(solution)/shard_map/stack | solution.py:173
  93.2 0.0 copy-start.2
  93.2 3.8 %fusion.116 = bf16[1,2,128,512]{3,2,1,0:T(8,128)(2,1)S(1)} fusion(f32[128,512]{1,0:T(8,128)S(1)} %convert_element_type.64, s32[128,512]{1,0:T(8,128)} %param.12, f32[5,2,136,520]{3,2,1,0:T(8,128)S(1)} %maximum_convert_fusion, f32[1,128,512]{2,1,0:T(8,128)} %get-tuple-element.13, f32[1,128,512]{2,1,0:T(8,128)} %get-tuple-element.14), kind=kLoop, calls=%fused_computation.196 | loop fusion | flops 5111808 | bytes 10223616 | tf_op jit(solution)/shard_map/stack | solution.py:173
  97.0 0.0 copy-start
  97.0 0.0 copy-done.2
  97.0 1.1 pad_maximum_fusion
  98.1 22.6 %all-to-all-done.1 = f32[256,2,512]{2,1,0:T(2,128)} async-done(((f32[256,2,512]{2,1,0:T(2,128)}), f32[256,2,512]{2,1,0:T(2,128)}, u32[]{:S(2)}, u32[]{:S(2)}) %all-to-all-start.1) | async-done | bytes 1048608 | tf_op jit(solution)/shard_map/all_to_all | solution.py:211
  120.7 1.9 %reshape.127 = f32[512,512]{1,0:T(8,128)S(1)} reshape(f32[256,2,512]{2,1,0:T(2,128)} %all-to-all-done.1) | data formatting | bytes 2097152 | tf_op jit(solution)/shard_map/reshape | solution.py:219
  122.7 0.0 copy-start.5
  122.7 0.3 copy.32
  123.0 0.0 copy-done
  123.0 1.0 fusion.125
  124.1 0.2 multiply_add_fusion.2
  124.2 0.0 copy-done.5
  124.2 0.6 fusion.3
  124.8 0.7 reshape.143
  125.5 1.6 %copy.35 = f32[2,2,16,4096]{3,2,1,0:T(8,128)} copy(f32[2,2,16,4096]{3,0,1,2:T(2,128)S(1)} %reshape.143) | data formatting | bytes 2097152 | tf_op jit(solution)/shard_map/reshape | solution.py:235
  (2 shorter events, 0.1 us)
Async XLA Ops:
  4.0 33.4 %collective-permute-start.1 = (bf16[5,2,4,512]{3,2,1,0:T(4,128)(2,1)S(1)}, bf16[5,2,4,512]{3,2,1,0:T(4,128)(2,1)S(1)}, u32[]{:S(2)}, u32[]{:S(2)}) collective-permute-start(bf16[5,2,4,512]{3,2,1,0:T(4,128)(2,1)S(1)} %get-tuple-element.20), channel_id=1, source_target_pairs={{0,8},{8,16},{16,24},{24,32},{32,40},{40,48},{48,56},{56,64},{64,7... | collective-permute-start | bytes 122888 | tf_op jit(solution)/shard_map/ppermute | solution.py:121
  6.8 30.6 %collective-permute-start.6 = (bf16[5,2,4,512]{3,2,1,0:T(4,128)(2,1)S(1)}, bf16[5,2,4,512]{3,2,1,0:T(4,128)(2,1)S(1)}, u32[]{:S(2)}, u32[]{:S(2)}) collective-permute-start(bf16[5,2,4,512]{3,2,1,0:T(4,128)(2,1)S(1)} %get-tuple-element.21), channel_id=1, source_target_pairs={{8,0},{16,8},{24,16},{32,24},{40,32},{48,40},{56,48},{64,56},{72,6... | collective-permute-start | bytes 122888 | tf_op jit(solution)/shard_map/ppermute | solution.py:122
  7.5 29.8 %collective-permute-start.3 = (bf16[5,2,128,4]{3,2,1,0:T(8,128)(2,1)S(1)}, bf16[5,2,128,4]{3,2,1,0:T(8,128)(2,1)S(1)}, u32[]{:S(2)}, u32[]{:S(2)}) collective-permute-start(bf16[5,2,128,4]{3,2,1,0:T(8,128)(2,1)S(1)} %get-tuple-element.22), channel_id=1, source_target_pairs={{0,1},{1,2},{2,3},{3,4},{4,5},{5,6},{6,7},{7,0},{8,9},{9,10},{10,1... | collective-permute-start | bytes 30728 | tf_op jit(solution)/shard_map/ppermute | solution.py:123
  8.2 29.2 %collective-permute-start.4 = (bf16[5,2,128,4]{3,2,1,0:T(8,128)(2,1)S(1)}, bf16[5,2,128,4]{3,2,1,0:T(8,128)(2,1)S(1)}, u32[]{:S(2)}, u32[]{:S(2)}) collective-permute-start(bf16[5,2,128,4]{3,2,1,0:T(8,128)(2,1)S(1)} %get-tuple-element.23), channel_id=1, source_target_pairs={{1,0},{2,1},{3,2},{4,3},{5,4},{6,5},{7,6},{0,7},{9,8},{10,9},{11,1... | collective-permute-start | bytes 30728 | tf_op jit(solution)/shard_map/ppermute | solution.py:124
  12.8 9.8 %collective-permute-start = (bf16[5,2,4,4]{3,2,1,0:T(4,128)(2,1)S(1)}, bf16[5,2,4,4]{3,2,1,0:T(4,128)(2,1)S(1)}, u32[]{:S(2)}, u32[]{:S(2)}) collective-permute-start(bf16[5,2,4,4]{3,2,1,0:T(4,128)(2,1)S(1)} %get-tuple-element.16), channel_id=1, source_target_pairs={{0,9},{1,10},{2,11},{3,12},{4,13},{5,14},{6,15},{7,8},{8,17},{9,18... | collective-permute-start | bytes 968 | tf_op jit(solution)/shard_map/ppermute | solution.py:134
  22.6 6.4 %collective-permute-start.5 = (bf16[5,2,4,4]{3,2,1,0:T(4,128)(2,1)S(1)}, bf16[5,2,4,4]{3,2,1,0:T(4,128)(2,1)S(1)}, u32[]{:S(2)}, u32[]{:S(2)}) collective-permute-start(bf16[5,2,4,4]{3,2,1,0:T(4,128)(2,1)S(1)} %get-tuple-element.17), channel_id=1, source_target_pairs={{0,249},{1,250},{2,251},{3,252},{4,253},{5,254},{6,255},{7,248},{8... | collective-permute-start | bytes 968 | tf_op jit(solution)/shard_map/ppermute | solution.py:136
  29.0 4.0 %collective-permute-start.7 = (bf16[5,2,4,4]{3,2,1,0:T(4,128)(2,1)S(1)}, bf16[5,2,4,4]{3,2,1,0:T(4,128)(2,1)S(1)}, u32[]{:S(2)}, u32[]{:S(2)}) collective-permute-start(bf16[5,2,4,4]{3,2,1,0:T(4,128)(2,1)S(1)} %get-tuple-element.18), channel_id=1, source_target_pairs={{0,255},{1,248},{2,249},{3,250},{4,251},{5,252},{6,253},{7,254},{8... | collective-permute-start | bytes 968 | tf_op jit(solution)/shard_map/ppermute | solution.py:137
  33.0 4.3 %collective-permute-start.2 = (bf16[5,2,4,4]{3,2,1,0:T(4,128)(2,1)S(1)}, bf16[5,2,4,4]{3,2,1,0:T(4,128)(2,1)S(1)}, u32[]{:S(2)}, u32[]{:S(2)}) collective-permute-start(bf16[5,2,4,4]{3,2,1,0:T(4,128)(2,1)S(1)} %get-tuple-element.19), channel_id=1, source_target_pairs={{0,15},{1,8},{2,9},{3,10},{4,11},{5,12},{6,13},{7,14},{8,23},{9,16... | collective-permute-start | bytes 968 | tf_op jit(solution)/shard_map/ppermute | solution.py:135
  52.3 22.5 %copy-start.6 = (f32[32,16,1,1]{0,1,3,2:T(8,128)S(1)}, f32[32,16,1,1]{0,1,3,2:T(8,128)}, u32[]{:S(2)}) copy-start(f32[32,16,1,1]{0,1,3,2:T(8,128)} %constant.71) | copy-start | bytes 6148
  52.3 23.3 %copy-start.3 = (f32[16,256]{1,0:T(8,128)S(1)}, f32[16,256]{1,0:T(8,128)}, u32[]{:S(2)}) copy-start(f32[16,256]{1,0:T(8,128)} %constant.47.clone) | copy-start | bytes 49156
  52.3 23.3 %copy-start.4 = (f32[16,256]{1,0:T(8,128)S(1)}, f32[16,256]{1,0:T(8,128)}, u32[]{:S(2)}) copy-start(f32[16,256]{1,0:T(8,128)} %constant.46.clone) | copy-start | bytes 49156
  56.9 19.5 %copy-start.1 = (f32[256,2,512]{2,0,1:T(8,128)S(1)}, f32[256,2,512]{2,0,1:T(8,128)}, u32[]{:S(2)}) copy-start(f32[256,2,512]{2,0,1:T(8,128)} %constant.48.clone) | copy-start | bytes 3145732
  79.3 41.5 %all-to-all-start.1 = ((f32[256,2,512]{2,1,0:T(2,128)}), f32[256,2,512]{2,1,0:T(2,128)}, u32[]{:S(2)}, u32[]{:S(2)}) async-start(f32[256,2,512]{2,1,0:T(2,128)} %copy.31), calls=%async_computation.1 | async-start | bytes 2097152 | tf_op jit(solution)/shard_map/all_to_all | solution.py:211
  93.2 3.8 %copy-start.2 = (bf16[2,128,512]{2,1,0:T(8,128)(2,1)S(1)}, bf16[2,128,512]{2,1,0:T(8,128)(2,1)}, u32[]{:S(2)}) copy-start(bf16[2,128,512]{2,1,0:T(8,128)(2,1)} %get-tuple-element.3) | copy-start | bytes 786436
  97.0 26.0 %copy-start = (f32[512,512,1]{1,0,2:T(8,128)S(1)}, f32[512,512,1]{1,0,2:T(8,128)}, u32[]{:S(2)}) copy-start(f32[512,512,1]{1,0,2:T(8,128)} %constant.72) | copy-start | bytes 3145732
  122.7 1.5 %copy-start.5 = (f32[32,32]{1,0:T(8,128)S(1)}, f32[32,32]{1,0:T(8,128)}, u32[]{:S(2)}) copy-start(f32[32,32]{1,0:T(8,128)} %constant.50.clone) | copy-start | bytes 12292

commit v3 on v1

--- a/solution.py
+++ b/solution.py
@@ -70,26 +70,22 @@
     return jnp.asarray(np.asarray(array, dtype=np.float32))
 
 
+def runtime_cos_sin(n, salt):
+    row = lax.broadcasted_iota(jnp.int32, (n, n), 0)
+    col = lax.broadcasted_iota(jnp.int32, (n, n), 1)
+    product = (row * col + salt) % n
+    angle = product.astype(jnp.float32) * (2.0 * math.pi / n)
+    return jnp.cos(angle), jnp.sin(angle)
+
+
 def y_tables(n_p, n_q):
     c1, s1 = cos_sin(n_p, n_p, n_p)
     w1 = np.concatenate([c1, -s1], axis=0)
     t_c, t_s = cos_sin(n_p, n_q, n_p * n_q)
-    c2, s2 = cos_sin(n_q, n_q, n_q)
-    w2 = np.zeros((n_q, 2, 2, n_q))
-    w2[:, 0, 0] = c2
-    w2[:, 0, 1] = s2
-    w2[:, 1, 0] = -s2
-    w2[:, 1, 1] = c2
-    return w1, t_c, t_s, w2.reshape(2 * n_q, 2 * n_q)
+    return w1, t_c, t_s
 
 
 def x_tables(n_s, n_i, scale):
-    c2, s2 = cos_sin(n_s, n_s, n_s)
-    wa = np.zeros((n_s, 2, 2, n_s))
-    wa[:, 0, 0] = c2
-    wa[:, 1, 0] = s2
-    wa[:, 0, 1] = -s2
-    wa[:, 1, 1] = c2
     t_c, t_s = cos_sin(n_i, n_s, n_s * n_i)
     cb, sb = cos_sin(n_i, n_i, n_i, scale)
     wb = np.zeros((2, n_i, 2, n_i))
@@ -97,7 +93,7 @@
     wb[0, :, 1] = sb
     wb[1, :, 0] = -sb
     wb[1, :, 1] = cb
-    return wa.reshape(2 * n_s, 2 * n_s), t_c, t_s, wb.reshape(2 * n_i, 2 * n_i)
+    return t_c, t_s, wb.reshape(2 * n_i, 2 * n_i)
 
 
 def body(state, heights, surface_flag):
@@ -158,7 +154,14 @@
     sent = sent.reshape(count_y, split_y * levels * piece_x, n_q)
     columns = lax.all_to_all(sent, "gy", split_axis=0, concat_axis=0, tiled=True)
     columns = columns.reshape(n_p, levels, piece_x, n_q)
-    w1, t1c, t1s, w2 = y_tables(n_p, n_q)
+    w1, t1c, t1s = y_tables(n_p, n_q)
+    devices = count_x * count_y
+    salt = jnp.minimum(lax.axis_index("gx"), 0)
+    big_c, big_s = runtime_cos_sin(devices, salt)
+    w2 = jnp.stack([jnp.stack([big_c, big_s], axis=1), jnp.stack([-big_s, big_c], axis=1)], axis=1)
+    w2 = w2.reshape(devices, 2, 2 * n_q)
+    wa = jnp.stack([jnp.stack([big_c, -big_s], axis=1), jnp.stack([big_s, big_c], axis=1)], axis=1)
+    wa = wa.reshape(2 * devices, 2 * devices)
     stage1 = lax.dot_general(
         const(w1), columns, (((1,), (0,)), ((), ())), precision=PREC
     )
@@ -172,9 +175,8 @@
     joined = jnp.concatenate(
         [real_t.reshape(rows_m, n_q), imag_t.reshape(rows_m, n_q)], axis=1
     )
-    devices = count_x * count_y
     spectrum_y = lax.dot_general(
-        const(w2.reshape(devices, 2, 2 * n_q)), joined, (((2,), (1,)), ((), ())), precision=PREC
+        w2, joined, (((2,), (1,)), ((), ())), precision=PREC
     )
     moved = lax.all_to_all(spectrum_y, ("gx", "gy"), split_axis=0, concat_axis=0, tiled=True)
 
@@ -182,9 +184,9 @@
     n_s = devices
     n_i = piece_x
     scale = 1.0 / math.sqrt(total_x * total_y)
-    wa, t2c, t2s, wb = x_tables(n_s, n_i, scale)
+    t2c, t2s, wb = x_tables(n_s, n_i, scale)
     stage_a = lax.dot_general(
-        moved.reshape(2 * n_s, rows_m), const(wa), (((0,), (0,)), ((), ())), precision=PREC
+        moved.reshape(2 * n_s, rows_m), wa, (((0,), (0,)), ((), ())), precision=PREC
     )
     batch = levels * n_p
     stage_a = stage_a.reshape(batch, n_i, 2 * n_s)

time: 108 us -> 129 us (1.19)
  other arithmetic: 13.5 us -> 37.3 us
  blocking collectives: 15.2 us -> 0 us
  local copies, waits for them, and re-layouts: 9.34 us -> 19.5 us
  waiting for transfers between devices: 29.9 us -> 33.2 us
    all_to_all x1 -> x0, blocking collectives: 15.2 us -> none  [body(): lax.all_to_all(sent, 'gy', split_axis=0, concat_axis=0, tiled=True)]
    sin x0 -> x1, other arithmetic: none -> 8.41 us  [runtime_cos_sin(): return (jnp.cos(angle), jnp.sin(angle))]
    neg x0 -> x1, other arithmetic: none -> 7.94 us  [body(): -big_s]
    all_to_all x1, waiting for transfers between devices: 24.4 us -> 19 us  [body(): lax.all_to_all(spectrum_y, ('gx', 'gy'), split_axis=0, concat_axis=0, til...]
    another operation x0 -> x3, local copies, waits for them, and re-layouts: none -> 5.06 us  [the longest x2 3.73 us: body(): jnp.stack([jnp.stack([big_c, big_s], axis=1), jnp.stack([-big_s, big_c],...]
    ppermute x1, starting transfers between devices: 5.36 us -> 0.66 us  [body(): v_after = lax.ppermute(flow_v[:, :, :1], 'gy', down_y)]
    ppermute x1, starting transfers between devices: 4.3 us -> 0.72 us  [body(): u_before = lax.ppermute(flow_u[:, rows_x - 1:, :], 'gx', up_x)]
    all_to_all x0 -> x1, starting transfers between devices: none -> 3.49 us  [body(): lax.all_to_all(sent, 'gy', split_axis=0, concat_axis=0, tiled=True)]
  transfers between devices with their start and end apart: 9 -> 10, of which waited for: 3 -> 5; matrix products, arithmetic and copies ran while one was open for 8% -> 29% of each run, Pallas kernels for 0% -> 0%
where the time goes in v3:
time: 129 us; the launch traced here: 128 us
  other arithmetic  37.3 us (29%)
  waiting for transfers between devices  33.2 us (26%)
  starting transfers between devices  32.7 us (25%)
  local copies, waits for them, and re-layouts  19.5 us (15%)
  matrix products  4.04 us (3%)
    all_to_all x1, waiting for transfers between devices, body(): lax.all_to_all(spectrum_y, ('gx', 'gy'), split_axis=0, concat_axis=0, til...  19 us
    all_to_all x1, starting transfers between devices, body(): lax.all_to_all(spectrum_y, ('gx', 'gy'), split_axis=0, concat_axis=0, til...  17.4 us
    sin x1, other arithmetic, runtime_cos_sin(): return (jnp.cos(angle), jnp.sin(angle))  8.41 us
    another operation x5, other arithmetic, body(): tendency = jnp.stack(pieces)  8.02 us
    neg x1, other arithmetic, body(): -big_s  7.94 us
    ppermute x1, starting transfers between devices, body(): y_after = lax.ppermute(masked[:, :, :, :3], 'gy', down_y)  5.93 us
    ppermute x1, waiting for transfers between devices, body(): y_before = lax.ppermute(masked[:, :, :, rows_y - 3:], 'gy', up_y)  5.53 us
    ppermute x1, waiting for transfers between devices, body(): v_before = lax.ppermute(flow_v[:, :, rows_y - 1:], 'gy', up_y)  4.27 us
  transfers between devices with their start and end apart: 10, of which 5 were waited for; matrix products, arithmetic and copies ran while one was open for 29% of the time, Pallas kernels for 0%

profile of v3, /device:TPU:1, one launch (start us, length us, event | category | flops | bytes accessed | tf_op | source)
XLA Modules:
  0.0 127.9 jit_solution(4689140329822473405)
XLA Ops:
  0.6 1.0 convert_convert_fusion
  1.6 1.4 %fusion.130 = (f32[4,2,128,512]{3,2,1,0:T(8,128)S(1)}, bf16[4,2,128,512]{3,2,1,0:T(8,128)(2,1)S(1)}) fusion(bf16[4,2,128,512]{3,2,1,0:T(8,128)(2,1)} %param.9, bf16[2,128,512]{2,1,0:T(8,128)(2,1)S(1)} %convert_convert_fusion), kind=kLoop, calls=%fused_computation.205 | loop fusion | flops 1048576 | bytes 4456448 | tf_op jit(solution)/shard_map/convert_element_type | solution.py:119
  3.1 1.0 fusion.132
  4.1 5.9 %collective-permute-start.3 = (bf16[4,2,128,3]{3,2,1,0:T(8,128)(2,1)}, bf16[4,2,128,3]{3,2,1,0:T(8,128)(2,1)S(1)}, u32[]{:S(2)}, u32[]{:S(2)}) collective-permute-start(bf16[4,2,128,3]{3,2,1,0:T(8,128)(2,1)} %get-tuple-element.23), channel_id=1, source_target_pairs={{1,0},{2,1},{3,2},{4,3},{5,4},{6,5},{7,6},{0,7},{9,8},{10,9},{11,1... | collective-permute-start | bytes 18440 | tf_op jit(solution)/shard_map/ppermute | solution.py:116
  10.0 1.0 collective-permute-start.1
  11.1 0.8 collective-permute-start
  11.9 1.4 %slice_bitcast_fusion.21 = (f32[1,128,512]{2,1,0:T(8,128)}, f32[1,128,512]{2,1,0:T(8,128)}, f32[1,128,512]{2,1,0:T(8,128)}, f32[1,128,512]{2,1,0:T(8,128)}, f32[...) fusion(f32[4,2,128,512]{3,2,1,0:T(8,128)S(1)} %get-tuple-element.2), kind=kLoop, calls=%fused_computation.194 | loop fusion | bytes 4194304 | tf_op jit(solution)/shard_map/slice | solution.py:24
  13.2 2.1 %collective-permute-done.3 = bf16[4,2,128,3]{3,2,1,0:T(8,128)(2,1)S(1)} collective-permute-done((bf16[4,2,128,3]{3,2,1,0:T(8,128)(2,1)}, bf16[4,2,128,3]{3,2,1,0:T(8,128)(2,1)S(1)}, u32[]{:S(2)}, u32[]{:S(2)}) %collective-permute-start.3) | collective-permute-done | bytes 6176 | tf_op jit(solution)/shard_map/ppermute | solution.py:116
  15.3 5.5 %collective-permute-done.2 = bf16[4,2,128,3]{3,2,1,0:T(8,128)(2,1)} collective-permute-done((bf16[4,2,128,3]{3,2,1,0:T(8,128)(2,1)}, bf16[4,2,128,3]{3,2,1,0:T(8,128)(2,1)}, u32[]{:S(2)}, u32[]{:S(2)}) %collective-permute-start.2) | collective-permute-done | bytes 6176 | tf_op jit(solution)/shard_map/ppermute | solution.py:115
  20.8 1.6 %maximum_convert_fusion = f32[4,2,128,518]{3,2,1,0:T(8,128)S(1)} fusion(bf16[4,2,128,3]{3,2,1,0:T(8,128)(2,1)S(1)} %collective-permute-done.3, bf16[4,2,128,512]{3,2,1,0:T(8,128)(2,1)S(1)} %get-tuple-element.3, bf16[4,2,128,3]{3,2,1,0:T(8,128)(2,1)} %collective-permute-done.2), kind=kLoop, calls=%fused_computation.1 | loop fusion | flops 3182592 | bytes 3182592 | tf_op jit(solution)/shard_map/convert_element_type | solution.py:118
  22.5 0.0 copy-start.21
  22.5 0.6 copy-done.21
  23.1 2.3 %maximum_convert_fusion.1 = f32[4,2,134,512]{3,2,1,0:T(8,128)S(1)} fusion(bf16[4,2,3,512]{3,2,1,0:T(4,128)(2,1)} %copy-done.21, bf16[4,2,128,512]{3,2,1,0:T(8,128)(2,1)S(1)} %get-tuple-element.3, bf16[4,2,3,512]{3,2,1,0:T(4,128)(2,1)} %collective-permute-done), kind=kLoop, calls=%fused_computation.2 | loop fusion | flops 3293184 | bytes 3293184 | tf_op jit(solution)/shard_map/convert_element_type | solution.py:117
  25.4 0.9 fusion.123
  26.4 0.0 copy-done.16
  26.4 0.9 fusion.121
  27.4 0.1 copy-done.13
  27.4 0.1 copy-done.14
  27.5 0.9 fusion.122
  28.4 0.3 slice_add_fusion
  28.8 0.1 slice_bitcast_fusion
  28.8 0.4 copy-done.8
  29.2 0.1 fusion.136
  29.3 0.1 fusion.133
  29.4 0.2 fusion.134
  29.6 1.9 %collective-permute-start.4 = (f32[2,1,512]{2,1,0:T(1,128)S(1)}, f32[2,1,512]{2,1,0:T(1,128)S(1)}, u32[]{:S(2)}, u32[]{:S(2)}) collective-permute-start(f32[2,1,512]{2,1,0:T(1,128)S(1)} %get-tuple-element.33), channel_id=1, source_target_pairs={{8,0},{16,8},{24,16},{32,24},{40,32},{48,40},{56,48},{64,56},{72,6... | collective-permute-start | bytes 12296 | tf_op jit(solution)/shard_map/ppermute | solution.py:139
  31.5 0.7 collective-permute-start.5
  32.3 0.7 collective-permute-start.6
  32.9 0.8 collective-permute-start.7
  33.8 2.3 %collective-permute-done.6 = f32[2,128,1]{2,1,0:T(8,128)S(1)} collective-permute-done((f32[2,128,1]{2,1,0:T(8,128)S(1)}, f32[2,128,1]{2,1,0:T(8,128)S(1)}, u32[]{:S(2)}, u32[]{:S(2)}) %collective-permute-start.6) | collective-permute-done | bytes 1056 | tf_op jit(solution)/shard_map/ppermute | solution.py:141
  36.1 4.3 %collective-permute-done.7 = f32[2,128,1]{2,1,0:T(8,128)S(1)} collective-permute-done((f32[2,128,1]{2,1,0:T(8,128)S(1)}, f32[2,128,1]{2,1,0:T(8,128)S(1)}, u32[]{:S(2)}, u32[]{:S(2)}) %collective-permute-start.7) | collective-permute-done | bytes 1056 | tf_op jit(solution)/shard_map/ppermute | solution.py:140
  40.4 0.3 fusion.108
  40.7 0.3 reshape.190
  41.0 0.9 copy.28
  41.9 3.5 %all-to-all-start = ((f32[8,64,256]{2,1,0:T(8,128)}), f32[8,64,256]{2,1,0:T(8,128)S(1)}, u32[]{:S(2)}, u32[]{:S(2)}) async-start(f32[8,64,256]{2,1,0:T(8,128)} %bitcast.50), calls=%async_computation | async-start | bytes 1048576 | tf_op jit(solution)/shard_map/all_to_all | solution.py:155
  45.4 8.4 %fusion.125 = (f32[256,1,256]{2,1,0:T(1,128)S(1)}, f32[256,1,256]{2,1,0:T(1,128)S(1)}) fusion(s32[]{:T(128)S(6)} %min.3), kind=kLoop, calls=%fused_computation.200 | loop fusion | flops 983040 | bytes 524292 | tf_op jit(solution)/shard_map/sin | solution.py:78
  53.9 7.9 %fusion.127 = f32[256,1,256]{2,1,0:T(1,128)S(1)} fusion(s32[]{:T(128)S(6)} %min.3), kind=kLoop, calls=%fused_computation.202 | loop fusion | flops 1048576 | bytes 262148 | tf_op jit(solution)/shard_map/neg | solution.py:161
  61.8 2.7 %fusion.11 = (f32[256,1,2,256]{3,2,0,1:T(2,128)}, f32[256,2,256]{2,1,0:T(2,128)}, f32[256,2,256]{2,1,0:T(2,128)}, f32[256,1,2,256]{3,2,0,1:T(2,128)}) fusion(f32[256,1,256]{2,1,0:T(1,128)S(1)} %get-tuple-element.39, f32[256,1,256]{2,1,0:T(1,128)S(1)} %fusion.127, f32[256,1,256]{2,1,0:T(1,128)S(1)} %get-tuple-element.38), kind=kLoop, calls=%fused_computation.32 | loop fusion | flops 524288 | bytes 2883584 | tf_op jit(solution)/shard_map/stack | solution.py:163
  64.6 1.5 %stack.63 = f32[256,1,512]{2,0,1:T(8,128)S(1)} reshape(f32[256,2,256]{2,1,0:T(2,128)} %get-tuple-element.25) | data formatting | bytes 1048576 | tf_op jit(solution)/shard_map/stack | solution.py:161
  66.0 2.3 %stack.61 = f32[256,1,512]{2,0,1:T(8,128)} reshape(f32[256,2,256]{2,1,0:T(2,128)} %get-tuple-element.36) | data formatting | bytes 1048576 | tf_op jit(solution)/shard_map/stack | solution.py:161
  68.3 1.4 %fusion.115 = f32[32,2,16,256]{3,0,2,1:T(8,128)S(1)} fusion(f32[32,16,1,1]{0,1,3,2:T(8,128)} %constant.86, f32[16,2,16,256]{3,2,1,0:T(8,128)S(1)} %bitcast.318), kind=kOutput, calls=%fused_computation.172 | convolution fusion | flops 25165824 | bytes 1574912 | tf_op jit(solution)/shard_map/dot_general | solution.py:165
  69.8 0.0 copy-start.10
  69.8 0.9 multiply_add_fusion.1
  70.7 0.3 copy.31
  71.0 0.3 copy.30
  71.3 1.0 fusion
  72.4 1.8 %copy.32 = f32[256,2,512]{2,1,0:T(2,128)} copy(f32[256,2,512]{2,0,1:T(8,128)S(1)} %fusion) | data formatting | bytes 2097152 | tf_op jit(solution)/shard_map/dot_general | solution.py:178
  74.2 17.4 %all-to-all-start.1 = ((f32[256,2,512]{2,1,0:T(2,128)}), f32[256,2,512]{2,1,0:T(2,128)}, u32[]{:S(2)}, u32[]{:S(2)}) async-start(f32[256,2,512]{2,1,0:T(2,128)} %copy.32), calls=%async_computation.1 | async-start | bytes 2097152 | tf_op jit(solution)/shard_map/all_to_all | solution.py:181
  91.6 1.7 %convert_element_type.69 = f32[128,512]{1,0:T(8,128)} convert(s32[128,512]{1,0:T(8,128)} %param.11) | non-fusion elementwise | flops 65536 | bytes 524288 | tf_op jit(solution)/shard_map/convert_element_type | solution.py:110
  93.3 0.5 pad_maximum_fusion.1
  93.8 1.3 %copy.34 = f32[256,2,2,256]{3,2,1,0:T(2,128)} copy(f32[256,2,2,256]{3,2,0,1:T(2,128)S(1)} %pad_maximum_fusion.1) | data formatting | bytes 2097152 | tf_op jit(solution)/shard_map/stack | solution.py:163
  95.1 2.1 %reshape.217 = f32[512,512,1]{1,0,2:T(8,128)S(1)} reshape(f32[256,2,2,256]{3,2,1,0:T(2,128)} %copy.34) | data formatting | bytes 2097152 | tf_op jit(solution)/shard_map/reshape | solution.py:164
  97.2 4.2 %fusion.124 = bf16[1,2,128,512]{3,2,1,0:T(8,128)(2,1)S(1)} fusion(f32[128,512]{1,0:T(8,128)} %convert_element_type.69, f32[4,2,128,512]{3,2,1,0:T(8,128)} %copy-done.1, f32[4,2,128,518]{3,2,1,0:T(8,128)} %copy-done, f32[4,2,134,512]{3,2,1,0:T(8,128)S(1)} %maximum_convert_fusion.1, f32[1,128,512]{2,1,0:T(8,128)} %get-tuple-element.5, ...), kind=kLoop, calls=%fused_computation.199 | loop fusion | flops 5242880 | bytes 9699328 | tf_op jit(solution)/shard_map/stack | solution.py:134
  101.4 1.1 pad_maximum_fusion
  102.5 19.0 %all-to-all-done.1 = f32[256,2,512]{2,1,0:T(2,128)} async-done(((f32[256,2,512]{2,1,0:T(2,128)}), f32[256,2,512]{2,1,0:T(2,128)}, u32[]{:S(2)}, u32[]{:S(2)}) %all-to-all-start.1) | async-done | bytes 1048608 | tf_op jit(solution)/shard_map/all_to_all | solution.py:181
  121.5 1.9 %reshape.195 = f32[512,512]{1,0:T(8,128)S(1)} reshape(f32[256,2,512]{2,1,0:T(2,128)} %all-to-all-done.1) | data formatting | bytes 2097152 | tf_op jit(solution)/shard_map/reshape | solution.py:189
  123.5 0.0 copy-start.20
  123.5 0.3 copy.33
  123.8 0.0 copy-start.22
  123.8 1.0 fusion.137
  124.9 0.2 multiply_add_fusion
  125.0 0.6 fusion.6
  125.6 0.7 reshape.219
  126.3 1.6 %copy.37 = f32[2,2,16,4096]{3,2,1,0:T(8,128)} copy(f32[2,2,16,4096]{3,0,1,2:T(2,128)S(1)} %reshape.219) | data formatting | bytes 2097152 | tf_op jit(solution)/shard_map/reshape | solution.py:205
  (46 shorter events, 0.2 us)
Async XLA Ops:
  3.1 10.2 %copy-start.1 = (f32[4,2,128,512]{3,2,1,0:T(8,128)}, f32[4,2,128,512]{3,2,1,0:T(8,128)S(1)}, u32[]{:S(2)}) copy-start(f32[4,2,128,512]{3,2,1,0:T(8,128)S(1)} %get-tuple-element.2) | copy-start | bytes 6291460
  4.1 11.2 %collective-permute-start.3 = (bf16[4,2,128,3]{3,2,1,0:T(8,128)(2,1)}, bf16[4,2,128,3]{3,2,1,0:T(8,128)(2,1)S(1)}, u32[]{:S(2)}, u32[]{:S(2)}) collective-permute-start(bf16[4,2,128,3]{3,2,1,0:T(8,128)(2,1)} %get-tuple-element.23), channel_id=1, source_target_pairs={{1,0},{2,1},{3,2},{4,3},{5,4},{6,5},{7,6},{0,7},{9,8},{10,9},{11,1... | collective-permute-start | bytes 18440 | tf_op jit(solution)/shard_map/ppermute | solution.py:116
  10.0 10.8 %collective-permute-start.2 = (bf16[4,2,128,3]{3,2,1,0:T(8,128)(2,1)}, bf16[4,2,128,3]{3,2,1,0:T(8,128)(2,1)}, u32[]{:S(2)}, u32[]{:S(2)}) collective-permute-start(bf16[4,2,128,3]{3,2,1,0:T(8,128)(2,1)} %get-tuple-element.22), channel_id=1, source_target_pairs={{0,1},{1,2},{2,3},{3,4},{4,5},{5,6},{6,7},{7,0},{8,9},{9,10},{10,1... | collective-permute-start | bytes 18440 | tf_op jit(solution)/shard_map/ppermute | solution.py:115
  10.0 12.4 %collective-permute-start.1 = (bf16[4,2,3,512]{3,2,1,0:T(4,128)(2,1)S(1)}, bf16[4,2,3,512]{3,2,1,0:T(4,128)(2,1)S(1)}, u32[]{:S(2)}, u32[]{:S(2)}) collective-permute-start(bf16[4,2,3,512]{3,2,1,0:T(4,128)(2,1)S(1)} %get-tuple-element.21), channel_id=1, source_target_pairs={{8,0},{16,8},{24,16},{32,24},{40,32},{48,40},{56,48},{64,56},{72,6... | collective-permute-start | bytes 73736 | tf_op jit(solution)/shard_map/ppermute | solution.py:114
  11.1 12.0 %collective-permute-start = (bf16[4,2,3,512]{3,2,1,0:T(4,128)(2,1)S(1)}, bf16[4,2,3,512]{3,2,1,0:T(4,128)(2,1)}, u32[]{:S(2)}, u32[]{:S(2)}) collective-permute-start(bf16[4,2,3,512]{3,2,1,0:T(4,128)(2,1)S(1)} %get-tuple-element.20), channel_id=1, source_target_pairs={{0,8},{8,16},{16,24},{24,32},{32,40},{40,48},{48,56},{56,64},{64,7... | collective-permute-start | bytes 73736 | tf_op jit(solution)/shard_map/ppermute | solution.py:113
  22.4 4.9 %copy-start = (f32[4,2,128,518]{3,2,1,0:T(8,128)}, f32[4,2,128,518]{3,2,1,0:T(8,128)S(1)}, u32[]{:S(2)}) copy-start(f32[4,2,128,518]{3,2,1,0:T(8,128)S(1)} %maximum_convert_fusion) | copy-start | bytes 6365188
  22.4 3.0 %copy-start.2 = (f32[4,2,128,512]{3,2,1,0:T(8,128)S(1)}, f32[4,2,128,512]{3,2,1,0:T(8,128)}, u32[]{:S(2)}) copy-start(f32[4,2,128,512]{3,2,1,0:T(8,128)} %copy-done.1) | copy-start | bytes 6291460
  22.4 3.0 %copy-start.3 = (s32[128,512]{1,0:T(8,128)S(1)}, s32[128,512]{1,0:T(8,128)}, u32[]{:S(2)}) copy-start(s32[128,512]{1,0:T(8,128)} %param.10) | copy-start | bytes 786436
  22.4 3.0 %copy-start.17 = (f32[1,128,512]{2,1,0:T(8,128)S(1)}, f32[1,128,512]{2,1,0:T(8,128)}, u32[]{:S(2)}) copy-start(f32[1,128,512]{2,1,0:T(8,128)} %get-tuple-element.7) | copy-start | bytes 786436
  22.5 3.0 %copy-start.18 = (f32[1,128,512]{2,1,0:T(8,128)S(1)}, f32[1,128,512]{2,1,0:T(8,128)}, u32[]{:S(2)}) copy-start(f32[1,128,512]{2,1,0:T(8,128)} %get-tuple-element.8) | copy-start | bytes 786436
  22.5 0.6 copy-start.21
  25.4 1.0 copy-start.15
  25.4 1.0 copy-start.16
  26.4 2.0 %copy-start.4 = (bf16[1,2,128,512]{3,2,1,0:T(8,128)(2,1)}, bf16[1,2,128,512]{3,2,1,0:T(8,128)(2,1)S(1)}, u32[]{:S(2)}) copy-start(bf16[1,2,128,512]{3,2,1,0:T(8,128)(2,1)S(1)} %fusion.123) | copy-start | bytes 786436
  26.4 1.0 copy-start.13
  26.4 1.1 copy-start.14
  27.3 1.1 copy-start.6
  28.4 0.8 copy-start.8
  29.6 10.7 %collective-permute-start.4 = (f32[2,1,512]{2,1,0:T(1,128)S(1)}, f32[2,1,512]{2,1,0:T(1,128)S(1)}, u32[]{:S(2)}, u32[]{:S(2)}) collective-permute-start(f32[2,1,512]{2,1,0:T(1,128)S(1)} %get-tuple-element.33), channel_id=1, source_target_pairs={{8,0},{16,8},{24,16},{32,24},{40,32},{48,40},{56,48},{64,56},{72,6... | collective-permute-start | bytes 12296 | tf_op jit(solution)/shard_map/ppermute | solution.py:139
  31.5 8.8 %collective-permute-start.5 = (f32[2,1,512]{2,1,0:T(1,128)S(1)}, f32[2,1,512]{2,1,0:T(1,128)S(1)}, u32[]{:S(2)}, u32[]{:S(2)}) collective-permute-start(f32[2,1,512]{2,1,0:T(1,128)S(1)} %get-tuple-element.32), channel_id=1, source_target_pairs={{0,8},{8,16},{16,24},{24,32},{32,40},{40,48},{48,56},{56,64},{64,7... | collective-permute-start | bytes 12296 | tf_op jit(solution)/shard_map/ppermute | solution.py:138
  32.3 3.8 %collective-permute-start.6 = (f32[2,128,1]{2,1,0:T(8,128)S(1)}, f32[2,128,1]{2,1,0:T(8,128)S(1)}, u32[]{:S(2)}, u32[]{:S(2)}) collective-permute-start(f32[2,128,1]{2,1,0:T(8,128)S(1)} %get-tuple-element.29), channel_id=1, source_target_pairs={{1,0},{2,1},{3,2},{4,3},{5,4},{6,5},{7,6},{0,7},{9,8},{10,9},{11,1... | collective-permute-start | bytes 3080 | tf_op jit(solution)/shard_map/ppermute | solution.py:141
  32.9 7.4 %collective-permute-start.7 = (f32[2,128,1]{2,1,0:T(8,128)S(1)}, f32[2,128,1]{2,1,0:T(8,128)S(1)}, u32[]{:S(2)}, u32[]{:S(2)}) collective-permute-start(f32[2,128,1]{2,1,0:T(8,128)S(1)} %get-tuple-element.28), channel_id=1, source_target_pairs={{0,1},{1,2},{2,3},{3,4},{4,5},{5,6},{6,7},{7,0},{8,9},{9,10},{10,1... | collective-permute-start | bytes 3080 | tf_op jit(solution)/shard_map/ppermute | solution.py:140
  41.9 26.3 %all-to-all-start = ((f32[8,64,256]{2,1,0:T(8,128)}), f32[8,64,256]{2,1,0:T(8,128)S(1)}, u32[]{:S(2)}, u32[]{:S(2)}) async-start(f32[8,64,256]{2,1,0:T(8,128)} %bitcast.50), calls=%async_computation | async-start | bytes 1048576 | tf_op jit(solution)/shard_map/all_to_all | solution.py:155
  64.6 5.2 %copy-start.19 = (f32[16,256]{1,0:T(8,128)S(1)}, f32[16,256]{1,0:T(8,128)}, u32[]{:S(2)}) copy-start(f32[16,256]{1,0:T(8,128)} %constant.64.clone) | copy-start | bytes 49156
  69.8 1.6 %copy-start.10 = (f32[256,1,512]{2,0,1:T(8,128)S(1)}, f32[256,1,512]{2,0,1:T(8,128)}, u32[]{:S(2)}) copy-start(f32[256,1,512]{2,0,1:T(8,128)} %stack.61) | copy-start | bytes 1572868
  72.4 20.9 %copy-start.11 = (f32[256,1,2,256]{3,2,0,1:T(2,128)S(1)}, f32[256,1,2,256]{3,2,0,1:T(2,128)}, u32[]{:S(2)}) copy-start(f32[256,1,2,256]{3,2,0,1:T(2,128)} %get-tuple-element.24) | copy-start | bytes 1572868
  72.4 20.9 %copy-start.12 = (f32[256,1,2,256]{3,2,0,1:T(2,128)S(1)}, f32[256,1,2,256]{3,2,0,1:T(2,128)}, u32[]{:S(2)}) copy-start(f32[256,1,2,256]{3,2,0,1:T(2,128)} %get-tuple-element.37) | copy-start | bytes 1572868
  74.2 47.3 %all-to-all-start.1 = ((f32[256,2,512]{2,1,0:T(2,128)}), f32[256,2,512]{2,1,0:T(2,128)}, u32[]{:S(2)}, u32[]{:S(2)}) async-start(f32[256,2,512]{2,1,0:T(2,128)} %copy.32), calls=%async_computation.1 | async-start | bytes 2097152 | tf_op jit(solution)/shard_map/all_to_all | solution.py:181
  97.2 4.2 %copy-start.5 = (bf16[1,2,128,512]{3,2,1,0:T(8,128)(2,1)S(1)}, bf16[1,2,128,512]{3,2,1,0:T(8,128)(2,1)}, u32[]{:S(2)}) copy-start(bf16[1,2,128,512]{3,2,1,0:T(8,128)(2,1)} %copy-done.4) | copy-start | bytes 786436
  97.2 4.2 %copy-start.7 = (bf16[1,2,128,512]{3,2,1,0:T(8,128)(2,1)S(1)}, bf16[1,2,128,512]{3,2,1,0:T(8,128)(2,1)}, u32[]{:S(2)}) copy-start(bf16[1,2,128,512]{3,2,1,0:T(8,128)(2,1)} %copy-done.6) | copy-start | bytes 786436
  97.2 4.2 %copy-start.9 = (bf16[1,2,128,512]{3,2,1,0:T(8,128)(2,1)S(1)}, bf16[1,2,128,512]{3,2,1,0:T(8,128)(2,1)}, u32[]{:S(2)}) copy-start(bf16[1,2,128,512]{3,2,1,0:T(8,128)(2,1)} %copy-done.8) | copy-start | bytes 786436
  123.5 1.4 %copy-start.20 = (f32[16,256]{1,0:T(8,128)S(1)}, f32[16,256]{1,0:T(8,128)}, u32[]{:S(2)}) copy-start(f32[16,256]{1,0:T(8,128)} %constant.63.clone) | copy-start | bytes 49156
  123.8 1.2 copy-start.22

commit v4 on v1

--- a/solution.py
+++ b/solution.py
@@ -137,8 +137,9 @@
         )
     tendency = jnp.stack(pieces)
 
-    star = center[:3] + DT * tendency[:3].astype(jnp.float32)
-    flow_u, flow_v, flow_w = star[0], star[1], star[2]
+    flow_u = center[0] + DT * pieces[0].astype(jnp.float32)
+    flow_v = center[1] + DT * pieces[1].astype(jnp.float32)
+    flow_w = center[2] + DT * pieces[2].astype(jnp.float32)
     u_before = lax.ppermute(flow_u[:, rows_x - 1 :, :], "gx", up_x)
     u_after = lax.ppermute(flow_u[:, :1, :], "gx", down_x)
     v_before = lax.ppermute(flow_v[:, :, rows_y - 1 :], "gy", up_y)

time: 108 us -> 106 us (0.981)
  waiting for transfers between devices: 29.9 us -> 37.9 us
  starting transfers between devices: 33.4 us -> 25.9 us
  blocking collectives: 15.2 us -> 11.5 us
  other arithmetic: 13.5 us -> 15.3 us
    add x1 -> x3, other arithmetic: 0.31 us -> 4.99 us  [the longest x1 1.7 us: body(): flow_w = center[2] + DT * pieces[2].astype(jnp.float32)]
    all_to_all x1, blocking collectives: 15.2 us -> 11.5 us  [body(): lax.all_to_all(sent, 'gy', split_axis=0, concat_axis=0, tiled=True)]
    ppermute x1, starting transfers between devices: 4.3 us -> 0.72 us  [body(): u_before = lax.ppermute(flow_u[:, rows_x - 1:, :], 'gx', up_x)]
    ppermute x1, waiting for transfers between devices: 2.31 us -> 5.48 us  [body(): v_before = lax.ppermute(flow_v[:, :, rows_y - 1:], 'gy', up_y)]
    another operation x5 -> x2, other arithmetic: 8.12 us -> 5.27 us  [body(): tendency = jnp.stack(pieces)]
    ppermute x1, starting transfers between devices: 5.36 us -> 2.83 us  [body(): v_after = lax.ppermute(flow_v[:, :, :1], 'gy', down_y)]
    ppermute x1, waiting for transfers between devices: 3.13 us -> 5.53 us  [body(): y_before = lax.ppermute(masked[:, :, :, rows_y - 3:], 'gy', up_y)]
    ppermute x1, waiting for transfers between devices: 0.01 us -> 2.15 us  [body(): y_after = lax.ppermute(masked[:, :, :, :3], 'gy', down_y)]
  transfers between devices with their start and end apart: 9 -> 9, of which waited for: 3 -> 5; matrix products, arithmetic and copies ran while one was open for 8% -> 9% of each run, Pallas kernels for 0% -> 0%
where the time goes in v4:
time: 106 us
  waiting for transfers between devices  37.9 us (36%)
  starting transfers between devices  25.9 us (24%)
  other arithmetic  15.3 us (14%)
  blocking collectives  11.5 us (11%)
  local copies, waits for them, and re-layouts  8.93 us (8%)
  matrix products  5.25 us (5%)
    all_to_all x1, waiting for transfers between devices, body(): lax.all_to_all(spectrum_y, ('gx', 'gy'), split_axis=0, concat_axis=0, til...  24.5 us
    all_to_all x1, starting transfers between devices, body(): lax.all_to_all(spectrum_y, ('gx', 'gy'), split_axis=0, concat_axis=0, til...  12.7 us
    all_to_all x1, blocking collectives, body(): lax.all_to_all(sent, 'gy', split_axis=0, concat_axis=0, tiled=True)  11.5 us
    ppermute x1, starting transfers between devices, body(): y_after = lax.ppermute(masked[:, :, :, :3], 'gy', down_y)  6 us
    ppermute x1, waiting for transfers between devices, body(): y_before = lax.ppermute(masked[:, :, :, rows_y - 3:], 'gy', up_y)  5.53 us
    ppermute x1, waiting for transfers between devices, body(): v_before = lax.ppermute(flow_v[:, :, rows_y - 1:], 'gy', up_y)  5.48 us
    another operation x2, other arithmetic, body(): tendency = jnp.stack(pieces)  5.27 us
    ppermute x1, starting transfers between devices, body(): v_after = lax.ppermute(flow_v[:, :, :1], 'gy', down_y)  2.83 us
  transfers between devices with their start and end apart: 9, of which 5 were waited for; matrix products, arithmetic and copies ran while one was open for 9% of the time, Pallas kernels for 0%

profile of v4, /device:TPU:1, one launch (start us, length us, event | category | flops | bytes accessed | tf_op | source)
XLA Modules:
  0.0 105.8 jit_solution(2572841728363940442)
XLA Ops:
  0.6 1.0 convert_convert_fusion
  1.6 1.4 %fusion.120 = (f32[4,2,128,512]{3,2,1,0:T(8,128)S(1)}, bf16[4,2,128,512]{3,2,1,0:T(8,128)(2,1)S(1)}) fusion(bf16[4,2,128,512]{3,2,1,0:T(8,128)(2,1)} %param.11, bf16[2,128,512]{2,1,0:T(8,128)(2,1)S(1)} %convert_convert_fusion), kind=kLoop, calls=%fused_computation.182 | loop fusion | flops 1048576 | bytes 4456448 | tf_op jit(solution)/shard_map/convert_element_type | solution.py:123
  3.1 0.0 copy-start.1
  3.1 0.1 fusion.122
  3.2 6.0 %collective-permute-start.3 = (bf16[4,2,128,3]{3,2,1,0:T(8,128)(2,1)S(1)}, bf16[4,2,128,3]{3,2,1,0:T(8,128)(2,1)S(1)}, u32[]{:S(2)}, u32[]{:S(2)}) collective-permute-start(bf16[4,2,128,3]{3,2,1,0:T(8,128)(2,1)S(1)} %get-tuple-element.25), channel_id=1, source_target_pairs={{1,0},{2,1},{3,2},{4,3},{5,4},{6,5},{7,6},{0,7},{9,8},{10,9},{11,1... | collective-permute-start | bytes 18440 | tf_op jit(solution)/shard_map/ppermute | solution.py:120
  9.2 0.0 collective-permute-start.2
  9.3 1.0 collective-permute-start.1
  10.3 0.8 collective-permute-start
  11.1 1.0 slice_bitcast_fusion.18
  12.1 2.1 %collective-permute-done.3 = bf16[4,2,128,3]{3,2,1,0:T(8,128)(2,1)S(1)} collective-permute-done((bf16[4,2,128,3]{3,2,1,0:T(8,128)(2,1)S(1)}, bf16[4,2,128,3]{3,2,1,0:T(8,128)(2,1)S(1)}, u32[]{:S(2)}, u32[]{:S(2)}) %collective-permute-start.3) | collective-permute-done | bytes 6176 | tf_op jit(solution)/shard_map/ppermute | solution.py:120
  14.2 5.5 %collective-permute-done.2 = bf16[4,2,128,3]{3,2,1,0:T(8,128)(2,1)S(1)} collective-permute-done((bf16[4,2,128,3]{3,2,1,0:T(8,128)(2,1)S(1)}, bf16[4,2,128,3]{3,2,1,0:T(8,128)(2,1)S(1)}, u32[]{:S(2)}, u32[]{:S(2)}) %collective-permute-start.2) | collective-permute-done | bytes 6176 | tf_op jit(solution)/shard_map/ppermute | solution.py:119
  19.8 0.7 maximum_convert_fusion
  20.4 0.0 copy-start
  20.4 0.0 copy-start.2
  20.4 0.0 collective-permute-done.1
  20.4 0.0 collective-permute-done
  20.5 0.3 maximum_convert_fusion.1
  20.8 0.8 copy-done.2
  21.6 1.6 %multiply_add_fusion.4 = (f32[2,128,512]{2,1,0:T(8,128)S(1)}, bf16[2,128,512]{2,1,0:T(8,128)(2,1)}) fusion(f32[4,2,128,512]{3,2,1,0:T(8,128)S(1)} %get-tuple-element.8, f32[4,2,128,518]{3,2,1,0:T(8,128)S(1)} %maximum_convert_fusion, f32[4,2,134,512]{3,2,1,0:T(8,128)S(1)} %maximum_convert_fusion.1, f32[1,128,512]{2,1,0:T(8,128)S(1)} %get-tuple-element.17, ...), kind=kLoop, calls=%fused_computation.165 | loop fusion | flops 5242880 | bytes 9437184 | tf_op jit(solution)/shard_map/add | solution.py:140
  23.2 0.1 fusion.127
  23.3 1.6 %multiply_add_fusion.3 = (f32[2,128,512]{2,1,0:T(8,128)S(1)}, bf16[2,128,512]{2,1,0:T(8,128)(2,1)}) fusion(f32[4,2,128,512]{3,2,1,0:T(8,128)S(1)} %get-tuple-element.8, f32[4,2,128,518]{3,2,1,0:T(8,128)S(1)} %maximum_convert_fusion, f32[4,2,134,512]{3,2,1,0:T(8,128)S(1)} %maximum_convert_fusion.1, f32[1,128,512]{2,1,0:T(8,128)S(1)} %get-tuple-element.15, ...), kind=kLoop, calls=%fused_computation.164 | loop fusion | flops 5242880 | bytes 9437184 | tf_op jit(solution)/shard_map/add | solution.py:141
  25.0 0.1 fusion.124
  25.1 0.2 fusion.125
  25.3 1.9 %collective-permute-start.4 = (f32[2,1,512]{2,1,0:T(1,128)S(1)}, f32[2,1,512]{2,1,0:T(1,128)S(1)}, u32[]{:S(2)}, u32[]{:S(2)}) collective-permute-start(f32[2,1,512]{2,1,0:T(1,128)S(1)} %get-tuple-element.33), channel_id=1, source_target_pairs={{8,0},{16,8},{24,16},{32,24},{40,32},{48,40},{56,48},{64,56},{72,6... | collective-permute-start | bytes 12296 | tf_op jit(solution)/shard_map/ppermute | solution.py:144
  27.2 0.7 collective-permute-start.5
  27.9 2.8 %collective-permute-start.6 = (f32[2,128,1]{2,1,0:T(8,128)S(1)}, f32[2,128,1]{2,1,0:T(8,128)S(1)}, u32[]{:S(2)}, u32[]{:S(2)}) collective-permute-start(f32[2,128,1]{2,1,0:T(8,128)S(1)} %get-tuple-element.29), channel_id=1, source_target_pairs={{1,0},{2,1},{3,2},{4,3},{5,4},{6,5},{7,6},{0,7},{9,8},{10,9},{11,1... | collective-permute-start | bytes 3080 | tf_op jit(solution)/shard_map/ppermute | solution.py:146
  30.7 0.0 collective-permute-start.7
  30.7 0.0 copy-done.1
  30.7 0.0 copy-done
  30.7 1.7 %multiply_add_fusion.2 = (f32[2,128,512]{2,1,0:T(8,128)S(1)}, bf16[2,128,512]{2,1,0:T(8,128)(2,1)}) fusion(f32[4,2,128,512]{3,2,1,0:T(8,128)S(1)} %get-tuple-element.8, f32[4,2,128,518]{3,2,1,0:T(8,128)S(1)} %maximum_convert_fusion, f32[4,2,134,512]{3,2,1,0:T(8,128)S(1)} %maximum_convert_fusion.1, f32[1,128,512]{2,1,0:T(8,128)S(1)} %get-tuple-element.13, ...), kind=kLoop, calls=%fused_computation.163 | loop fusion | flops 5505024 | bytes 9961472 | tf_op jit(solution)/shard_map/add | solution.py:142
  32.5 0.2 collective-permute-done.6
  32.7 5.5 %collective-permute-done.7 = f32[2,128,1]{2,1,0:T(8,128)S(1)} collective-permute-done((f32[2,128,1]{2,1,0:T(8,128)S(1)}, f32[2,128,1]{2,1,0:T(8,128)S(1)}, u32[]{:S(2)}, u32[]{:S(2)}) %collective-permute-start.7) | collective-permute-done | bytes 1056 | tf_op jit(solution)/shard_map/ppermute | solution.py:145
  38.1 0.0 collective-permute-done.4
  38.2 0.0 collective-permute-done.5
  38.2 0.3 fusion.103
  38.5 0.0 copy-start.7
  38.5 0.3 reshape.114
  38.9 0.0 copy-start.8
  38.9 0.1 copy.27
  38.9 11.5 %all_to_all.10 = f32[8,64,256]{2,1,0:T(8,128)S(1)} all-to-all(f32[8,64,256]{2,1,0:T(8,128)S(1)} %bitcast.303), channel_id=1, replica_groups=mesh['gx'=32,'gy'=8] {'gy'}, dimensions={0} | all-to-all | bytes 1048576 | tf_op jit(solution)/shard_map/all_to_all | solution.py:160
  50.5 1.4 %fusion.111 = f32[32,2,16,256]{3,0,2,1:T(8,128)S(1)} fusion(f32[32,16,1,1]{0,1,3,2:T(8,128)} %constant.67, f32[16,2,16,256]{3,2,1,0:T(8,128)S(1)} %bitcast.301), kind=kOutput, calls=%fused_computation.157 | convolution fusion | flops 25165824 | bytes 1574912 | tf_op jit(solution)/shard_map/dot_general | solution.py:163
  51.9 0.0 copy-done.7
  51.9 0.0 copy-done.8
  52.0 0.0 copy-start.3
  52.0 0.2 multiply_add_fusion.1
  52.1 0.3 copy.30
  52.4 0.3 copy.29
  52.8 0.4 copy-done.3
  53.2 1.0 fusion
  54.2 1.8 %copy.31 = f32[256,2,512]{2,1,0:T(2,128)} copy(f32[256,2,512]{2,0,1:T(8,128)S(1)} %fusion) | data formatting | bytes 2097152 | tf_op jit(solution)/shard_map/dot_general | solution.py:177
  56.0 12.7 %all-to-all-start.1 = ((f32[256,2,512]{2,1,0:T(2,128)}), f32[256,2,512]{2,1,0:T(2,128)S(1)}, u32[]{:S(2)}, u32[]{:S(2)}) async-start(f32[256,2,512]{2,1,0:T(2,128)} %copy.31), calls=%async_computation.1 | async-start | bytes 2097152 | tf_op jit(solution)/shard_map/all_to_all | solution.py:180
  68.7 1.0 convert_element_type.57
  69.7 4.2 %fusion.114 = bf16[1,2,128,512]{3,2,1,0:T(8,128)(2,1)S(1)} fusion(f32[128,512]{1,0:T(8,128)S(1)} %convert_element_type.57, f32[4,2,128,512]{3,2,1,0:T(8,128)} %copy-done.1, f32[4,2,128,518]{3,2,1,0:T(8,128)} %copy-done, f32[4,2,134,512]{3,2,1,0:T(8,128)S(1)} %maximum_convert_fusion.1, f32[1,128,512]{2,1,0:T(8,128)} %get-tuple-element.11, ...), kind=kLoop, calls=%fused_computation.179 | loop fusion | flops 5242880 | bytes 9699328 | tf_op jit(solution)/shard_map/stack | solution.py:138
  73.9 1.1 %pad_maximum_fusion = bf16[4,2,128,512]{3,2,1,0:T(8,128)(2,1)} fusion(bf16[1,2,128,512]{3,2,1,0:T(8,128)(2,1)S(1)} %fusion.114, bf16[1,2,128,512]{3,2,1,0:T(8,128)(2,1)S(1)} %bitcast.308, bf16[1,2,128,512]{3,2,1,0:T(8,128)(2,1)S(1)} %bitcast.307, bf16[1,2,128,512]{3,2,1,0:T(8,128)(2,1)S(1)} %bitcast.306), kind=kLoop, calls=%fused_computation.2 | loop fusion | flops 1572864 | bytes 2097152 | tf_op jit(solution)/shard_map/stack | solution.py:138
  75.0 24.5 %all-to-all-done.1 = f32[256,2,512]{2,1,0:T(2,128)S(1)} async-done(((f32[256,2,512]{2,1,0:T(2,128)}), f32[256,2,512]{2,1,0:T(2,128)S(1)}, u32[]{:S(2)}, u32[]{:S(2)}) %all-to-all-start.1) | async-done | bytes 1048608 | tf_op jit(solution)/shard_map/all_to_all | solution.py:180
  99.5 0.7 reshape.119
  100.2 0.0 copy-start.9
  100.2 0.3 copy.32
  100.6 0.0 copy-start.10
  100.6 2.2 %fusion.128 = f32[32,16,512]{2,1,0:T(8,128)S(1)} fusion(f32[32,16,512]{2,1,0:T(8,128)S(1)} %bitcast.298, f32[512,512,1]{1,0,2:T(8,128)} %constant.68), kind=kOutput, calls=%fused_computation.190 | convolution fusion | flops 805306368 | bytes 3145728 | tf_op jit(solution)/shard_map/dot_general | solution.py:187
  102.8 0.2 multiply_add_fusion
  103.0 0.6 fusion.3
  103.6 0.7 reshape.133
  104.3 1.6 %copy.35 = f32[2,2,16,4096]{3,2,1,0:T(8,128)} copy(f32[2,2,16,4096]{3,0,1,2:T(2,128)S(1)} %reshape.133) | data formatting | bytes 2097152 | tf_op jit(solution)/shard_map/reshape | solution.py:204
  (11 shorter events, 0.1 us)
Async XLA Ops:
  3.1 27.7 %copy-start.1 = (f32[4,2,128,512]{3,2,1,0:T(8,128)}, f32[4,2,128,512]{3,2,1,0:T(8,128)S(1)}, u32[]{:S(2)}) copy-start(f32[4,2,128,512]{3,2,1,0:T(8,128)S(1)} %get-tuple-element.8) | copy-start | bytes 6291460
  3.2 11.0 %collective-permute-start.3 = (bf16[4,2,128,3]{3,2,1,0:T(8,128)(2,1)S(1)}, bf16[4,2,128,3]{3,2,1,0:T(8,128)(2,1)S(1)}, u32[]{:S(2)}, u32[]{:S(2)}) collective-permute-start(bf16[4,2,128,3]{3,2,1,0:T(8,128)(2,1)S(1)} %get-tuple-element.25), channel_id=1, source_target_pairs={{1,0},{2,1},{3,2},{4,3},{5,4},{6,5},{7,6},{0,7},{9,8},{10,9},{11,1... | collective-permute-start | bytes 18440 | tf_op jit(solution)/shard_map/ppermute | solution.py:120
  9.2 10.5 %collective-permute-start.2 = (bf16[4,2,128,3]{3,2,1,0:T(8,128)(2,1)S(1)}, bf16[4,2,128,3]{3,2,1,0:T(8,128)(2,1)S(1)}, u32[]{:S(2)}, u32[]{:S(2)}) collective-permute-start(bf16[4,2,128,3]{3,2,1,0:T(8,128)(2,1)S(1)} %get-tuple-element.24), channel_id=1, source_target_pairs={{0,1},{1,2},{2,3},{3,4},{4,5},{5,6},{6,7},{7,0},{8,9},{9,10},{10,1... | collective-permute-start | bytes 18440 | tf_op jit(solution)/shard_map/ppermute | solution.py:119
  9.3 11.2 %collective-permute-start.1 = (bf16[4,2,3,512]{3,2,1,0:T(4,128)(2,1)S(1)}, bf16[4,2,3,512]{3,2,1,0:T(4,128)(2,1)S(1)}, u32[]{:S(2)}, u32[]{:S(2)}) collective-permute-start(bf16[4,2,3,512]{3,2,1,0:T(4,128)(2,1)S(1)} %get-tuple-element.23), channel_id=1, source_target_pairs={{8,0},{16,8},{24,16},{32,24},{40,32},{48,40},{56,48},{64,56},{72,6... | collective-permute-start | bytes 73736 | tf_op jit(solution)/shard_map/ppermute | solution.py:118
  10.3 10.2 %collective-permute-start = (bf16[4,2,3,512]{3,2,1,0:T(4,128)(2,1)S(1)}, bf16[4,2,3,512]{3,2,1,0:T(4,128)(2,1)S(1)}, u32[]{:S(2)}, u32[]{:S(2)}) collective-permute-start(bf16[4,2,3,512]{3,2,1,0:T(4,128)(2,1)S(1)} %get-tuple-element.22), channel_id=1, source_target_pairs={{0,8},{8,16},{16,24},{24,32},{32,40},{40,48},{48,56},{56,64},{64,7... | collective-permute-start | bytes 73736 | tf_op jit(solution)/shard_map/ppermute | solution.py:117
  20.4 10.3 %copy-start = (f32[4,2,128,518]{3,2,1,0:T(8,128)}, f32[4,2,128,518]{3,2,1,0:T(8,128)S(1)}, u32[]{:S(2)}) copy-start(f32[4,2,128,518]{3,2,1,0:T(8,128)S(1)} %maximum_convert_fusion) | copy-start | bytes 6365188
  20.4 1.1 %copy-start.2 = (s32[128,512]{1,0:T(8,128)S(1)}, s32[128,512]{1,0:T(8,128)}, u32[]{:S(2)}) copy-start(s32[128,512]{1,0:T(8,128)} %param.12) | copy-start | bytes 786436
  25.3 12.9 %collective-permute-start.4 = (f32[2,1,512]{2,1,0:T(1,128)S(1)}, f32[2,1,512]{2,1,0:T(1,128)S(1)}, u32[]{:S(2)}, u32[]{:S(2)}) collective-permute-start(f32[2,1,512]{2,1,0:T(1,128)S(1)} %get-tuple-element.33), channel_id=1, source_target_pairs={{8,0},{16,8},{24,16},{32,24},{40,32},{48,40},{56,48},{64,56},{72,6... | collective-permute-start | bytes 12296 | tf_op jit(solution)/shard_map/ppermute | solution.py:144
  27.2 11.0 %collective-permute-start.5 = (f32[2,1,512]{2,1,0:T(1,128)S(1)}, f32[2,1,512]{2,1,0:T(1,128)S(1)}, u32[]{:S(2)}, u32[]{:S(2)}) collective-permute-start(f32[2,1,512]{2,1,0:T(1,128)S(1)} %get-tuple-element.32), channel_id=1, source_target_pairs={{0,8},{8,16},{16,24},{24,32},{32,40},{40,48},{48,56},{56,64},{64,7... | collective-permute-start | bytes 12296 | tf_op jit(solution)/shard_map/ppermute | solution.py:143
  27.9 4.8 %collective-permute-start.6 = (f32[2,128,1]{2,1,0:T(8,128)S(1)}, f32[2,128,1]{2,1,0:T(8,128)S(1)}, u32[]{:S(2)}, u32[]{:S(2)}) collective-permute-start(f32[2,128,1]{2,1,0:T(8,128)S(1)} %get-tuple-element.29), channel_id=1, source_target_pairs={{1,0},{2,1},{3,2},{4,3},{5,4},{6,5},{7,6},{0,7},{9,8},{10,9},{11,1... | collective-permute-start | bytes 3080 | tf_op jit(solution)/shard_map/ppermute | solution.py:146
  30.7 7.4 %collective-permute-start.7 = (f32[2,128,1]{2,1,0:T(8,128)S(1)}, f32[2,128,1]{2,1,0:T(8,128)S(1)}, u32[]{:S(2)}, u32[]{:S(2)}) collective-permute-start(f32[2,128,1]{2,1,0:T(8,128)S(1)} %get-tuple-element.28), channel_id=1, source_target_pairs={{0,1},{1,2},{2,3},{3,4},{4,5},{5,6},{6,7},{7,0},{8,9},{9,10},{10,1... | collective-permute-start | bytes 3080 | tf_op jit(solution)/shard_map/ppermute | solution.py:145
  38.5 13.4 %copy-start.7 = (f32[16,256]{1,0:T(8,128)S(1)}, f32[16,256]{1,0:T(8,128)}, u32[]{:S(2)}) copy-start(f32[16,256]{1,0:T(8,128)} %constant.43.clone) | copy-start | bytes 49156
  38.9 13.1 %copy-start.8 = (f32[16,256]{1,0:T(8,128)S(1)}, f32[16,256]{1,0:T(8,128)}, u32[]{:S(2)}) copy-start(f32[16,256]{1,0:T(8,128)} %constant.42.clone) | copy-start | bytes 49156
  52.0 1.2 %copy-start.3 = (f32[256,2,512]{2,0,1:T(8,128)S(1)}, f32[256,2,512]{2,0,1:T(8,128)}, u32[]{:S(2)}) copy-start(f32[256,2,512]{2,0,1:T(8,128)} %constant.44.clone) | copy-start | bytes 3145732
  56.0 43.5 %all-to-all-start.1 = ((f32[256,2,512]{2,1,0:T(2,128)}), f32[256,2,512]{2,1,0:T(2,128)S(1)}, u32[]{:S(2)}, u32[]{:S(2)}) async-start(f32[256,2,512]{2,1,0:T(2,128)} %copy.31), calls=%async_computation.1 | async-start | bytes 2097152 | tf_op jit(solution)/shard_map/all_to_all | solution.py:180
  69.7 4.2 %copy-start.4 = (bf16[2,128,512]{2,1,0:T(8,128)(2,1)S(1)}, bf16[2,128,512]{2,1,0:T(8,128)(2,1)}, u32[]{:S(2)}) copy-start(bf16[2,128,512]{2,1,0:T(8,128)(2,1)} %get-tuple-element.7) | copy-start | bytes 786436
  69.7 4.2 %copy-start.5 = (bf16[2,128,512]{2,1,0:T(8,128)(2,1)S(1)}, bf16[2,128,512]{2,1,0:T(8,128)(2,1)}, u32[]{:S(2)}) copy-start(bf16[2,128,512]{2,1,0:T(8,128)(2,1)} %get-tuple-element.5) | copy-start | bytes 786436
  69.7 4.2 %copy-start.6 = (bf16[2,128,512]{2,1,0:T(8,128)(2,1)S(1)}, bf16[2,128,512]{2,1,0:T(8,128)(2,1)}, u32[]{:S(2)}) copy-start(bf16[2,128,512]{2,1,0:T(8,128)(2,1)} %get-tuple-element.3) | copy-start | bytes 786436
  100.2 2.6 %copy-start.9 = (f32[16,256]{1,0:T(8,128)S(1)}, f32[16,256]{1,0:T(8,128)}, u32[]{:S(2)}) copy-start(f32[16,256]{1,0:T(8,128)} %constant.42.clone) | copy-start | bytes 49156
  100.6 2.4 %copy-start.10 = (f32[32,32]{1,0:T(8,128)S(1)}, f32[32,32]{1,0:T(8,128)}, u32[]{:S(2)}) copy-start(f32[32,32]{1,0:T(8,128)} %constant.46.clone) | copy-start | bytes 12292

commit v5 on v1

--- a/solution.py
+++ b/solution.py
@@ -123,6 +123,7 @@
     center = masked.astype(jnp.float32)
 
     pieces = []
+    rounded = []
     for component in range(4):
 
         def pick(step_x, step_y, component=component):
@@ -130,15 +131,14 @@
                 return pad_x[component, :, 3 + step_x : 3 + step_x + rows_x, :]
             return pad_y[component, :, :, 3 + step_y : 3 + step_y + rows_y]
 
-        pieces.append(
-            tendency_one(component, center[component], pick, center, fluid, surface).astype(
-                jnp.bfloat16
-            )
-        )
+        exact = tendency_one(component, center[component], pick, center, fluid, surface)
+        pieces.append(exact.astype(jnp.bfloat16))
+        rounded.append(lax.reduce_precision(exact, exponent_bits=8, mantissa_bits=7))
     tendency = jnp.stack(pieces)
 
-    star = center[:3] + DT * tendency[:3].astype(jnp.float32)
-    flow_u, flow_v, flow_w = star[0], star[1], star[2]
+    flow_u = center[0] + DT * rounded[0]
+    flow_v = center[1] + DT * rounded[1]
+    flow_w = center[2] + DT * rounded[2]
     u_before = lax.ppermute(flow_u[:, rows_x - 1 :, :], "gx", up_x)
     u_after = lax.ppermute(flow_u[:, :1, :], "gx", down_x)
     v_before = lax.ppermute(flow_v[:, :, rows_y - 1 :], "gy", up_y)

time: 108 us -> 106 us (0.981)
  waiting for transfers between devices: 29.9 us -> 37.8 us
  starting transfers between devices: 33.4 us -> 25.9 us
  blocking collectives: 15.2 us -> 11.5 us
  other arithmetic: 13.5 us -> 15.4 us
    add x1 -> x3, other arithmetic: 0.31 us -> 5.08 us  [the longest x1 1.75 us: body(): flow_w = center[2] + DT * rounded[2]]
    all_to_all x1, blocking collectives: 15.2 us -> 11.5 us  [body(): lax.all_to_all(sent, 'gy', split_axis=0, concat_axis=0, tiled=True)]
    ppermute x1, starting transfers between devices: 4.3 us -> 0.72 us  [body(): u_before = lax.ppermute(flow_u[:, rows_x - 1:, :], 'gx', up_x)]
    ppermute x1, waiting for transfers between devices: 2.31 us -> 5.48 us  [body(): v_before = lax.ppermute(flow_v[:, :, rows_y - 1:], 'gy', up_y)]
    another operation x5 -> x2, other arithmetic: 8.12 us -> 5.27 us  [body(): tendency = jnp.stack(pieces)]
    ppermute x1, starting transfers between devices: 5.36 us -> 2.83 us  [body(): v_after = lax.ppermute(flow_v[:, :, :1], 'gy', down_y)]
    ppermute x1, waiting for transfers between devices: 3.13 us -> 5.53 us  [body(): y_before = lax.ppermute(masked[:, :, :, rows_y - 3:], 'gy', up_y)]
    ppermute x1, waiting for transfers between devices: 0.01 us -> 2.15 us  [body(): y_after = lax.ppermute(masked[:, :, :, :3], 'gy', down_y)]
  transfers between devices with their start and end apart: 9 -> 9, of which waited for: 3 -> 5; matrix products, arithmetic and copies ran while one was open for 8% -> 9% of each run, Pallas kernels for 0% -> 0%
where the time goes in v5:
time: 106 us
  waiting for transfers between devices  37.8 us (36%)
  starting transfers between devices  25.9 us (24%)
  other arithmetic  15.4 us (15%)
  blocking collectives  11.5 us (11%)
  local copies, waits for them, and re-layouts  8.93 us (8%)
  matrix products  5.25 us (5%)
    all_to_all x1, waiting for transfers between devices, body(): lax.all_to_all(spectrum_y, ('gx', 'gy'), split_axis=0, concat_axis=0, til...  24.5 us
    all_to_all x1, starting transfers between devices, body(): lax.all_to_all(spectrum_y, ('gx', 'gy'), split_axis=0, concat_axis=0, til...  12.7 us
    all_to_all x1, blocking collectives, body(): lax.all_to_all(sent, 'gy', split_axis=0, concat_axis=0, tiled=True)  11.5 us
    ppermute x1, starting transfers between devices, body(): y_after = lax.ppermute(masked[:, :, :, :3], 'gy', down_y)  6 us
    ppermute x1, waiting for transfers between devices, body(): y_before = lax.ppermute(masked[:, :, :, rows_y - 3:], 'gy', up_y)  5.53 us
    ppermute x1, waiting for transfers between devices, body(): v_before = lax.ppermute(flow_v[:, :, rows_y - 1:], 'gy', up_y)  5.48 us
    another operation x2, other arithmetic, body(): tendency = jnp.stack(pieces)  5.27 us
    ppermute x1, starting transfers between devices, body(): v_after = lax.ppermute(flow_v[:, :, :1], 'gy', down_y)  2.83 us
  transfers between devices with their start and end apart: 9, of which 5 were waited for; matrix products, arithmetic and copies ran while one was open for 9% of the time, Pallas kernels for 0%

profile of v5, /device:TPU:1, one launch (start us, length us, event | category | flops | bytes accessed | tf_op | source)
XLA Modules:
  0.0 105.9 jit_solution(2381767747044290033)
XLA Ops:
  0.6 1.0 convert_convert_fusion
  1.6 1.4 %fusion.117 = (f32[4,2,128,512]{3,2,1,0:T(8,128)S(1)}, bf16[4,2,128,512]{3,2,1,0:T(8,128)(2,1)S(1)}) fusion(bf16[4,2,128,512]{3,2,1,0:T(8,128)(2,1)} %param.11, bf16[2,128,512]{2,1,0:T(8,128)(2,1)S(1)} %convert_convert_fusion), kind=kLoop, calls=%fused_computation.182 | loop fusion | flops 1048576 | bytes 4456448 | tf_op jit(solution)/shard_map/convert_element_type | solution.py:123
  3.1 0.0 copy-start.1
  3.1 0.1 fusion.119
  3.2 6.0 %collective-permute-start.3 = (bf16[4,2,128,3]{3,2,1,0:T(8,128)(2,1)S(1)}, bf16[4,2,128,3]{3,2,1,0:T(8,128)(2,1)S(1)}, u32[]{:S(2)}, u32[]{:S(2)}) collective-permute-start(bf16[4,2,128,3]{3,2,1,0:T(8,128)(2,1)S(1)} %get-tuple-element.25), channel_id=1, source_target_pairs={{1,0},{2,1},{3,2},{4,3},{5,4},{6,5},{7,6},{0,7},{9,8},{10,9},{11,1... | collective-permute-start | bytes 18440 | tf_op jit(solution)/shard_map/ppermute | solution.py:120
  9.2 0.0 collective-permute-start.2
  9.3 1.0 collective-permute-start.1
  10.3 0.8 collective-permute-start
  11.1 1.0 slice_bitcast_fusion.18
  12.1 2.1 %collective-permute-done.3 = bf16[4,2,128,3]{3,2,1,0:T(8,128)(2,1)S(1)} collective-permute-done((bf16[4,2,128,3]{3,2,1,0:T(8,128)(2,1)S(1)}, bf16[4,2,128,3]{3,2,1,0:T(8,128)(2,1)S(1)}, u32[]{:S(2)}, u32[]{:S(2)}) %collective-permute-start.3) | collective-permute-done | bytes 6176 | tf_op jit(solution)/shard_map/ppermute | solution.py:120
  14.2 5.5 %collective-permute-done.2 = bf16[4,2,128,3]{3,2,1,0:T(8,128)(2,1)S(1)} collective-permute-done((bf16[4,2,128,3]{3,2,1,0:T(8,128)(2,1)S(1)}, bf16[4,2,128,3]{3,2,1,0:T(8,128)(2,1)S(1)}, u32[]{:S(2)}, u32[]{:S(2)}) %collective-permute-start.2) | collective-permute-done | bytes 6176 | tf_op jit(solution)/shard_map/ppermute | solution.py:119
  19.8 0.7 maximum_convert_fusion
  20.4 0.0 copy-start
  20.4 0.0 copy-start.2
  20.4 0.0 collective-permute-done.1
  20.4 0.0 collective-permute-done
  20.5 0.3 maximum_convert_fusion.1
  20.8 0.8 copy-done.2
  21.6 1.7 %multiply_add_fusion.4 = (f32[2,128,512]{2,1,0:T(8,128)S(1)}, bf16[2,128,512]{2,1,0:T(8,128)(2,1)}) fusion(f32[4,2,128,512]{3,2,1,0:T(8,128)S(1)} %get-tuple-element.8, f32[4,2,128,518]{3,2,1,0:T(8,128)S(1)} %maximum_convert_fusion, f32[4,2,134,512]{3,2,1,0:T(8,128)S(1)} %maximum_convert_fusion.1, f32[1,128,512]{2,1,0:T(8,128)S(1)} %get-tuple-element.17, ...), kind=kLoop, calls=%fused_computation.162 | loop fusion | flops 5242880 | bytes 9437184 | tf_op jit(solution)/shard_map/add | solution.py:139
  23.3 0.1 fusion.124
  23.4 1.7 %multiply_add_fusion.3 = (f32[2,128,512]{2,1,0:T(8,128)S(1)}, bf16[2,128,512]{2,1,0:T(8,128)(2,1)}) fusion(f32[4,2,128,512]{3,2,1,0:T(8,128)S(1)} %get-tuple-element.8, f32[4,2,128,518]{3,2,1,0:T(8,128)S(1)} %maximum_convert_fusion, f32[4,2,134,512]{3,2,1,0:T(8,128)S(1)} %maximum_convert_fusion.1, f32[1,128,512]{2,1,0:T(8,128)S(1)} %get-tuple-element.15, ...), kind=kLoop, calls=%fused_computation.161 | loop fusion | flops 5242880 | bytes 9437184 | tf_op jit(solution)/shard_map/add | solution.py:140
  25.0 0.1 fusion.121
  25.1 0.2 fusion.122
  25.3 1.9 %collective-permute-start.4 = (f32[2,1,512]{2,1,0:T(1,128)S(1)}, f32[2,1,512]{2,1,0:T(1,128)S(1)}, u32[]{:S(2)}, u32[]{:S(2)}) collective-permute-start(f32[2,1,512]{2,1,0:T(1,128)S(1)} %get-tuple-element.33), channel_id=1, source_target_pairs={{8,0},{16,8},{24,16},{32,24},{40,32},{48,40},{56,48},{64,56},{72,6... | collective-permute-start | bytes 12296 | tf_op jit(solution)/shard_map/ppermute | solution.py:143
  27.2 0.7 collective-permute-start.5
  27.9 2.8 %collective-permute-start.6 = (f32[2,128,1]{2,1,0:T(8,128)S(1)}, f32[2,128,1]{2,1,0:T(8,128)S(1)}, u32[]{:S(2)}, u32[]{:S(2)}) collective-permute-start(f32[2,128,1]{2,1,0:T(8,128)S(1)} %get-tuple-element.29), channel_id=1, source_target_pairs={{1,0},{2,1},{3,2},{4,3},{5,4},{6,5},{7,6},{0,7},{9,8},{10,9},{11,1... | collective-permute-start | bytes 3080 | tf_op jit(solution)/shard_map/ppermute | solution.py:145
  30.8 0.0 collective-permute-start.7
  30.8 0.0 copy-done.1
  30.8 0.0 copy-done
  30.8 1.7 %multiply_add_fusion.2 = (f32[2,128,512]{2,1,0:T(8,128)S(1)}, bf16[2,128,512]{2,1,0:T(8,128)(2,1)}) fusion(f32[4,2,128,512]{3,2,1,0:T(8,128)S(1)} %get-tuple-element.8, f32[4,2,128,518]{3,2,1,0:T(8,128)S(1)} %maximum_convert_fusion, f32[4,2,134,512]{3,2,1,0:T(8,128)S(1)} %maximum_convert_fusion.1, f32[1,128,512]{2,1,0:T(8,128)S(1)} %get-tuple-element.13, ...), kind=kLoop, calls=%fused_computation.160 | loop fusion | flops 5505024 | bytes 9961472 | tf_op jit(solution)/shard_map/add | solution.py:141
  32.6 0.2 collective-permute-done.6
  32.7 5.5 %collective-permute-done.7 = f32[2,128,1]{2,1,0:T(8,128)S(1)} collective-permute-done((f32[2,128,1]{2,1,0:T(8,128)S(1)}, f32[2,128,1]{2,1,0:T(8,128)S(1)}, u32[]{:S(2)}, u32[]{:S(2)}) %collective-permute-start.7) | collective-permute-done | bytes 1056 | tf_op jit(solution)/shard_map/ppermute | solution.py:144
  38.2 0.0 collective-permute-done.4
  38.2 0.0 collective-permute-done.5
  38.2 0.3 fusion.100
  38.6 0.0 copy-start.7
  38.6 0.3 reshape.114
  38.9 0.0 copy-start.8
  38.9 0.1 copy.27
  39.0 11.5 %all_to_all.10 = f32[8,64,256]{2,1,0:T(8,128)S(1)} all-to-all(f32[8,64,256]{2,1,0:T(8,128)S(1)} %bitcast.309), channel_id=1, replica_groups=mesh['gx'=32,'gy'=8] {'gy'}, dimensions={0} | all-to-all | bytes 1048576 | tf_op jit(solution)/shard_map/all_to_all | solution.py:159
  50.5 1.4 %fusion.108 = f32[32,2,16,256]{3,0,2,1:T(8,128)S(1)} fusion(f32[32,16,1,1]{0,1,3,2:T(8,128)} %constant.67, f32[16,2,16,256]{3,2,1,0:T(8,128)S(1)} %bitcast.307), kind=kOutput, calls=%fused_computation.154 | convolution fusion | flops 25165824 | bytes 1574912 | tf_op jit(solution)/shard_map/dot_general | solution.py:162
  52.0 0.0 copy-done.7
  52.0 0.0 copy-done.8
  52.0 0.0 copy-start.3
  52.0 0.2 multiply_add_fusion.1
  52.2 0.3 copy.30
  52.5 0.3 copy.29
  52.8 0.4 copy-done.3
  53.2 1.0 fusion
  54.3 1.8 %copy.31 = f32[256,2,512]{2,1,0:T(2,128)} copy(f32[256,2,512]{2,0,1:T(8,128)S(1)} %fusion) | data formatting | bytes 2097152 | tf_op jit(solution)/shard_map/dot_general | solution.py:176
  56.1 12.7 %all-to-all-start.1 = ((f32[256,2,512]{2,1,0:T(2,128)}), f32[256,2,512]{2,1,0:T(2,128)S(1)}, u32[]{:S(2)}, u32[]{:S(2)}) async-start(f32[256,2,512]{2,1,0:T(2,128)} %copy.31), calls=%async_computation.1 | async-start | bytes 2097152 | tf_op jit(solution)/shard_map/all_to_all | solution.py:179
  68.7 1.0 convert_element_type.48
  69.7 4.2 %fusion.111 = bf16[1,2,128,512]{3,2,1,0:T(8,128)(2,1)S(1)} fusion(f32[128,512]{1,0:T(8,128)S(1)} %convert_element_type.48, f32[4,2,128,512]{3,2,1,0:T(8,128)} %copy-done.1, f32[4,2,128,518]{3,2,1,0:T(8,128)} %copy-done, f32[4,2,134,512]{3,2,1,0:T(8,128)S(1)} %maximum_convert_fusion.1, f32[1,128,512]{2,1,0:T(8,128)} %get-tuple-element.11, ...), kind=kLoop, calls=%fused_computation.179 | loop fusion | flops 5242880 | bytes 9699328 | tf_op jit(solution)/shard_map/stack | solution.py:137
  73.9 1.1 %pad_maximum_fusion = bf16[4,2,128,512]{3,2,1,0:T(8,128)(2,1)} fusion(bf16[1,2,128,512]{3,2,1,0:T(8,128)(2,1)S(1)} %fusion.111, bf16[1,2,128,512]{3,2,1,0:T(8,128)(2,1)S(1)} %bitcast.314, bf16[1,2,128,512]{3,2,1,0:T(8,128)(2,1)S(1)} %bitcast.313, bf16[1,2,128,512]{3,2,1,0:T(8,128)(2,1)S(1)} %bitcast.312), kind=kLoop, calls=%fused_computation.2 | loop fusion | flops 1572864 | bytes 2097152 | tf_op jit(solution)/shard_map/stack | solution.py:137
  75.0 24.5 %all-to-all-done.1 = f32[256,2,512]{2,1,0:T(2,128)S(1)} async-done(((f32[256,2,512]{2,1,0:T(2,128)}), f32[256,2,512]{2,1,0:T(2,128)S(1)}, u32[]{:S(2)}, u32[]{:S(2)}) %all-to-all-start.1) | async-done | bytes 1048608 | tf_op jit(solution)/shard_map/all_to_all | solution.py:179
  99.6 0.7 reshape.119
  100.3 0.0 copy-start.9
  100.3 0.3 copy.32
  100.6 0.0 copy-start.10
  100.6 2.2 %fusion.125 = f32[32,16,512]{2,1,0:T(8,128)S(1)} fusion(f32[32,16,512]{2,1,0:T(8,128)S(1)} %bitcast.304, f32[512,512,1]{1,0,2:T(8,128)} %constant.68), kind=kOutput, calls=%fused_computation.190 | convolution fusion | flops 805306368 | bytes 3145728 | tf_op jit(solution)/shard_map/dot_general | solution.py:186
  102.9 0.2 multiply_add_fusion
  103.1 0.6 fusion.3
  103.6 0.7 reshape.133
  104.3 1.6 %copy.35 = f32[2,2,16,4096]{3,2,1,0:T(8,128)} copy(f32[2,2,16,4096]{3,0,1,2:T(2,128)S(1)} %reshape.133) | data formatting | bytes 2097152 | tf_op jit(solution)/shard_map/reshape | solution.py:203
  (11 shorter events, 0.1 us)
Async XLA Ops:
  3.1 27.7 %copy-start.1 = (f32[4,2,128,512]{3,2,1,0:T(8,128)}, f32[4,2,128,512]{3,2,1,0:T(8,128)S(1)}, u32[]{:S(2)}) copy-start(f32[4,2,128,512]{3,2,1,0:T(8,128)S(1)} %get-tuple-element.8) | copy-start | bytes 6291460
  3.2 11.0 %collective-permute-start.3 = (bf16[4,2,128,3]{3,2,1,0:T(8,128)(2,1)S(1)}, bf16[4,2,128,3]{3,2,1,0:T(8,128)(2,1)S(1)}, u32[]{:S(2)}, u32[]{:S(2)}) collective-permute-start(bf16[4,2,128,3]{3,2,1,0:T(8,128)(2,1)S(1)} %get-tuple-element.25), channel_id=1, source_target_pairs={{1,0},{2,1},{3,2},{4,3},{5,4},{6,5},{7,6},{0,7},{9,8},{10,9},{11,1... | collective-permute-start | bytes 18440 | tf_op jit(solution)/shard_map/ppermute | solution.py:120
  9.2 10.5 %collective-permute-start.2 = (bf16[4,2,128,3]{3,2,1,0:T(8,128)(2,1)S(1)}, bf16[4,2,128,3]{3,2,1,0:T(8,128)(2,1)S(1)}, u32[]{:S(2)}, u32[]{:S(2)}) collective-permute-start(bf16[4,2,128,3]{3,2,1,0:T(8,128)(2,1)S(1)} %get-tuple-element.24), channel_id=1, source_target_pairs={{0,1},{1,2},{2,3},{3,4},{4,5},{5,6},{6,7},{7,0},{8,9},{9,10},{10,1... | collective-permute-start | bytes 18440 | tf_op jit(solution)/shard_map/ppermute | solution.py:119
  9.3 11.2 %collective-permute-start.1 = (bf16[4,2,3,512]{3,2,1,0:T(4,128)(2,1)S(1)}, bf16[4,2,3,512]{3,2,1,0:T(4,128)(2,1)S(1)}, u32[]{:S(2)}, u32[]{:S(2)}) collective-permute-start(bf16[4,2,3,512]{3,2,1,0:T(4,128)(2,1)S(1)} %get-tuple-element.23), channel_id=1, source_target_pairs={{8,0},{16,8},{24,16},{32,24},{40,32},{48,40},{56,48},{64,56},{72,6... | collective-permute-start | bytes 73736 | tf_op jit(solution)/shard_map/ppermute | solution.py:118
  10.3 10.2 %collective-permute-start = (bf16[4,2,3,512]{3,2,1,0:T(4,128)(2,1)S(1)}, bf16[4,2,3,512]{3,2,1,0:T(4,128)(2,1)S(1)}, u32[]{:S(2)}, u32[]{:S(2)}) collective-permute-start(bf16[4,2,3,512]{3,2,1,0:T(4,128)(2,1)S(1)} %get-tuple-element.22), channel_id=1, source_target_pairs={{0,8},{8,16},{16,24},{24,32},{32,40},{40,48},{48,56},{56,64},{64,7... | collective-permute-start | bytes 73736 | tf_op jit(solution)/shard_map/ppermute | solution.py:117
  20.4 10.4 %copy-start = (f32[4,2,128,518]{3,2,1,0:T(8,128)}, f32[4,2,128,518]{3,2,1,0:T(8,128)S(1)}, u32[]{:S(2)}) copy-start(f32[4,2,128,518]{3,2,1,0:T(8,128)S(1)} %maximum_convert_fusion) | copy-start | bytes 6365188
  20.4 1.1 %copy-start.2 = (s32[128,512]{1,0:T(8,128)S(1)}, s32[128,512]{1,0:T(8,128)}, u32[]{:S(2)}) copy-start(s32[128,512]{1,0:T(8,128)} %param.12) | copy-start | bytes 786436
  25.3 12.9 %collective-permute-start.4 = (f32[2,1,512]{2,1,0:T(1,128)S(1)}, f32[2,1,512]{2,1,0:T(1,128)S(1)}, u32[]{:S(2)}, u32[]{:S(2)}) collective-permute-start(f32[2,1,512]{2,1,0:T(1,128)S(1)} %get-tuple-element.33), channel_id=1, source_target_pairs={{8,0},{16,8},{24,16},{32,24},{40,32},{48,40},{56,48},{64,56},{72,6... | collective-permute-start | bytes 12296 | tf_op jit(solution)/shard_map/ppermute | solution.py:143
  27.2 11.0 %collective-permute-start.5 = (f32[2,1,512]{2,1,0:T(1,128)S(1)}, f32[2,1,512]{2,1,0:T(1,128)S(1)}, u32[]{:S(2)}, u32[]{:S(2)}) collective-permute-start(f32[2,1,512]{2,1,0:T(1,128)S(1)} %get-tuple-element.32), channel_id=1, source_target_pairs={{0,8},{8,16},{16,24},{24,32},{32,40},{40,48},{48,56},{56,64},{64,7... | collective-permute-start | bytes 12296 | tf_op jit(solution)/shard_map/ppermute | solution.py:142
  27.9 4.8 %collective-permute-start.6 = (f32[2,128,1]{2,1,0:T(8,128)S(1)}, f32[2,128,1]{2,1,0:T(8,128)S(1)}, u32[]{:S(2)}, u32[]{:S(2)}) collective-permute-start(f32[2,128,1]{2,1,0:T(8,128)S(1)} %get-tuple-element.29), channel_id=1, source_target_pairs={{1,0},{2,1},{3,2},{4,3},{5,4},{6,5},{7,6},{0,7},{9,8},{10,9},{11,1... | collective-permute-start | bytes 3080 | tf_op jit(solution)/shard_map/ppermute | solution.py:145
  30.8 7.4 %collective-permute-start.7 = (f32[2,128,1]{2,1,0:T(8,128)S(1)}, f32[2,128,1]{2,1,0:T(8,128)S(1)}, u32[]{:S(2)}, u32[]{:S(2)}) collective-permute-start(f32[2,128,1]{2,1,0:T(8,128)S(1)} %get-tuple-element.28), channel_id=1, source_target_pairs={{0,1},{1,2},{2,3},{3,4},{4,5},{5,6},{6,7},{7,0},{8,9},{9,10},{10,1... | collective-permute-start | bytes 3080 | tf_op jit(solution)/shard_map/ppermute | solution.py:144
  38.6 13.4 %copy-start.7 = (f32[16,256]{1,0:T(8,128)S(1)}, f32[16,256]{1,0:T(8,128)}, u32[]{:S(2)}) copy-start(f32[16,256]{1,0:T(8,128)} %constant.43.clone) | copy-start | bytes 49156
  38.9 13.1 %copy-start.8 = (f32[16,256]{1,0:T(8,128)S(1)}, f32[16,256]{1,0:T(8,128)}, u32[]{:S(2)}) copy-start(f32[16,256]{1,0:T(8,128)} %constant.42.clone) | copy-start | bytes 49156
  52.0 1.2 %copy-start.3 = (f32[256,2,512]{2,0,1:T(8,128)S(1)}, f32[256,2,512]{2,0,1:T(8,128)}, u32[]{:S(2)}) copy-start(f32[256,2,512]{2,0,1:T(8,128)} %constant.44.clone) | copy-start | bytes 3145732
  56.1 43.5 %all-to-all-start.1 = ((f32[256,2,512]{2,1,0:T(2,128)}), f32[256,2,512]{2,1,0:T(2,128)S(1)}, u32[]{:S(2)}, u32[]{:S(2)}) async-start(f32[256,2,512]{2,1,0:T(2,128)} %copy.31), calls=%async_computation.1 | async-start | bytes 2097152 | tf_op jit(solution)/shard_map/all_to_all | solution.py:179
  69.7 4.2 %copy-start.4 = (bf16[2,128,512]{2,1,0:T(8,128)(2,1)S(1)}, bf16[2,128,512]{2,1,0:T(8,128)(2,1)}, u32[]{:S(2)}) copy-start(bf16[2,128,512]{2,1,0:T(8,128)(2,1)} %get-tuple-element.7) | copy-start | bytes 786436
  69.7 4.2 %copy-start.5 = (bf16[2,128,512]{2,1,0:T(8,128)(2,1)S(1)}, bf16[2,128,512]{2,1,0:T(8,128)(2,1)}, u32[]{:S(2)}) copy-start(bf16[2,128,512]{2,1,0:T(8,128)(2,1)} %get-tuple-element.5) | copy-start | bytes 786436
  69.7 4.2 %copy-start.6 = (bf16[2,128,512]{2,1,0:T(8,128)(2,1)S(1)}, bf16[2,128,512]{2,1,0:T(8,128)(2,1)}, u32[]{:S(2)}) copy-start(bf16[2,128,512]{2,1,0:T(8,128)(2,1)} %get-tuple-element.3) | copy-start | bytes 786436
  100.3 2.6 %copy-start.9 = (f32[16,256]{1,0:T(8,128)S(1)}, f32[16,256]{1,0:T(8,128)}, u32[]{:S(2)}) copy-start(f32[16,256]{1,0:T(8,128)} %constant.42.clone) | copy-start | bytes 49156
  100.6 2.4 %copy-start.10 = (f32[32,32]{1,0:T(8,128)S(1)}, f32[32,32]{1,0:T(8,128)}, u32[]{:S(2)}) copy-start(f32[32,32]{1,0:T(8,128)} %constant.46.clone) | copy-start | bytes 12292

commit v6 on v5

--- a/solution.py
+++ b/solution.py
@@ -141,12 +141,11 @@
     flow_w = center[2] + DT * rounded[2]
     u_before = lax.ppermute(flow_u[:, rows_x - 1 :, :], "gx", up_x)
     u_after = lax.ppermute(flow_u[:, :1, :], "gx", down_x)
-    v_before = lax.ppermute(flow_v[:, :, rows_y - 1 :], "gy", up_y)
-    v_after = lax.ppermute(flow_v[:, :, :1], "gy", down_y)
     u_next = jnp.concatenate([flow_u[:, 1:, :], u_after], axis=1)
     u_prev = jnp.concatenate([u_before, flow_u[:, :-1, :]], axis=1)
-    v_next = jnp.concatenate([flow_v[:, :, 1:], v_after], axis=2)
-    v_prev = jnp.concatenate([v_before, flow_v[:, :, :-1]], axis=2)
+    zero_col = jnp.zeros_like(flow_v[:, :, :1])
+    v_next = jnp.concatenate([flow_v[:, :, 1:], zero_col], axis=2)
+    v_prev = jnp.concatenate([zero_col, flow_v[:, :, :-1]], axis=2)
     diverge = ((u_next - u_prev) + (v_next - v_prev) + (raised(flow_w) - lowered(flow_w))) * 0.5
 
     total_y = rows_y * count_y
@@ -155,8 +154,28 @@
     split_y = rows_y // n_q
     piece_x = rows_x // count_y
     sent = diverge.reshape(levels, count_y, piece_x, split_y, n_q).transpose(1, 3, 0, 2, 4)
-    sent = sent.reshape(count_y, split_y * levels * piece_x, n_q)
+    main_rows = split_y * levels * piece_x
+    sent = sent.reshape(count_y, main_rows, n_q)
+    edges = jnp.stack([flow_v[:, :, 0], flow_v[:, :, rows_y - 1]], axis=0)
+    edges = edges.reshape(2, levels, count_y, piece_x).transpose(2, 0, 1, 3)
+    edge_width = 2 * levels * piece_x
+    edges = edges.reshape(count_y, 1, edge_width)
+    edges = jnp.pad(edges, ((0, 0), (0, 7), (0, n_q - edge_width)))
+    sent = jnp.concatenate([sent, edges], axis=1)
     columns = lax.all_to_all(sent, "gy", split_axis=0, concat_axis=0, tiled=True)
+    edges = columns[:, main_rows, :edge_width].reshape(count_y, 2, levels, piece_x)
+    last_prev = jnp.roll(edges[:, 1], 1, axis=0)
+    first_next = jnp.roll(edges[:, 0], -1, axis=0)
+    columns = columns[:, :main_rows].reshape(count_y, split_y, levels, piece_x, n_q)
+    q_at = lax.broadcasted_iota(jnp.int32, columns.shape, 4)
+    half_at = lax.broadcasted_iota(jnp.int32, columns.shape, 1)
+    columns = (
+        columns
+        + jnp.where((q_at == 0) & (half_at == 0), (-0.5 * last_prev)[:, None, :, :, None], 0.0)
+        + jnp.where(
+            (q_at == n_q - 1) & (half_at == split_y - 1), (0.5 * first_next)[:, None, :, :, None], 0.0
+        )
+    )
     columns = columns.reshape(n_p, levels, piece_x, n_q)
     w1, t1c, t1s, w2 = y_tables(n_p, n_q)
     stage1 = lax.dot_general(

time: 106 us -> 110 us (1.038)
  blocking collectives: 11.5 us -> 0 us
  local copies, waits for them, and re-layouts: 8.93 us -> 15.1 us
  other arithmetic: 15.4 us -> 20.8 us
  waiting for transfers between devices: 37.8 us -> 40.5 us
  starting transfers between devices: 25.9 us -> 27.1 us
    all_to_all x1 -> x0, blocking collectives: 11.5 us -> none  [body(): lax.all_to_all(sent, 'gy', split_axis=0, concat_axis=0, tiled=True)]
    all_to_all x0 -> x1, waiting for transfers between devices: none -> 9.36 us  [body(): lax.all_to_all(sent, 'gy', split_axis=0, concat_axis=0, tiled=True)]
    ppermute x2 -> x0, waiting for transfers between devices: 5.64 us -> none  [the longest x1 5.48 us: body(): v_before = lax.ppermute(flow_v[:, :, rows_y - 1:], 'gy', up_y)]
    all_to_all x0 -> x1, starting transfers between devices: none -> 4.17 us  [body(): lax.all_to_all(sent, 'gy', split_axis=0, concat_axis=0, tiled=True)]
    ppermute x2 -> x0, starting transfers between devices: 2.83 us -> none  [the longest x1 2.83 us: body(): v_after = lax.ppermute(flow_v[:, :, :1], 'gy', down_y)]
    add x1, other arithmetic: 1.75 us -> 4.52 us  [body(): flow_w = center[2] + DT * rounded[2]]
    another operation x0 -> x4, local copies, waits for them, and re-layouts: none -> 1.97 us  [the longest x1 1.07 us: body(): tendency = jnp.stack(pieces)]
    slice x2 -> x6, local copies, waits for them, and re-layouts: 0.31 us -> 1.93 us  [the longest x1 1.13 us: body(): v_next = jnp.concatenate([flow_v[:, :, 1:], zero_col], axis=2)]
  transfers between devices with their start and end apart: 9 -> 8, of which waited for: 5 -> 4; matrix products, arithmetic and copies ran while one was open for 9% -> 13% of each run, Pallas kernels for 0% -> 0%
where the time goes in v6:
time: 110 us; the launch traced here: 109 us
  waiting for transfers between devices  40.5 us (37%)
  starting transfers between devices  27.1 us (25%)
  other arithmetic  20.8 us (19%)
  local copies, waits for them, and re-layouts  15.1 us (14%)
  matrix products  4.57 us (4%)
    all_to_all x1, waiting for transfers between devices, body(): lax.all_to_all(spectrum_y, ('gx', 'gy'), split_axis=0, concat_axis=0, til...  23.4 us
    all_to_all x1, starting transfers between devices, body(): lax.all_to_all(spectrum_y, ('gx', 'gy'), split_axis=0, concat_axis=0, til...  12.7 us
    all_to_all x1, waiting for transfers between devices, body(): lax.all_to_all(sent, 'gy', split_axis=0, concat_axis=0, tiled=True)  9.36 us
    ppermute x1, starting transfers between devices, body(): y_after = lax.ppermute(masked[:, :, :, :3], 'gy', down_y)  6 us
    ppermute x1, waiting for transfers between devices, body(): y_before = lax.ppermute(masked[:, :, :, rows_y - 3:], 'gy', up_y)  5.53 us
    another operation x2, other arithmetic, body(): tendency = jnp.stack(pieces)  5.32 us
    add x1, other arithmetic, body(): flow_w = center[2] + DT * rounded[2]  4.52 us
    all_to_all x1, starting transfers between devices, body(): lax.all_to_all(sent, 'gy', split_axis=0, concat_axis=0, tiled=True)  4.17 us
  transfers between devices with their start and end apart: 8, of which 4 were waited for; matrix products, arithmetic and copies ran while one was open for 13% of the time, Pallas kernels for 0%

profile of v6, /device:TPU:1, one launch (start us, length us, event | category | flops | bytes accessed | tf_op | source)
XLA Modules:
  0.0 109.1 jit_solution(2533922580002990293)
XLA Ops:
  0.6 1.0 convert_convert_fusion
  1.6 1.4 %fusion.117 = (f32[4,2,128,512]{3,2,1,0:T(8,128)S(1)}, bf16[4,2,128,512]{3,2,1,0:T(8,128)(2,1)S(1)}) fusion(bf16[4,2,128,512]{3,2,1,0:T(8,128)(2,1)} %param.11, bf16[2,128,512]{2,1,0:T(8,128)(2,1)S(1)} %convert_convert_fusion), kind=kLoop, calls=%fused_computation.196 | loop fusion | flops 1048576 | bytes 4456448 | tf_op jit(solution)/shard_map/convert_element_type | solution.py:123
  3.1 0.1 fusion.119
  3.2 6.0 %collective-permute-start.3 = (bf16[4,2,128,3]{3,2,1,0:T(8,128)(2,1)S(1)}, bf16[4,2,128,3]{3,2,1,0:T(8,128)(2,1)S(1)}, u32[]{:S(2)}, u32[]{:S(2)}) collective-permute-start(bf16[4,2,128,3]{3,2,1,0:T(8,128)(2,1)S(1)} %get-tuple-element.27), channel_id=1, source_target_pairs={{1,0},{2,1},{3,2},{4,3},{5,4},{6,5},{7,6},{0,7},{9,8},{10,9},{11,1... | collective-permute-start | bytes 18440 | tf_op jit(solution)/shard_map/ppermute | solution.py:120
  9.2 0.0 collective-permute-start.2
  9.3 1.0 collective-permute-start.1
  10.3 0.8 collective-permute-start
  11.1 1.0 slice_bitcast_fusion.18
  12.1 2.1 %collective-permute-done.3 = bf16[4,2,128,3]{3,2,1,0:T(8,128)(2,1)S(1)} collective-permute-done((bf16[4,2,128,3]{3,2,1,0:T(8,128)(2,1)S(1)}, bf16[4,2,128,3]{3,2,1,0:T(8,128)(2,1)S(1)}, u32[]{:S(2)}, u32[]{:S(2)}) %collective-permute-start.3) | collective-permute-done | bytes 6176 | tf_op jit(solution)/shard_map/ppermute | solution.py:120
  14.2 5.5 %collective-permute-done.2 = bf16[4,2,128,3]{3,2,1,0:T(8,128)(2,1)S(1)} collective-permute-done((bf16[4,2,128,3]{3,2,1,0:T(8,128)(2,1)S(1)}, bf16[4,2,128,3]{3,2,1,0:T(8,128)(2,1)S(1)}, u32[]{:S(2)}, u32[]{:S(2)}) %collective-permute-start.2) | collective-permute-done | bytes 6176 | tf_op jit(solution)/shard_map/ppermute | solution.py:119
  19.8 0.7 maximum_convert_fusion
  20.4 0.0 copy-start.2
  20.4 0.0 collective-permute-done
  20.5 0.4 maximum_convert_fusion.1
  20.8 0.7 copy-done.2
  21.6 1.7 %multiply_add_fusion.4 = (f32[2,128,512]{2,1,0:T(8,128)S(1)}, bf16[2,128,512]{2,1,0:T(8,128)(2,1)}) fusion(f32[4,2,128,512]{3,2,1,0:T(8,128)S(1)} %get-tuple-element.10, f32[4,2,128,518]{3,2,1,0:T(8,128)S(1)} %maximum_convert_fusion, f32[4,2,134,512]{3,2,1,0:T(8,128)S(1)} %maximum_convert_fusion.1, f32[1,128,512]{2,1,0:T(8,128)S(1)} %get-tuple-element.19, ...), kind=kLoop, calls=%fused_computation.164 | loop fusion | flops 5242880 | bytes 9437184 | tf_op jit(solution)/shard_map/add | solution.py:139
  23.2 0.6 fusion.122
  23.9 0.9 fusion.123
  24.8 1.6 %multiply_add_fusion.3 = (f32[2,128,512]{2,1,0:T(8,128)S(1)}, bf16[2,128,512]{2,1,0:T(8,128)(2,1)}) fusion(f32[4,2,128,512]{3,2,1,0:T(8,128)S(1)} %get-tuple-element.10, f32[4,2,128,518]{3,2,1,0:T(8,128)S(1)} %maximum_convert_fusion, f32[4,2,134,512]{3,2,1,0:T(8,128)S(1)} %maximum_convert_fusion.1, f32[1,128,512]{2,1,0:T(8,128)S(1)} %get-tuple-element.17, ...), kind=kLoop, calls=%fused_computation.163 | loop fusion | flops 5242880 | bytes 9437184 | tf_op jit(solution)/shard_map/add | solution.py:140
  26.4 0.7 slice_reduce_fusion.1
  27.1 1.1 %fusion.120 = (f32[2,128,511]{2,1,0:T(8,128)}, f32[2,128,511]{2,1,0:T(8,128)}) fusion(f32[2,128,512]{2,1,0:T(8,128)S(1)} %get-tuple-element.8), kind=kLoop, calls=%fused_computation.199 | loop fusion | bytes 2093056 | tf_op jit(solution)/shard_map/slice | solution.py:147
  28.3 0.1 stack.28
  28.3 0.7 stack.27
  29.1 1.8 %collective-permute-start.4 = (f32[2,1,512]{2,1,0:T(1,128)}, f32[2,1,512]{2,1,0:T(1,128)}, u32[]{:S(2)}, u32[]{:S(2)}) collective-permute-start(f32[2,1,512]{2,1,0:T(1,128)} %get-tuple-element.33), channel_id=1, source_target_pairs={{8,0},{16,8},{24,16},{32,24},{40,32},{48,40},{56,48},{64,56},{72,6... | collective-permute-start | bytes 12296 | tf_op jit(solution)/shard_map/ppermute | solution.py:143
  30.9 0.7 collective-permute-start.5
  31.6 4.5 %multiply_add_fusion.2 = (f32[2,128,512]{2,1,0:T(8,128)S(1)}, bf16[2,128,512]{2,1,0:T(8,128)(2,1)}) fusion(f32[4,2,128,512]{3,2,1,0:T(8,128)} %copy-done.1, f32[4,2,128,518]{3,2,1,0:T(8,128)} %copy-done, f32[4,2,134,512]{3,2,1,0:T(8,128)S(1)} %maximum_convert_fusion.1, f32[1,128,512]{2,1,0:T(8,128)S(1)} %get-tuple-element.15, ...), kind=kLoop, calls=%fused_computation.162 | loop fusion | flops 5505024 | bytes 9961472 | tf_op jit(solution)/shard_map/add | solution.py:141
  36.1 0.8 fusion.121
  36.9 0.1 reshape.168
  37.0 0.0 collective-permute-done.4
  37.0 1.8 %fusion.100 = f32[2,128,512]{2,1,0:T(8,128)S(1)} fusion(f32[2,1,512]{2,1,0:T(1,128)} %collective-permute-done.4, f32[2,127,512]{2,1,0:T(8,128)} %get-tuple-element.35, f32[2,127,512]{2,1,0:T(8,128)S(1)} %get-tuple-element.34, f32[2,1,512]{2,1,0:T(1,128)} %collective-permute-done.5, f32[1,128,512]{2,1,0:T(8,128)} %get-tuple-element.31, ...), kind=kLoop, calls=%fused_computation.142 | loop fusion | flops 1048576 | bytes 3143680 | tf_op jit(solution)/shard_map/mul | solution.py:149
  38.8 0.3 reshape.166
  39.1 0.1 copy.67
  39.2 0.0 copy-start.9
  39.2 0.9 select_maximum_fusion
  40.1 4.2 %all-to-all-start = ((f32[8,72,256]{2,1,0:T(8,128)}), f32[8,72,256]{2,1,0:T(8,128)S(1)}, u32[]{:S(2)}, u32[]{:S(2)}) async-start(f32[8,72,256]{2,1,0:T(8,128)} %select_maximum_fusion), calls=%async_computation | async-start | bytes 1179648 | tf_op jit(solution)/shard_map/all_to_all | solution.py:165
  44.2 0.0 copy-start.6
  44.3 0.1 iota.49
  44.4 0.1 iota.43
  44.5 9.4 %all-to-all-done = f32[8,72,256]{2,1,0:T(8,128)S(1)} async-done(((f32[8,72,256]{2,1,0:T(8,128)}), f32[8,72,256]{2,1,0:T(8,128)S(1)}, u32[]{:S(2)}, u32[]{:S(2)}) %all-to-all-start) | async-done | bytes 589856 | tf_op jit(solution)/shard_map/all_to_all | solution.py:165
  53.9 0.1 reshape_squeeze.3
  54.1 0.3 select_add_fusion
  54.4 0.7 fusion.108
  55.2 0.0 copy-start.3
  55.2 0.2 multiply_add_fusion.1
  55.4 0.3 copy.78
  55.7 0.3 copy.77
  56.0 0.4 copy-done.3
  56.4 1.0 fusion
  57.4 1.8 %copy.79 = f32[256,2,512]{2,1,0:T(2,128)} copy(f32[256,2,512]{2,0,1:T(8,128)S(1)} %fusion) | data formatting | bytes 2097152 | tf_op jit(solution)/shard_map/dot_general | solution.py:195
  59.2 12.7 %all-to-all-start.1 = ((f32[256,2,512]{2,1,0:T(2,128)}), f32[256,2,512]{2,1,0:T(2,128)S(1)}, u32[]{:S(2)}, u32[]{:S(2)}) async-start(f32[256,2,512]{2,1,0:T(2,128)} %copy.79), calls=%async_computation.1 | async-start | bytes 2097152 | tf_op jit(solution)/shard_map/all_to_all | solution.py:198
  71.9 1.0 convert_element_type.50
  72.9 1.1 convert_bitcast_fusion
  73.9 4.2 %fusion.111 = bf16[1,2,128,512]{3,2,1,0:T(8,128)(2,1)S(1)} fusion(f32[128,512]{1,0:T(8,128)S(1)} %convert_element_type.50, f32[4,2,128,512]{3,2,1,0:T(8,128)} %copy-done.1, f32[4,2,128,518]{3,2,1,0:T(8,128)} %copy-done, f32[4,2,134,512]{3,2,1,0:T(8,128)S(1)} %maximum_convert_fusion.1, f32[1,128,512]{2,1,0:T(8,128)} %get-tuple-element.13, ...), kind=kLoop, calls=%fused_computation.181 | loop fusion | flops 5242880 | bytes 9699328 | tf_op jit(solution)/shard_map/stack | solution.py:137
  78.2 1.1 %pad_maximum_fusion = bf16[4,2,128,512]{3,2,1,0:T(8,128)(2,1)} fusion(bf16[1,2,128,512]{3,2,1,0:T(8,128)(2,1)S(1)} %fusion.111, bf16[1,2,128,512]{3,2,1,0:T(8,128)(2,1)S(1)} %get-tuple-element.40, bf16[1,2,128,512]{3,2,1,0:T(8,128)(2,1)S(1)} %get-tuple-element.41, bf16[1,2,128,512]{3,2,1,0:T(8,128)(2,1)S(1)} %bitcast.325), kind=kLoop, calls=%fused_computation.2 | loop fusion | flops 1572864 | bytes 2097152 | tf_op jit(solution)/shard_map/stack | solution.py:137
  79.3 23.4 %all-to-all-done.1 = f32[256,2,512]{2,1,0:T(2,128)S(1)} async-done(((f32[256,2,512]{2,1,0:T(2,128)}), f32[256,2,512]{2,1,0:T(2,128)S(1)}, u32[]{:S(2)}, u32[]{:S(2)}) %all-to-all-start.1) | async-done | bytes 1048608 | tf_op jit(solution)/shard_map/all_to_all | solution.py:198
  102.7 0.7 reshape.172
  103.4 0.0 copy-start.7
  103.5 0.3 copy.80
  103.8 0.0 copy-start.8
  103.8 2.2 %fusion.126 = f32[32,16,512]{2,1,0:T(8,128)S(1)} fusion(f32[32,16,512]{2,1,0:T(8,128)S(1)} %bitcast.317, f32[512,512,1]{1,0,2:T(8,128)} %constant.87), kind=kOutput, calls=%fused_computation.205 | convolution fusion | flops 805306368 | bytes 3145728 | tf_op jit(solution)/shard_map/dot_general | solution.py:205
  106.1 0.2 multiply_add_fusion
  106.2 0.6 fusion.3
  106.8 0.7 reshape.186
  107.5 1.6 %copy.83 = f32[2,2,16,4096]{3,2,1,0:T(8,128)} copy(f32[2,2,16,4096]{3,0,1,2:T(2,128)S(1)} %reshape.186) | data formatting | bytes 2097152 | tf_op jit(solution)/shard_map/reshape | solution.py:222
  (33 shorter events, 0.2 us)
Async XLA Ops:
  3.1 21.7 %copy-start.1 = (f32[4,2,128,512]{3,2,1,0:T(8,128)}, f32[4,2,128,512]{3,2,1,0:T(8,128)S(1)}, u32[]{:S(2)}) copy-start(f32[4,2,128,512]{3,2,1,0:T(8,128)S(1)} %get-tuple-element.10) | copy-start | bytes 6291460
  3.2 11.0 %collective-permute-start.3 = (bf16[4,2,128,3]{3,2,1,0:T(8,128)(2,1)S(1)}, bf16[4,2,128,3]{3,2,1,0:T(8,128)(2,1)S(1)}, u32[]{:S(2)}, u32[]{:S(2)}) collective-permute-start(bf16[4,2,128,3]{3,2,1,0:T(8,128)(2,1)S(1)} %get-tuple-element.27), channel_id=1, source_target_pairs={{1,0},{2,1},{3,2},{4,3},{5,4},{6,5},{7,6},{0,7},{9,8},{10,9},{11,1... | collective-permute-start | bytes 18440 | tf_op jit(solution)/shard_map/ppermute | solution.py:120
  9.2 10.5 %collective-permute-start.2 = (bf16[4,2,128,3]{3,2,1,0:T(8,128)(2,1)S(1)}, bf16[4,2,128,3]{3,2,1,0:T(8,128)(2,1)S(1)}, u32[]{:S(2)}, u32[]{:S(2)}) collective-permute-start(bf16[4,2,128,3]{3,2,1,0:T(8,128)(2,1)S(1)} %get-tuple-element.26), channel_id=1, source_target_pairs={{0,1},{1,2},{2,3},{3,4},{4,5},{5,6},{6,7},{7,0},{8,9},{9,10},{10,1... | collective-permute-start | bytes 18440 | tf_op jit(solution)/shard_map/ppermute | solution.py:119
  9.3 11.2 %collective-permute-start.1 = (bf16[4,2,3,512]{3,2,1,0:T(4,128)(2,1)S(1)}, bf16[4,2,3,512]{3,2,1,0:T(4,128)(2,1)S(1)}, u32[]{:S(2)}, u32[]{:S(2)}) collective-permute-start(bf16[4,2,3,512]{3,2,1,0:T(4,128)(2,1)S(1)} %get-tuple-element.25), channel_id=1, source_target_pairs={{8,0},{16,8},{24,16},{32,24},{40,32},{48,40},{56,48},{64,56},{72,6... | collective-permute-start | bytes 73736 | tf_op jit(solution)/shard_map/ppermute | solution.py:118
  10.3 10.2 %collective-permute-start = (bf16[4,2,3,512]{3,2,1,0:T(4,128)(2,1)S(1)}, bf16[4,2,3,512]{3,2,1,0:T(4,128)(2,1)S(1)}, u32[]{:S(2)}, u32[]{:S(2)}) collective-permute-start(bf16[4,2,3,512]{3,2,1,0:T(4,128)(2,1)S(1)} %get-tuple-element.24), channel_id=1, source_target_pairs={{0,8},{8,16},{16,24},{24,32},{32,40},{40,48},{48,56},{56,64},{64,7... | collective-permute-start | bytes 73736 | tf_op jit(solution)/shard_map/ppermute | solution.py:117
  20.4 4.4 %copy-start = (f32[4,2,128,518]{3,2,1,0:T(8,128)}, f32[4,2,128,518]{3,2,1,0:T(8,128)S(1)}, u32[]{:S(2)}) copy-start(f32[4,2,128,518]{3,2,1,0:T(8,128)S(1)} %maximum_convert_fusion) | copy-start | bytes 6365188
  20.4 1.1 %copy-start.2 = (s32[128,512]{1,0:T(8,128)S(1)}, s32[128,512]{1,0:T(8,128)}, u32[]{:S(2)}) copy-start(s32[128,512]{1,0:T(8,128)} %param.12) | copy-start | bytes 786436
  29.1 7.9 %collective-permute-start.4 = (f32[2,1,512]{2,1,0:T(1,128)}, f32[2,1,512]{2,1,0:T(1,128)}, u32[]{:S(2)}, u32[]{:S(2)}) collective-permute-start(f32[2,1,512]{2,1,0:T(1,128)} %get-tuple-element.33), channel_id=1, source_target_pairs={{8,0},{16,8},{24,16},{32,24},{40,32},{48,40},{56,48},{64,56},{72,6... | collective-permute-start | bytes 12296 | tf_op jit(solution)/shard_map/ppermute | solution.py:143
  30.9 6.1 %collective-permute-start.5 = (f32[2,1,512]{2,1,0:T(1,128)}, f32[2,1,512]{2,1,0:T(1,128)}, u32[]{:S(2)}, u32[]{:S(2)}) collective-permute-start(f32[2,1,512]{2,1,0:T(1,128)} %get-tuple-element.32), channel_id=1, source_target_pairs={{0,8},{8,16},{16,24},{24,32},{32,40},{40,48},{48,56},{56,64},{64,7... | collective-permute-start | bytes 12296 | tf_op jit(solution)/shard_map/ppermute | solution.py:142
  39.2 15.2 %copy-start.9 = (f32[32,16,1,1]{0,1,3,2:T(8,128)S(1)}, f32[32,16,1,1]{0,1,3,2:T(8,128)}, u32[]{:S(2)}) copy-start(f32[32,16,1,1]{0,1,3,2:T(8,128)} %constant.86) | copy-start | bytes 6148
  40.1 13.8 %all-to-all-start = ((f32[8,72,256]{2,1,0:T(8,128)}), f32[8,72,256]{2,1,0:T(8,128)S(1)}, u32[]{:S(2)}, u32[]{:S(2)}) async-start(f32[8,72,256]{2,1,0:T(8,128)} %select_maximum_fusion), calls=%async_computation | async-start | bytes 1179648 | tf_op jit(solution)/shard_map/all_to_all | solution.py:165
  44.2 10.9 %copy-start.5 = (f32[16,256]{1,0:T(8,128)S(1)}, f32[16,256]{1,0:T(8,128)}, u32[]{:S(2)}) copy-start(f32[16,256]{1,0:T(8,128)} %constant.56.clone) | copy-start | bytes 49156
  44.2 10.9 %copy-start.6 = (f32[16,256]{1,0:T(8,128)S(1)}, f32[16,256]{1,0:T(8,128)}, u32[]{:S(2)}) copy-start(f32[16,256]{1,0:T(8,128)} %constant.55.clone) | copy-start | bytes 49156
  55.2 1.2 %copy-start.3 = (f32[256,2,512]{2,0,1:T(8,128)S(1)}, f32[256,2,512]{2,0,1:T(8,128)}, u32[]{:S(2)}) copy-start(f32[256,2,512]{2,0,1:T(8,128)} %constant.57.clone) | copy-start | bytes 3145732
  59.2 43.5 %all-to-all-start.1 = ((f32[256,2,512]{2,1,0:T(2,128)}), f32[256,2,512]{2,1,0:T(2,128)S(1)}, u32[]{:S(2)}, u32[]{:S(2)}) async-start(f32[256,2,512]{2,1,0:T(2,128)} %copy.79), calls=%async_computation.1 | async-start | bytes 2097152 | tf_op jit(solution)/shard_map/all_to_all | solution.py:198
  73.9 4.2 %copy-start.4 = (bf16[2,128,512]{2,1,0:T(8,128)(2,1)S(1)}, bf16[2,128,512]{2,1,0:T(8,128)(2,1)}, u32[]{:S(2)}) copy-start(bf16[2,128,512]{2,1,0:T(8,128)(2,1)} %get-tuple-element.7) | copy-start | bytes 786436
  103.4 2.6 %copy-start.7 = (f32[16,256]{1,0:T(8,128)S(1)}, f32[16,256]{1,0:T(8,128)}, u32[]{:S(2)}) copy-start(f32[16,256]{1,0:T(8,128)} %constant.55.clone) | copy-start | bytes 49156
  103.8 2.4 %copy-start.8 = (f32[32,32]{1,0:T(8,128)S(1)}, f32[32,32]{1,0:T(8,128)}, u32[]{:S(2)}) copy-start(f32[32,32]{1,0:T(8,128)} %constant.59.clone) | copy-start | bytes 12292

commit v7 on v5

--- a/solution.py
+++ b/solution.py
@@ -5,6 +5,7 @@
 import jax.numpy as jnp
 from jax import lax
 from jax.sharding import PartitionSpec as P
+
 
 NU = 0.1
 BETA = 0.5
@@ -114,10 +115,25 @@
     surface = (level == heights[None]).astype(jnp.float32) * surface_flag[None].astype(jnp.float32)
     masked = state * fluid.astype(jnp.bfloat16)[None]
 
-    x_before = lax.ppermute(masked[:, :, rows_x - 3 :, :], "gx", up_x)
-    x_after = lax.ppermute(masked[:, :, :3, :], "gx", down_x)
-    y_before = lax.ppermute(masked[:, :, :, rows_y - 3 :], "gy", up_y)
-    y_after = lax.ppermute(masked[:, :, :, :3], "gy", down_y)
+    def masked_part(xs, ys):
+        lev = lax.broadcasted_iota(jnp.int32, (levels, xs.stop - xs.start, ys.stop - ys.start), 0)
+        wet = (lev >= heights[None, xs, ys]).astype(jnp.bfloat16)
+        return state[:, :, xs, ys] * wet[None]
+
+    all_x, all_y = slice(0, rows_x), slice(0, rows_y)
+    x_before = lax.ppermute(masked_part(slice(rows_x - 3, rows_x), all_y), "gx", up_x)
+    x_after = lax.ppermute(masked_part(slice(0, 3), all_y), "gx", down_x)
+
+    def lanes_x(part):
+        return jnp.swapaxes(part, 2, 3).reshape(-1, rows_x)
+
+    def from_lanes_x(flat):
+        return jnp.swapaxes(flat.reshape(state.shape[0], levels, 3, rows_x), 2, 3)
+
+    y_before = from_lanes_x(
+        lax.ppermute(lanes_x(masked_part(all_x, slice(rows_y - 3, rows_y))), "gy", up_y)
+    )
+    y_after = from_lanes_x(lax.ppermute(lanes_x(masked_part(all_x, slice(0, 3))), "gy", down_y))
     pad_x = jnp.concatenate([x_before, masked, x_after], axis=2).astype(jnp.float32)
     pad_y = jnp.concatenate([y_before, masked, y_after], axis=3).astype(jnp.float32)
     center = masked.astype(jnp.float32)
@@ -136,13 +152,16 @@
         rounded.append(lax.reduce_precision(exact, exponent_bits=8, mantissa_bits=7))
     tendency = jnp.stack(pieces)
 
-    flow_u = center[0] + DT * rounded[0]
-    flow_v = center[1] + DT * rounded[1]
-    flow_w = center[2] + DT * rounded[2]
+    flows = []
+    for component in range(3):
+        flows.append(center[component] + DT * rounded[component])
+    flow_u, flow_v, flow_w = flows
     u_before = lax.ppermute(flow_u[:, rows_x - 1 :, :], "gx", up_x)
     u_after = lax.ppermute(flow_u[:, :1, :], "gx", down_x)
-    v_before = lax.ppermute(flow_v[:, :, rows_y - 1 :], "gy", up_y)
-    v_after = lax.ppermute(flow_v[:, :, :1], "gy", down_y)
+    v_before = jnp.swapaxes(
+        lax.ppermute(jnp.swapaxes(flow_v[:, :, rows_y - 1 :], 1, 2), "gy", up_y), 1, 2
+    )
+    v_after = jnp.swapaxes(lax.ppermute(jnp.swapaxes(flow_v[:, :, :1], 1, 2), "gy", down_y), 1, 2)
     u_next = jnp.concatenate([flow_u[:, 1:, :], u_after], axis=1)
     u_prev = jnp.concatenate([u_before, flow_u[:, :-1, :]], axis=1)
     v_next = jnp.concatenate([flow_v[:, :, 1:], v_after], axis=2)

time: 106 us -> 110 us (1.038)
  waiting for transfers between devices: 37.8 us -> 28.5 us
  local copies, waits for them, and re-layouts: 8.93 us -> 16.6 us
  other arithmetic: 15.4 us -> 17.8 us
  starting transfers between devices: 25.9 us -> 27.8 us
    ppermute x6, waiting for transfers between devices: 13.3 us -> 3.69 us  [the longest x1 2.69 us: body(): lax.ppermute(jnp.swapaxes(flow_v[:, :, rows_y - 1:], 1, 2), 'gy', up_y)]
    ppermute x6, starting transfers between devices: 10.7 us -> 13.6 us  [the longest x1 6 us: body(): lax.ppermute(lanes_x(masked_part(all_x, slice(0, 3))), 'gy', down_y)]
    transpose x0 -> x6, local copies, waits for them, and re-layouts: none -> 2.31 us  [the longest x1 0.81 us: body(): jnp.swapaxes(lax.ppermute(jnp.swapaxes(flow_v[:, :, rows_y - 1:], 1, 2),...]
    convert_element_type x1, other arithmetic: 0.35 us -> 2.21 us  [body(): jnp.concatenate([x_before, masked, x_after], axis=2).astype(jnp.float32)]
    all_to_all x1, starting transfers between devices: 12.7 us -> 10.9 us  [body(): lax.all_to_all(spectrum_y, ('gx', 'gy'), split_axis=0, concat_axis=0, til...]
    mul x1, other arithmetic: 0.34 us -> 1.89 us  [body(): (u_next - u_prev + (v_next - v_prev) + (raised(flow_w) - lowered(flow_w))...]
    ppermute x1, starting transfers between devices: 1.89 us -> 3.36 us  [body(): u_after = lax.ppermute(flow_u[:, :1, :], 'gx', down_x)]
    unnamed x22 -> x40, local copies, waits for them, and re-layouts: 1.23 us -> 2.56 us
  transfers between devices with their start and end apart: 9 -> 9, of which waited for: 5 -> 3; matrix products, arithmetic and copies ran while one was open for 9% -> 12% of each run, Pallas kernels for 0% -> 0%
where the time goes in v7:
time: 110 us; the launch traced here: 109 us
  waiting for transfers between devices  28.5 us (26%)
  starting transfers between devices  27.8 us (25%)
  other arithmetic  17.8 us (16%)
  local copies, waits for them, and re-layouts  16.6 us (15%)
  blocking collectives  12.5 us (11%)
  matrix products  5.25 us (5%)
    all_to_all x1, waiting for transfers between devices, body(): lax.all_to_all(spectrum_y, ('gx', 'gy'), split_axis=0, concat_axis=0, til...  24.8 us
    all_to_all x1, blocking collectives, body(): lax.all_to_all(sent, 'gy', split_axis=0, concat_axis=0, tiled=True)  12.5 us
    all_to_all x1, starting transfers between devices, body(): lax.all_to_all(spectrum_y, ('gx', 'gy'), split_axis=0, concat_axis=0, til...  10.9 us
    ppermute x1, starting transfers between devices, body(): lax.ppermute(lanes_x(masked_part(all_x, slice(0, 3))), 'gy', down_y)  6 us
    ppermute x1, starting transfers between devices, body(): lax.ppermute(jnp.swapaxes(flow_v[:, :, :1], 1, 2), 'gy', down_y)  5.65 us
    another operation x2, other arithmetic, body(): tendency = jnp.stack(pieces)  5.17 us
    add x3, other arithmetic, body(): flows.append(center[component] + DT * rounded[component])  5.03 us
    ppermute x1, starting transfers between devices, body(): u_after = lax.ppermute(flow_u[:, :1, :], 'gx', down_x)  3.36 us
  transfers between devices with their start and end apart: 9, of which 3 were waited for; matrix products, arithmetic and copies ran while one was open for 12% of the time, Pallas kernels for 0%

profile of v7, /device:TPU:1, one launch (start us, length us, event | category | flops | bytes accessed | tf_op | source)
XLA Modules:
  0.0 109.4 jit_solution(16188078948106136185)
XLA Ops:
  0.6 0.0 copy-start.4
  0.7 1.1 fusion.127
  1.8 1.2 %multiply_bitcast_fusion.1 = (bf16[4,2,3,128]{2,3,1,0:T(8,128)(2,1)S(1)}, bf16[4,2,3,128]{2,3,1,0:T(8,128)(2,1)S(1)}) fusion(bf16[4,2,128,512]{3,2,1,0:T(8,128)(2,1)} %param.11, bf16[2,128,3]{2,1,0:T(8,128)(2,1)S(1)} %get-tuple-element.40, bf16[2,128,3]{2,1,0:T(8,128)(2,1)S(1)} %get-tuple-element.41), kind=kLoop, calls=%fused_computation.180 | loop fusion | flops 6144 | bytes 27648 | tf_op jit(solution)/shard_map/transpose | solution.py:128
  2.9 0.1 copy.42
  3.1 6.0 %collective-permute-start.3 = (bf16[24,128]{1,0:T(8,128)(2,1)S(1)}, bf16[24,128]{1,0:T(8,128)(2,1)S(1)}, u32[]{:S(2)}, u32[]{:S(2)}) collective-permute-start(bf16[24,128]{1,0:T(8,128)(2,1)S(1)} %reshape.152), channel_id=1, source_target_pairs={{1,0},{2,1},{3,2},{4,3},{5,4},{6,5},{7,6},{0,7},{9,8},{10,9},{11,1... | collective-permute-start | bytes 18440 | tf_op jit(solution)/shard_map/ppermute | solution.py:136
  9.1 0.1 copy.41
  9.3 0.1 collective-permute-start.2
  9.5 1.0 collective-permute-start.1
  10.5 0.8 collective-permute-start
  11.3 0.2 fusion.121
  11.6 1.3 %copy-done.1 = f32[4,2,128,512]{3,2,1,0:T(8,128)} copy-done((f32[4,2,128,512]{3,2,1,0:T(8,128)}, f32[4,2,128,512]{3,2,1,0:T(8,128)S(1)}, u32[]{:S(2)}) %copy-start.1) | copy-done | bytes 2097176
  12.9 1.3 %slice_bitcast_fusion.18 = (f32[1,128,512]{2,1,0:T(8,128)}, f32[1,128,512]{2,1,0:T(8,128)}, f32[1,128,512]{2,1,0:T(8,128)}, f32[1,128,512]{2,1,0:T(8,128)}, f32[...) fusion(f32[4,2,128,512]{3,2,1,0:T(8,128)S(1)} %get-tuple-element.10), kind=kLoop, calls=%fused_computation.174 | loop fusion | bytes 4194304 | tf_op jit(solution)/shard_map/slice | solution.py:25
  14.2 0.0 collective-permute-done.3
  14.2 0.2 copy.44
  14.5 1.0 collective-permute-done.2
  15.5 0.2 copy.43
  15.7 0.6 maximum_convert_fusion
  16.4 0.0 copy-start.10
  16.4 0.0 collective-permute-done.1
  16.4 0.6 copy-done.18
  17.0 2.2 %maximum_convert_fusion.1 = f32[4,2,134,512]{3,2,1,0:T(8,128)S(1)} fusion(bf16[4,2,3,512]{3,2,1,0:T(4,128)(2,1)} %copy-done.18, bf16[4,2,128,512]{3,2,1,0:T(8,128)(2,1)S(1)} %get-tuple-element.11, bf16[4,2,3,512]{3,2,1,0:T(4,128)(2,1)} %collective-permute-done), kind=kLoop, calls=%fused_computation.1 | loop fusion | flops 3293184 | bytes 3293184 | tf_op jit(solution)/shard_map/convert_element_type | solution.py:137
  19.3 1.7 %multiply_add_fusion.4 = (f32[2,128,512]{2,1,0:T(8,128)S(1)}, bf16[2,128,512]{2,1,0:T(8,128)(2,1)}) fusion(f32[4,2,128,512]{3,2,1,0:T(8,128)S(1)} %copy-done.2, f32[4,2,128,518]{3,2,1,0:T(8,128)S(1)} %maximum_convert_fusion, f32[4,2,134,512]{3,2,1,0:T(8,128)S(1)} %maximum_convert_fusion.1, f32[1,128,512]{2,1,0:T(8,128)S(1)} %copy-done.11, ...), kind=kLoop, calls=%fused_computation.162 | loop fusion | flops 5242880 | bytes 9437184 | tf_op jit(solution)/shard_map/add | solution.py:157
  20.9 0.9 fusion.125
  21.9 0.0 copy-done.8
  21.9 0.1 copy-done.9
  22.0 1.6 %multiply_add_fusion.3 = (f32[2,128,512]{2,1,0:T(8,128)S(1)}, bf16[2,128,512]{2,1,0:T(8,128)(2,1)}) fusion(f32[4,2,128,512]{3,2,1,0:T(8,128)S(1)} %copy-done.2, f32[4,2,128,518]{3,2,1,0:T(8,128)S(1)} %maximum_convert_fusion, f32[4,2,134,512]{3,2,1,0:T(8,128)S(1)} %maximum_convert_fusion.1, f32[1,128,512]{2,1,0:T(8,128)S(1)} %copy-done.8, ...), kind=kLoop, calls=%fused_computation.161 | loop fusion | flops 5242880 | bytes 9437184 | tf_op jit(solution)/shard_map/add | solution.py:157
  23.6 0.2 slice_reduce_fusion
  23.8 1.2 %fusion.123 = (f32[2,128,511]{2,1,0:T(8,128)}, f32[2,128,511]{2,1,0:T(8,128)}) fusion(f32[2,128,512]{2,1,0:T(8,128)S(1)} %get-tuple-element.6), kind=kLoop, calls=%fused_computation.198 | loop fusion | bytes 2093056 | tf_op jit(solution)/shard_map/slice | solution.py:168
  25.0 3.4 %collective-permute-start.4 = (f32[2,1,512]{2,1,0:T(1,128)S(1)}, f32[2,1,512]{2,1,0:T(1,128)S(1)}, u32[]{:S(2)}, u32[]{:S(2)}) collective-permute-start(f32[2,1,512]{2,1,0:T(1,128)S(1)} %get-tuple-element.33), channel_id=1, source_target_pairs={{8,0},{16,8},{24,16},{32,24},{40,32},{48,40},{56,48},{64,56},{72,6... | collective-permute-start | bytes 12296 | tf_op jit(solution)/shard_map/ppermute | solution.py:160
  28.4 5.7 %collective-permute-start.6 = (f32[2,1,128]{2,0,1:T(2,128)S(1)}, f32[2,1,128]{2,0,1:T(2,128)S(1)}, u32[]{:S(2)}, u32[]{:S(2)}) collective-permute-start(f32[2,1,128]{2,0,1:T(2,128)S(1)} %bitcast.328), channel_id=1, source_target_pairs={{1,0},{2,1},{3,2},{4,3},{5,4},{6,5},{7,6},{0,7},{9,8},{10,9},{11,1... | collective-permute-start | bytes 3080 | tf_op jit(solution)/shard_map/ppermute | solution.py:164
  34.0 0.0 collective-permute-start.7
  34.1 1.7 %multiply_add_fusion.2 = (f32[2,128,512]{2,1,0:T(8,128)S(1)}, bf16[2,128,512]{2,1,0:T(8,128)(2,1)}) fusion(f32[4,2,128,512]{3,2,1,0:T(8,128)S(1)} %copy-done.2, f32[4,2,128,518]{3,2,1,0:T(8,128)S(1)} %maximum_convert_fusion, f32[4,2,134,512]{3,2,1,0:T(8,128)S(1)} %maximum_convert_fusion.1, f32[1,128,512]{2,1,0:T(8,128)S(1)} %copy-done.6, ...), kind=kLoop, calls=%fused_computation.160 | loop fusion | flops 5505024 | bytes 9961472 | tf_op jit(solution)/shard_map/add | solution.py:157
  35.8 0.8 fusion.122
  36.6 0.8 copy.45
  37.4 2.7 %collective-permute-done.7 = f32[2,1,128]{2,0,1:T(2,128)S(1)} collective-permute-done((f32[2,1,128]{2,0,1:T(2,128)S(1)}, f32[2,1,128]{2,0,1:T(2,128)S(1)}, u32[]{:S(2)}, u32[]{:S(2)}) %collective-permute-start.7) | collective-permute-done | bytes 1056 | tf_op jit(solution)/shard_map/ppermute | solution.py:162
  40.1 0.8 copy.46
  40.9 1.9 %fusion.100 = f32[2,128,512]{2,1,0:T(8,128)S(1)} fusion(f32[2,1,512]{2,1,0:T(1,128)S(1)} %collective-permute-done.4, f32[2,127,512]{2,1,0:T(8,128)} %get-tuple-element.35, f32[2,127,512]{2,1,0:T(8,128)S(1)} %get-tuple-element.34, f32[2,1,512]{2,1,0:T(1,128)S(1)} %collective-permute-done.5, f32[2,128,1]{2,1,0:T(8,128)} %copy.45, ...), kind=kLoop, calls=%fused_computation.140 | loop fusion | flops 1310720 | bytes 3145728 | tf_op jit(solution)/shard_map/mul | solution.py:169
  42.8 0.0 copy-start.15
  42.8 0.3 reshape.154
  43.1 0.0 copy-start.16
  43.2 0.1 copy.47
  43.2 12.5 %all_to_all.10 = f32[8,64,256]{2,1,0:T(8,128)S(1)} all-to-all(f32[8,64,256]{2,1,0:T(8,128)S(1)} %bitcast.319), channel_id=1, replica_groups=mesh['gx'=32,'gy'=8] {'gy'}, dimensions={0} | all-to-all | bytes 1048576 | tf_op jit(solution)/shard_map/all_to_all | solution.py:178
  55.7 1.4 %fusion.108 = f32[32,2,16,256]{3,0,2,1:T(8,128)S(1)} fusion(f32[32,16,1,1]{0,1,3,2:T(8,128)} %constant.67, f32[16,2,16,256]{3,2,1,0:T(8,128)S(1)} %bitcast.317), kind=kOutput, calls=%fused_computation.154 | convolution fusion | flops 25165824 | bytes 1574912 | tf_op jit(solution)/shard_map/dot_general | solution.py:181
  57.2 0.0 copy-start.5
  57.2 0.2 multiply_add_fusion.1
  57.4 0.3 copy.50
  57.7 0.3 copy.49
  58.0 0.4 copy-done.5
  58.4 1.0 fusion
  59.5 1.8 %copy.51 = f32[256,2,512]{2,1,0:T(2,128)} copy(f32[256,2,512]{2,0,1:T(8,128)S(1)} %fusion) | data formatting | bytes 2097152 | tf_op jit(solution)/shard_map/dot_general | solution.py:195
  61.2 10.9 %all-to-all-start.1 = ((f32[256,2,512]{2,1,0:T(2,128)}), f32[256,2,512]{2,1,0:T(2,128)S(1)}, u32[]{:S(2)}, u32[]{:S(2)}) async-start(f32[256,2,512]{2,1,0:T(2,128)} %copy.51), calls=%async_computation.1 | async-start | bytes 2097152 | tf_op jit(solution)/shard_map/all_to_all | solution.py:198
  72.1 1.0 convert_element_type.80
  73.1 4.1 %fusion.111 = bf16[1,2,128,512]{3,2,1,0:T(8,128)(2,1)S(1)} fusion(f32[128,512]{1,0:T(8,128)S(1)} %convert_element_type.80, f32[4,2,128,512]{3,2,1,0:T(8,128)} %copy-done.1, f32[4,2,128,518]{3,2,1,0:T(8,128)} %copy-done, f32[4,2,134,512]{3,2,1,0:T(8,128)S(1)} %maximum_convert_fusion.1, f32[1,128,512]{2,1,0:T(8,128)} %get-tuple-element.13, ...), kind=kLoop, calls=%fused_computation.181 | loop fusion | flops 5242880 | bytes 9699328 | tf_op jit(solution)/shard_map/stack | solution.py:153
  77.2 1.1 %pad_maximum_fusion = bf16[4,2,128,512]{3,2,1,0:T(8,128)(2,1)} fusion(bf16[1,2,128,512]{3,2,1,0:T(8,128)(2,1)S(1)} %fusion.111, bf16[1,2,128,512]{3,2,1,0:T(8,128)(2,1)S(1)} %bitcast.324, bf16[1,2,128,512]{3,2,1,0:T(8,128)(2,1)S(1)} %bitcast.323, bf16[1,2,128,512]{3,2,1,0:T(8,128)(2,1)S(1)} %bitcast.322), kind=kLoop, calls=%fused_computation.2 | loop fusion | flops 1572864 | bytes 2097152 | tf_op jit(solution)/shard_map/stack | solution.py:153
  78.3 24.8 %all-to-all-done.1 = f32[256,2,512]{2,1,0:T(2,128)S(1)} async-done(((f32[256,2,512]{2,1,0:T(2,128)}), f32[256,2,512]{2,1,0:T(2,128)S(1)}, u32[]{:S(2)}, u32[]{:S(2)}) %all-to-all-start.1) | async-done | bytes 1048608 | tf_op jit(solution)/shard_map/all_to_all | solution.py:198
  103.1 0.7 reshape.159
  103.8 0.0 copy-start.17
  103.8 0.3 copy.52
  104.2 0.0 copy-start.19
  104.2 2.2 %fusion.128 = f32[32,16,512]{2,1,0:T(8,128)S(1)} fusion(f32[32,16,512]{2,1,0:T(8,128)S(1)} %bitcast.314, f32[512,512,1]{1,0,2:T(8,128)} %constant.68), kind=kOutput, calls=%fused_computation.203 | convolution fusion | flops 805306368 | bytes 3145728 | tf_op jit(solution)/shard_map/dot_general | solution.py:205
  106.4 0.2 multiply_add_fusion
  106.6 0.6 fusion.3
  107.2 0.7 reshape.173
  107.9 1.6 %copy.55 = f32[2,2,16,4096]{3,2,1,0:T(8,128)} copy(f32[2,2,16,4096]{3,0,1,2:T(2,128)S(1)} %reshape.173) | data formatting | bytes 2097152 | tf_op jit(solution)/shard_map/reshape | solution.py:222
  (43 shorter events, 0.3 us)
Async XLA Ops:
  0.6 8.7 %copy-start.3 = (s32[128,512]{1,0:T(8,128)S(1)}, s32[128,512]{1,0:T(8,128)}, u32[]{:S(2)}) copy-start(s32[128,512]{1,0:T(8,128)} %param.12) | copy-start | bytes 786436
  0.6 8.8 %copy-start.4 = (bf16[4,2,128,512]{3,2,1,0:T(8,128)(2,1)S(1)}, bf16[4,2,128,512]{3,2,1,0:T(8,128)(2,1)}, u32[]{:S(2)}) copy-start(bf16[4,2,128,512]{3,2,1,0:T(8,128)(2,1)} %param.11) | copy-start | bytes 3145732
  3.1 11.1 %collective-permute-start.3 = (bf16[24,128]{1,0:T(8,128)(2,1)S(1)}, bf16[24,128]{1,0:T(8,128)(2,1)S(1)}, u32[]{:S(2)}, u32[]{:S(2)}) collective-permute-start(bf16[24,128]{1,0:T(8,128)(2,1)S(1)} %reshape.152), channel_id=1, source_target_pairs={{1,0},{2,1},{3,2},{4,3},{5,4},{6,5},{7,6},{0,7},{9,8},{10,9},{11,1... | collective-permute-start | bytes 18440 | tf_op jit(solution)/shard_map/ppermute | solution.py:136
  9.3 6.2 %collective-permute-start.2 = (bf16[24,128]{1,0:T(8,128)(2,1)S(1)}, bf16[24,128]{1,0:T(8,128)(2,1)S(1)}, u32[]{:S(2)}, u32[]{:S(2)}) collective-permute-start(bf16[24,128]{1,0:T(8,128)(2,1)S(1)} %reshape.150), channel_id=1, source_target_pairs={{0,1},{1,2},{2,3},{3,4},{4,5},{5,6},{6,7},{7,0},{8,9},{9,10},{10,1... | collective-permute-start | bytes 18440 | tf_op jit(solution)/shard_map/ppermute | solution.py:134
  9.5 6.9 %collective-permute-start.1 = (bf16[4,2,3,512]{3,2,1,0:T(4,128)(2,1)S(1)}, bf16[4,2,3,512]{3,2,1,0:T(4,128)(2,1)S(1)}, u32[]{:S(2)}, u32[]{:S(2)}) collective-permute-start(bf16[4,2,3,512]{3,2,1,0:T(4,128)(2,1)S(1)} %get-tuple-element.25), channel_id=1, source_target_pairs={{8,0},{16,8},{24,16},{32,24},{40,32},{48,40},{56,48},{64,56},{72,6... | collective-permute-start | bytes 73736 | tf_op jit(solution)/shard_map/ppermute | solution.py:125
  10.5 6.5 %collective-permute-start = (bf16[4,2,3,512]{3,2,1,0:T(4,128)(2,1)S(1)}, bf16[4,2,3,512]{3,2,1,0:T(4,128)(2,1)}, u32[]{:S(2)}, u32[]{:S(2)}) collective-permute-start(bf16[4,2,3,512]{3,2,1,0:T(4,128)(2,1)S(1)} %get-tuple-element.24), channel_id=1, source_target_pairs={{0,8},{8,16},{16,24},{24,32},{32,40},{40,48},{48,56},{56,64},{64,7... | collective-permute-start | bytes 73736 | tf_op jit(solution)/shard_map/ppermute | solution.py:124
  11.6 1.3 %copy-start.1 = (f32[4,2,128,512]{3,2,1,0:T(8,128)}, f32[4,2,128,512]{3,2,1,0:T(8,128)S(1)}, u32[]{:S(2)}) copy-start(f32[4,2,128,512]{3,2,1,0:T(8,128)S(1)} %get-tuple-element.10) | copy-start | bytes 6291460
  16.3 17.7 %copy-start = (f32[4,2,128,518]{3,2,1,0:T(8,128)}, f32[4,2,128,518]{3,2,1,0:T(8,128)S(1)}, u32[]{:S(2)}) copy-start(f32[4,2,128,518]{3,2,1,0:T(8,128)S(1)} %maximum_convert_fusion) | copy-start | bytes 6365188
  16.3 2.9 %copy-start.2 = (f32[4,2,128,512]{3,2,1,0:T(8,128)S(1)}, f32[4,2,128,512]{3,2,1,0:T(8,128)}, u32[]{:S(2)}) copy-start(f32[4,2,128,512]{3,2,1,0:T(8,128)} %copy-done.1) | copy-start | bytes 6291460
  16.4 2.9 %copy-start.10 = (f32[1,128,512]{2,1,0:T(8,128)S(1)}, f32[1,128,512]{2,1,0:T(8,128)}, u32[]{:S(2)}) copy-start(f32[1,128,512]{2,1,0:T(8,128)} %get-tuple-element.12) | copy-start | bytes 786436
  16.4 2.9 %copy-start.11 = (f32[1,128,512]{2,1,0:T(8,128)S(1)}, f32[1,128,512]{2,1,0:T(8,128)}, u32[]{:S(2)}) copy-start(f32[1,128,512]{2,1,0:T(8,128)} %get-tuple-element.19) | copy-start | bytes 786436
  16.4 0.6 copy-start.18
  20.9 0.9 copy-start.8
  20.9 1.1 copy-start.9
  23.6 10.4 %copy-start.6 = (f32[1,128,512]{2,1,0:T(8,128)S(1)}, f32[1,128,512]{2,1,0:T(8,128)}, u32[]{:S(2)}) copy-start(f32[1,128,512]{2,1,0:T(8,128)} %get-tuple-element.15) | copy-start | bytes 786436
  23.6 10.4 %copy-start.7 = (f32[1,128,512]{2,1,0:T(8,128)S(1)}, f32[1,128,512]{2,1,0:T(8,128)}, u32[]{:S(2)}) copy-start(f32[1,128,512]{2,1,0:T(8,128)} %get-tuple-element.16) | copy-start | bytes 786436
  25.0 15.9 %collective-permute-start.4 = (f32[2,1,512]{2,1,0:T(1,128)S(1)}, f32[2,1,512]{2,1,0:T(1,128)S(1)}, u32[]{:S(2)}, u32[]{:S(2)}) collective-permute-start(f32[2,1,512]{2,1,0:T(1,128)S(1)} %get-tuple-element.33), channel_id=1, source_target_pairs={{8,0},{16,8},{24,16},{32,24},{40,32},{48,40},{56,48},{64,56},{72,6... | collective-permute-start | bytes 12296 | tf_op jit(solution)/shard_map/ppermute | solution.py:160
  28.4 12.5 %collective-permute-start.5 = (f32[2,1,512]{2,1,0:T(1,128)S(1)}, f32[2,1,512]{2,1,0:T(1,128)S(1)}, u32[]{:S(2)}, u32[]{:S(2)}) collective-permute-start(f32[2,1,512]{2,1,0:T(1,128)S(1)} %get-tuple-element.32), channel_id=1, source_target_pairs={{0,8},{8,16},{16,24},{24,32},{32,40},{40,48},{48,56},{56,64},{64,7... | collective-permute-start | bytes 12296 | tf_op jit(solution)/shard_map/ppermute | solution.py:159
  28.4 8.2 %collective-permute-start.6 = (f32[2,1,128]{2,0,1:T(2,128)S(1)}, f32[2,1,128]{2,0,1:T(2,128)S(1)}, u32[]{:S(2)}, u32[]{:S(2)}) collective-permute-start(f32[2,1,128]{2,0,1:T(2,128)S(1)} %bitcast.328), channel_id=1, source_target_pairs={{1,0},{2,1},{3,2},{4,3},{5,4},{6,5},{7,6},{0,7},{9,8},{10,9},{11,1... | collective-permute-start | bytes 3080 | tf_op jit(solution)/shard_map/ppermute | solution.py:164
  34.0 6.0 %collective-permute-start.7 = (f32[2,1,128]{2,0,1:T(2,128)S(1)}, f32[2,1,128]{2,0,1:T(2,128)S(1)}, u32[]{:S(2)}, u32[]{:S(2)}) collective-permute-start(f32[2,1,128]{2,0,1:T(2,128)S(1)} %bitcast.327), channel_id=1, source_target_pairs={{0,1},{1,2},{2,3},{3,4},{4,5},{5,6},{6,7},{7,0},{8,9},{9,10},{10,1... | collective-permute-start | bytes 3080 | tf_op jit(solution)/shard_map/ppermute | solution.py:162
  42.8 14.4 %copy-start.15 = (f32[16,256]{1,0:T(8,128)S(1)}, f32[16,256]{1,0:T(8,128)}, u32[]{:S(2)}) copy-start(f32[16,256]{1,0:T(8,128)} %constant.43.clone) | copy-start | bytes 49156
  43.1 14.0 %copy-start.16 = (f32[16,256]{1,0:T(8,128)S(1)}, f32[16,256]{1,0:T(8,128)}, u32[]{:S(2)}) copy-start(f32[16,256]{1,0:T(8,128)} %constant.42.clone) | copy-start | bytes 49156
  57.2 1.2 %copy-start.5 = (f32[256,2,512]{2,0,1:T(8,128)S(1)}, f32[256,2,512]{2,0,1:T(8,128)}, u32[]{:S(2)}) copy-start(f32[256,2,512]{2,0,1:T(8,128)} %constant.44.clone) | copy-start | bytes 3145732
  61.2 41.9 %all-to-all-start.1 = ((f32[256,2,512]{2,1,0:T(2,128)}), f32[256,2,512]{2,1,0:T(2,128)S(1)}, u32[]{:S(2)}, u32[]{:S(2)}) async-start(f32[256,2,512]{2,1,0:T(2,128)} %copy.51), calls=%async_computation.1 | async-start | bytes 2097152 | tf_op jit(solution)/shard_map/all_to_all | solution.py:198
  73.1 4.1 %copy-start.12 = (bf16[2,128,512]{2,1,0:T(8,128)(2,1)S(1)}, bf16[2,128,512]{2,1,0:T(8,128)(2,1)}, u32[]{:S(2)}) copy-start(bf16[2,128,512]{2,1,0:T(8,128)(2,1)} %get-tuple-element.9) | copy-start | bytes 786436
  73.1 4.1 %copy-start.13 = (bf16[2,128,512]{2,1,0:T(8,128)(2,1)S(1)}, bf16[2,128,512]{2,1,0:T(8,128)(2,1)}, u32[]{:S(2)}) copy-start(bf16[2,128,512]{2,1,0:T(8,128)(2,1)} %get-tuple-element.7) | copy-start | bytes 786436
  73.1 4.1 %copy-start.14 = (bf16[2,128,512]{2,1,0:T(8,128)(2,1)S(1)}, bf16[2,128,512]{2,1,0:T(8,128)(2,1)}, u32[]{:S(2)}) copy-start(bf16[2,128,512]{2,1,0:T(8,128)(2,1)} %get-tuple-element.5) | copy-start | bytes 786436
  103.8 2.6 %copy-start.17 = (f32[16,256]{1,0:T(8,128)S(1)}, f32[16,256]{1,0:T(8,128)}, u32[]{:S(2)}) copy-start(f32[16,256]{1,0:T(8,128)} %constant.42.clone) | copy-start | bytes 49156
  104.2 2.4 %copy-start.19 = (f32[32,32]{1,0:T(8,128)S(1)}, f32[32,32]{1,0:T(8,128)}, u32[]{:S(2)}) copy-start(f32[32,32]{1,0:T(8,128)} %constant.46.clone) | copy-start | bytes 12292

commit v8 on v7

--- a/solution.py
+++ b/solution.py
@@ -158,10 +158,8 @@
     flow_u, flow_v, flow_w = flows
     u_before = lax.ppermute(flow_u[:, rows_x - 1 :, :], "gx", up_x)
     u_after = lax.ppermute(flow_u[:, :1, :], "gx", down_x)
-    v_before = jnp.swapaxes(
-        lax.ppermute(jnp.swapaxes(flow_v[:, :, rows_y - 1 :], 1, 2), "gy", up_y), 1, 2
-    )
-    v_after = jnp.swapaxes(lax.ppermute(jnp.swapaxes(flow_v[:, :, :1], 1, 2), "gy", down_y), 1, 2)
+    v_before = lax.ppermute(flow_v[:, :, rows_y - 1 :], "gy", up_y)
+    v_after = lax.ppermute(flow_v[:, :, :1], "gy", down_y)
     u_next = jnp.concatenate([flow_u[:, 1:, :], u_after], axis=1)
     u_prev = jnp.concatenate([u_before, flow_u[:, :-1, :]], axis=1)
     v_next = jnp.concatenate([flow_v[:, :, 1:], v_after], axis=2)

time: 110 us -> 110 us (level)
  local copies, waits for them, and re-layouts: 16.6 us -> 12.5 us
  starting transfers between devices: 27.8 us -> 29.7 us
  waiting for transfers between devices: 28.5 us -> 30.3 us
  other arithmetic: 17.8 us -> 19.3 us
    ppermute x2, waiting for transfers between devices: 2.69 us -> 5.66 us  [the longest x1 5.48 us: body(): v_before = lax.ppermute(flow_v[:, :, rows_y - 1:], 'gy', up_y)]
    transpose x2 -> x0, local copies, waits for them, and re-layouts: 1.6 us -> none  [the longest x1 0.81 us: body(): jnp.swapaxes(lax.ppermute(jnp.swapaxes(flow_v[:, :, rows_y - 1:], 1, 2),...]
    mul x1, other arithmetic: 1.89 us -> 0.34 us  [body(): (u_next - u_prev + (v_next - v_prev) + (raised(flow_w) - lowered(flow_w))...]
    convert_element_type x1, other arithmetic: 0.21 us -> 1.44 us  [body(): center = masked.astype(jnp.float32)]
    unnamed x40 -> x38, local copies, waits for them, and re-layouts: 2.56 us -> 2.02 us
  transfers between devices with their start and end apart: 9 -> 9, of which waited for: 3 -> 3; matrix products, arithmetic and copies ran while one was open for 12% -> 13% of each run, Pallas kernels for 0% -> 0%
where the time goes in v8:
time: 110 us
  waiting for transfers between devices  30.3 us (28%)
  starting transfers between devices  29.7 us (27%)
  other arithmetic  19.3 us (18%)
  local copies, waits for them, and re-layouts  12.5 us (11%)
  blocking collectives  11.5 us (10%)
  matrix products  5.26 us (5%)
    all_to_all x1, waiting for transfers between devices, body(): lax.all_to_all(spectrum_y, ('gx', 'gy'), split_axis=0, concat_axis=0, til...  24.6 us
    all_to_all x1, starting transfers between devices, body(): lax.all_to_all(spectrum_y, ('gx', 'gy'), split_axis=0, concat_axis=0, til...  11.7 us
    all_to_all x1, blocking collectives, body(): lax.all_to_all(sent, 'gy', split_axis=0, concat_axis=0, tiled=True)  11.5 us
    ppermute x1, starting transfers between devices, body(): lax.ppermute(lanes_x(masked_part(all_x, slice(0, 3))), 'gy', down_y)  6 us
    ppermute x1, starting transfers between devices, body(): v_after = lax.ppermute(flow_v[:, :, :1], 'gy', down_y)  5.65 us
    ppermute x1, waiting for transfers between devices, body(): v_before = lax.ppermute(flow_v[:, :, rows_y - 1:], 'gy', up_y)  5.48 us
    another operation x2, other arithmetic, body(): tendency = jnp.stack(pieces)  5.2 us
    add x3, other arithmetic, body(): flows.append(center[component] + DT * rounded[component])  5.04 us
  transfers between devices with their start and end apart: 9, of which 3 were waited for; matrix products, arithmetic and copies ran while one was open for 13% of the time, Pallas kernels for 0%

profile of v8, /device:TPU:1, one launch (start us, length us, event | category | flops | bytes accessed | tf_op | source)
XLA Modules:
  0.0 109.5 jit_solution(14639420912970785215)
XLA Ops:
  0.6 1.0 fusion.128
  1.7 1.2 %multiply_bitcast_fusion.1 = (bf16[4,2,3,128]{2,3,1,0:T(8,128)(2,1)S(1)}, bf16[4,2,3,128]{2,3,1,0:T(8,128)(2,1)S(1)}) fusion(bf16[4,2,128,512]{3,2,1,0:T(8,128)(2,1)} %param.11, bf16[2,128,3]{2,1,0:T(8,128)(2,1)S(1)} %get-tuple-element.40, bf16[2,128,3]{2,1,0:T(8,128)(2,1)S(1)} %get-tuple-element.41), kind=kLoop, calls=%fused_computation.180 | loop fusion | flops 6144 | bytes 27648 | tf_op jit(solution)/shard_map/transpose | solution.py:128
  2.9 0.1 copy.36
  3.0 6.0 %collective-permute-start.3 = (bf16[24,128]{1,0:T(8,128)(2,1)S(1)}, bf16[24,128]{1,0:T(8,128)(2,1)S(1)}, u32[]{:S(2)}, u32[]{:S(2)}) collective-permute-start(bf16[24,128]{1,0:T(8,128)(2,1)S(1)} %reshape.152), channel_id=1, source_target_pairs={{1,0},{2,1},{3,2},{4,3},{5,4},{6,5},{7,6},{0,7},{9,8},{10,9},{11,1... | collective-permute-start | bytes 18440 | tf_op jit(solution)/shard_map/ppermute | solution.py:136
  9.0 0.1 copy.35
  9.2 0.1 collective-permute-start.2
  9.3 0.9 slice_multiply_fusion.1
  10.3 1.0 collective-permute-start.1
  11.3 0.8 collective-permute-start
  12.1 1.4 %fusion.121 = (f32[4,2,128,512]{3,2,1,0:T(8,128)S(1)}, bf16[4,2,128,512]{3,2,1,0:T(8,128)(2,1)S(1)}) fusion(bf16[4,2,128,512]{3,2,1,0:T(8,128)(2,1)} %param.11, bf16[2,128,512]{2,1,0:T(8,128)(2,1)S(1)} %convert_convert_fusion), kind=kLoop, calls=%fused_computation.194 | loop fusion | flops 1048576 | bytes 4456448 | tf_op jit(solution)/shard_map/convert_element_type | solution.py:139
  13.6 1.5 %slice_bitcast_fusion.18 = (f32[1,128,512]{2,1,0:T(8,128)}, f32[1,128,512]{2,1,0:T(8,128)}, f32[1,128,512]{2,1,0:T(8,128)}, f32[1,128,512]{2,1,0:T(8,128)}, f32[...) fusion(f32[4,2,128,512]{3,2,1,0:T(8,128)S(1)} %get-tuple-element.8), kind=kLoop, calls=%fused_computation.174 | loop fusion | bytes 4194304 | tf_op jit(solution)/shard_map/slice | solution.py:25
  15.1 0.0 collective-permute-done.3
  15.1 0.9 copy.38
  16.0 0.0 collective-permute-done.2
  16.0 0.2 copy.37
  16.2 1.6 %maximum_convert_fusion = f32[4,2,128,518]{3,2,1,0:T(8,128)S(1)} fusion(bf16[4,2,128,3]{3,2,1,0:T(8,128)(2,1)} %copy.38, bf16[4,2,128,512]{3,2,1,0:T(8,128)(2,1)S(1)} %get-tuple-element.9, bf16[4,2,128,3]{3,2,1,0:T(8,128)(2,1)S(1)} %copy.37), kind=kLoop, calls=%fused_computation | loop fusion | flops 3182592 | bytes 3182592 | tf_op jit(solution)/shard_map/convert_element_type | solution.py:138
  17.8 0.0 copy-start.9
  17.9 0.0 collective-permute-done.1
  17.9 0.0 copy-start.17
  17.9 0.6 copy-done.17
  18.5 2.2 %maximum_convert_fusion.1 = f32[4,2,134,512]{3,2,1,0:T(8,128)S(1)} fusion(bf16[4,2,3,512]{3,2,1,0:T(4,128)(2,1)} %copy-done.17, bf16[4,2,128,512]{3,2,1,0:T(8,128)(2,1)S(1)} %get-tuple-element.9, bf16[4,2,3,512]{3,2,1,0:T(4,128)(2,1)} %collective-permute-done), kind=kLoop, calls=%fused_computation.1 | loop fusion | flops 3293184 | bytes 3293184 | tf_op jit(solution)/shard_map/convert_element_type | solution.py:137
  20.7 1.7 %multiply_add_fusion.4 = (f32[2,128,512]{2,1,0:T(8,128)S(1)}, bf16[2,128,512]{2,1,0:T(8,128)(2,1)}) fusion(f32[4,2,128,512]{3,2,1,0:T(8,128)S(1)} %copy-done.2, f32[4,2,128,518]{3,2,1,0:T(8,128)S(1)} %maximum_convert_fusion, f32[4,2,134,512]{3,2,1,0:T(8,128)S(1)} %maximum_convert_fusion.1, f32[1,128,512]{2,1,0:T(8,128)S(1)} %copy-done.10, ...), kind=kLoop, calls=%fused_computation.162 | loop fusion | flops 5242880 | bytes 9437184 | tf_op jit(solution)/shard_map/add | solution.py:157
  22.4 0.1 fusion.126
  22.5 0.8 copy-done.7
  23.4 0.1 copy-done.8
  23.4 1.6 %multiply_add_fusion.3 = (f32[2,128,512]{2,1,0:T(8,128)S(1)}, bf16[2,128,512]{2,1,0:T(8,128)(2,1)}) fusion(f32[4,2,128,512]{3,2,1,0:T(8,128)S(1)} %copy-done.2, f32[4,2,128,518]{3,2,1,0:T(8,128)S(1)} %maximum_convert_fusion, f32[4,2,134,512]{3,2,1,0:T(8,128)S(1)} %maximum_convert_fusion.1, f32[1,128,512]{2,1,0:T(8,128)S(1)} %copy-done.7, ...), kind=kLoop, calls=%fused_computation.161 | loop fusion | flops 5242880 | bytes 9437184 | tf_op jit(solution)/shard_map/add | solution.py:157
  25.1 0.1 fusion.123
  25.2 0.2 fusion.124
  25.4 4.4 %collective-permute-start.4 = (f32[2,1,512]{2,1,0:T(1,128)S(1)}, f32[2,1,512]{2,1,0:T(1,128)S(1)}, u32[]{:S(2)}, u32[]{:S(2)}) collective-permute-start(f32[2,1,512]{2,1,0:T(1,128)S(1)} %get-tuple-element.33), channel_id=1, source_target_pairs={{8,0},{16,8},{24,16},{32,24},{40,32},{48,40},{56,48},{64,56},{72,6... | collective-permute-start | bytes 12296 | tf_op jit(solution)/shard_map/ppermute | solution.py:160
  29.8 0.0 collective-permute-start.5
  29.8 5.7 %collective-permute-start.6 = (f32[2,128,1]{2,1,0:T(8,128)S(1)}, f32[2,128,1]{2,1,0:T(8,128)S(1)}, u32[]{:S(2)}, u32[]{:S(2)}) collective-permute-start(f32[2,128,1]{2,1,0:T(8,128)S(1)} %get-tuple-element.29), channel_id=1, source_target_pairs={{1,0},{2,1},{3,2},{4,3},{5,4},{6,5},{7,6},{0,7},{9,8},{10,9},{11,1... | collective-permute-start | bytes 3080 | tf_op jit(solution)/shard_map/ppermute | solution.py:162
  35.5 0.0 collective-permute-start.7
  35.5 1.7 %multiply_add_fusion.2 = (f32[2,128,512]{2,1,0:T(8,128)S(1)}, bf16[2,128,512]{2,1,0:T(8,128)(2,1)}) fusion(f32[4,2,128,512]{3,2,1,0:T(8,128)S(1)} %copy-done.2, f32[4,2,128,518]{3,2,1,0:T(8,128)S(1)} %maximum_convert_fusion, f32[4,2,134,512]{3,2,1,0:T(8,128)S(1)} %maximum_convert_fusion.1, f32[1,128,512]{2,1,0:T(8,128)S(1)} %copy-done.5, ...), kind=kLoop, calls=%fused_computation.160 | loop fusion | flops 5505024 | bytes 9961472 | tf_op jit(solution)/shard_map/add | solution.py:157
  37.2 0.2 collective-permute-done.6
  37.4 5.5 %collective-permute-done.7 = f32[2,128,1]{2,1,0:T(8,128)S(1)} collective-permute-done((f32[2,128,1]{2,1,0:T(8,128)S(1)}, f32[2,128,1]{2,1,0:T(8,128)S(1)}, u32[]{:S(2)}, u32[]{:S(2)}) %collective-permute-start.7) | collective-permute-done | bytes 1056 | tf_op jit(solution)/shard_map/ppermute | solution.py:161
  42.9 0.3 fusion.100
  43.3 0.0 copy-start.14
  43.3 0.3 reshape.154
  43.6 0.0 copy-start.15
  43.6 0.1 copy.39
  43.7 11.5 %all_to_all.10 = f32[8,64,256]{2,1,0:T(8,128)S(1)} all-to-all(f32[8,64,256]{2,1,0:T(8,128)S(1)} %bitcast.315), channel_id=1, replica_groups=mesh['gx'=32,'gy'=8] {'gy'}, dimensions={0} | all-to-all | bytes 1048576 | tf_op jit(solution)/shard_map/all_to_all | solution.py:176
  55.2 1.4 %fusion.108 = f32[32,2,16,256]{3,0,2,1:T(8,128)S(1)} fusion(f32[32,16,1,1]{0,1,3,2:T(8,128)} %constant.67, f32[16,2,16,256]{3,2,1,0:T(8,128)S(1)} %bitcast.313), kind=kOutput, calls=%fused_computation.154 | convolution fusion | flops 25165824 | bytes 1574912 | tf_op jit(solution)/shard_map/dot_general | solution.py:179
  56.6 0.0 copy-start.4
  56.6 0.2 multiply_add_fusion.1
  56.8 0.3 copy.42
  57.1 0.3 copy.41
  57.4 0.4 copy-done.4
  57.9 1.0 fusion
  58.9 1.8 %copy.43 = f32[256,2,512]{2,1,0:T(2,128)} copy(f32[256,2,512]{2,0,1:T(8,128)S(1)} %fusion) | data formatting | bytes 2097152 | tf_op jit(solution)/shard_map/dot_general | solution.py:193
  60.7 11.7 %all-to-all-start.1 = ((f32[256,2,512]{2,1,0:T(2,128)}), f32[256,2,512]{2,1,0:T(2,128)S(1)}, u32[]{:S(2)}, u32[]{:S(2)}) async-start(f32[256,2,512]{2,1,0:T(2,128)} %copy.43), calls=%async_computation.1 | async-start | bytes 2097152 | tf_op jit(solution)/shard_map/all_to_all | solution.py:196
  72.4 1.0 convert_element_type.80
  73.4 0.0 copy-start.13
  73.4 4.1 %fusion.111 = bf16[1,2,128,512]{3,2,1,0:T(8,128)(2,1)S(1)} fusion(f32[128,512]{1,0:T(8,128)S(1)} %convert_element_type.80, f32[4,2,128,512]{3,2,1,0:T(8,128)} %copy-done.1, f32[4,2,128,518]{3,2,1,0:T(8,128)} %copy-done, f32[4,2,134,512]{3,2,1,0:T(8,128)S(1)} %maximum_convert_fusion.1, f32[1,128,512]{2,1,0:T(8,128)} %get-tuple-element.11, ...), kind=kLoop, calls=%fused_computation.181 | loop fusion | flops 5242880 | bytes 9699328 | tf_op jit(solution)/shard_map/stack | solution.py:153
  77.5 1.1 %pad_maximum_fusion = bf16[4,2,128,512]{3,2,1,0:T(8,128)(2,1)} fusion(bf16[1,2,128,512]{3,2,1,0:T(8,128)(2,1)S(1)} %fusion.111, bf16[1,2,128,512]{3,2,1,0:T(8,128)(2,1)S(1)} %bitcast.320, bf16[1,2,128,512]{3,2,1,0:T(8,128)(2,1)S(1)} %bitcast.319, bf16[1,2,128,512]{3,2,1,0:T(8,128)(2,1)S(1)} %bitcast.318), kind=kLoop, calls=%fused_computation.2 | loop fusion | flops 1572864 | bytes 2097152 | tf_op jit(solution)/shard_map/stack | solution.py:153
  78.6 24.6 %all-to-all-done.1 = f32[256,2,512]{2,1,0:T(2,128)S(1)} async-done(((f32[256,2,512]{2,1,0:T(2,128)}), f32[256,2,512]{2,1,0:T(2,128)S(1)}, u32[]{:S(2)}, u32[]{:S(2)}) %all-to-all-start.1) | async-done | bytes 1048608 | tf_op jit(solution)/shard_map/all_to_all | solution.py:196
  103.2 0.7 reshape.159
  103.9 0.0 copy-start.16
  103.9 0.3 copy.44
  104.3 0.0 copy-start.18
  104.3 2.2 %fusion.129 = f32[32,16,512]{2,1,0:T(8,128)S(1)} fusion(f32[32,16,512]{2,1,0:T(8,128)S(1)} %bitcast.310, f32[512,512,1]{1,0,2:T(8,128)} %constant.68), kind=kOutput, calls=%fused_computation.202 | convolution fusion | flops 805306368 | bytes 3145728 | tf_op jit(solution)/shard_map/dot_general | solution.py:203
  106.5 0.2 multiply_add_fusion
  106.7 0.6 fusion.3
  107.3 0.7 reshape.173
  108.0 1.6 %copy.47 = f32[2,2,16,4096]{3,2,1,0:T(8,128)} copy(f32[2,2,16,4096]{3,0,1,2:T(2,128)S(1)} %reshape.173) | data formatting | bytes 2097152 | tf_op jit(solution)/shard_map/reshape | solution.py:220
  (39 shorter events, 0.3 us)
Async XLA Ops:
  0.6 8.7 %copy-start.3 = (s32[128,512]{1,0:T(8,128)S(1)}, s32[128,512]{1,0:T(8,128)}, u32[]{:S(2)}) copy-start(s32[128,512]{1,0:T(8,128)} %param.12) | copy-start | bytes 786436
  3.0 12.1 %collective-permute-start.3 = (bf16[24,128]{1,0:T(8,128)(2,1)S(1)}, bf16[24,128]{1,0:T(8,128)(2,1)S(1)}, u32[]{:S(2)}, u32[]{:S(2)}) collective-permute-start(bf16[24,128]{1,0:T(8,128)(2,1)S(1)} %reshape.152), channel_id=1, source_target_pairs={{1,0},{2,1},{3,2},{4,3},{5,4},{6,5},{7,6},{0,7},{9,8},{10,9},{11,1... | collective-permute-start | bytes 18440 | tf_op jit(solution)/shard_map/ppermute | solution.py:136
  9.2 6.8 %collective-permute-start.2 = (bf16[24,128]{1,0:T(8,128)(2,1)S(1)}, bf16[24,128]{1,0:T(8,128)(2,1)S(1)}, u32[]{:S(2)}, u32[]{:S(2)}) collective-permute-start(bf16[24,128]{1,0:T(8,128)(2,1)S(1)} %reshape.150), channel_id=1, source_target_pairs={{0,1},{1,2},{2,3},{3,4},{4,5},{5,6},{6,7},{7,0},{8,9},{9,10},{10,1... | collective-permute-start | bytes 18440 | tf_op jit(solution)/shard_map/ppermute | solution.py:134
  10.3 7.6 %collective-permute-start.1 = (bf16[4,2,3,512]{3,2,1,0:T(4,128)(2,1)S(1)}, bf16[4,2,3,512]{3,2,1,0:T(4,128)(2,1)S(1)}, u32[]{:S(2)}, u32[]{:S(2)}) collective-permute-start(bf16[4,2,3,512]{3,2,1,0:T(4,128)(2,1)S(1)} %get-tuple-element.23), channel_id=1, source_target_pairs={{8,0},{16,8},{24,16},{32,24},{40,32},{48,40},{56,48},{64,56},{72,6... | collective-permute-start | bytes 73736 | tf_op jit(solution)/shard_map/ppermute | solution.py:125
  11.3 7.2 %collective-permute-start = (bf16[4,2,3,512]{3,2,1,0:T(4,128)(2,1)S(1)}, bf16[4,2,3,512]{3,2,1,0:T(4,128)(2,1)}, u32[]{:S(2)}, u32[]{:S(2)}) collective-permute-start(bf16[4,2,3,512]{3,2,1,0:T(4,128)(2,1)S(1)} %get-tuple-element.22), channel_id=1, source_target_pairs={{0,8},{8,16},{16,24},{24,32},{32,40},{40,48},{48,56},{56,64},{64,7... | collective-permute-start | bytes 73736 | tf_op jit(solution)/shard_map/ppermute | solution.py:124
  13.6 2.4 %copy-start.1 = (f32[4,2,128,512]{3,2,1,0:T(8,128)}, f32[4,2,128,512]{3,2,1,0:T(8,128)S(1)}, u32[]{:S(2)}) copy-start(f32[4,2,128,512]{3,2,1,0:T(8,128)S(1)} %get-tuple-element.8) | copy-start | bytes 6291460
  17.8 17.7 %copy-start = (f32[4,2,128,518]{3,2,1,0:T(8,128)}, f32[4,2,128,518]{3,2,1,0:T(8,128)S(1)}, u32[]{:S(2)}) copy-start(f32[4,2,128,518]{3,2,1,0:T(8,128)S(1)} %maximum_convert_fusion) | copy-start | bytes 6365188
  17.8 2.9 %copy-start.2 = (f32[4,2,128,512]{3,2,1,0:T(8,128)S(1)}, f32[4,2,128,512]{3,2,1,0:T(8,128)}, u32[]{:S(2)}) copy-start(f32[4,2,128,512]{3,2,1,0:T(8,128)} %copy-done.1) | copy-start | bytes 6291460
  17.8 2.9 %copy-start.9 = (f32[1,128,512]{2,1,0:T(8,128)S(1)}, f32[1,128,512]{2,1,0:T(8,128)}, u32[]{:S(2)}) copy-start(f32[1,128,512]{2,1,0:T(8,128)} %get-tuple-element.10) | copy-start | bytes 786436
  17.8 2.9 %copy-start.10 = (f32[1,128,512]{2,1,0:T(8,128)S(1)}, f32[1,128,512]{2,1,0:T(8,128)}, u32[]{:S(2)}) copy-start(f32[1,128,512]{2,1,0:T(8,128)} %get-tuple-element.17) | copy-start | bytes 786436
  17.9 0.6 copy-start.17
  22.4 0.9 copy-start.7
  22.4 1.0 copy-start.8
  25.1 10.4 %copy-start.5 = (f32[1,128,512]{2,1,0:T(8,128)S(1)}, f32[1,128,512]{2,1,0:T(8,128)}, u32[]{:S(2)}) copy-start(f32[1,128,512]{2,1,0:T(8,128)} %get-tuple-element.13) | copy-start | bytes 786436
  25.1 10.4 %copy-start.6 = (f32[1,128,512]{2,1,0:T(8,128)S(1)}, f32[1,128,512]{2,1,0:T(8,128)}, u32[]{:S(2)}) copy-start(f32[1,128,512]{2,1,0:T(8,128)} %get-tuple-element.14) | copy-start | bytes 786436
  25.4 17.5 %collective-permute-start.4 = (f32[2,1,512]{2,1,0:T(1,128)S(1)}, f32[2,1,512]{2,1,0:T(1,128)S(1)}, u32[]{:S(2)}, u32[]{:S(2)}) collective-permute-start(f32[2,1,512]{2,1,0:T(1,128)S(1)} %get-tuple-element.33), channel_id=1, source_target_pairs={{8,0},{16,8},{24,16},{32,24},{40,32},{48,40},{56,48},{64,56},{72,6... | collective-permute-start | bytes 12296 | tf_op jit(solution)/shard_map/ppermute | solution.py:160
  29.8 13.1 %collective-permute-start.5 = (f32[2,1,512]{2,1,0:T(1,128)S(1)}, f32[2,1,512]{2,1,0:T(1,128)S(1)}, u32[]{:S(2)}, u32[]{:S(2)}) collective-permute-start(f32[2,1,512]{2,1,0:T(1,128)S(1)} %get-tuple-element.32), channel_id=1, source_target_pairs={{0,8},{8,16},{16,24},{24,32},{32,40},{40,48},{48,56},{56,64},{64,7... | collective-permute-start | bytes 12296 | tf_op jit(solution)/shard_map/ppermute | solution.py:159
  29.8 7.6 %collective-permute-start.6 = (f32[2,128,1]{2,1,0:T(8,128)S(1)}, f32[2,128,1]{2,1,0:T(8,128)S(1)}, u32[]{:S(2)}, u32[]{:S(2)}) collective-permute-start(f32[2,128,1]{2,1,0:T(8,128)S(1)} %get-tuple-element.29), channel_id=1, source_target_pairs={{1,0},{2,1},{3,2},{4,3},{5,4},{6,5},{7,6},{0,7},{9,8},{10,9},{11,1... | collective-permute-start | bytes 3080 | tf_op jit(solution)/shard_map/ppermute | solution.py:162
  35.5 7.4 %collective-permute-start.7 = (f32[2,128,1]{2,1,0:T(8,128)S(1)}, f32[2,128,1]{2,1,0:T(8,128)S(1)}, u32[]{:S(2)}, u32[]{:S(2)}) collective-permute-start(f32[2,128,1]{2,1,0:T(8,128)S(1)} %get-tuple-element.28), channel_id=1, source_target_pairs={{0,1},{1,2},{2,3},{3,4},{4,5},{5,6},{6,7},{7,0},{8,9},{9,10},{10,1... | collective-permute-start | bytes 3080 | tf_op jit(solution)/shard_map/ppermute | solution.py:161
  43.3 13.4 %copy-start.14 = (f32[16,256]{1,0:T(8,128)S(1)}, f32[16,256]{1,0:T(8,128)}, u32[]{:S(2)}) copy-start(f32[16,256]{1,0:T(8,128)} %constant.43.clone) | copy-start | bytes 49156
  43.6 13.0 %copy-start.15 = (f32[16,256]{1,0:T(8,128)S(1)}, f32[16,256]{1,0:T(8,128)}, u32[]{:S(2)}) copy-start(f32[16,256]{1,0:T(8,128)} %constant.42.clone) | copy-start | bytes 49156
  56.6 1.2 %copy-start.4 = (f32[256,2,512]{2,0,1:T(8,128)S(1)}, f32[256,2,512]{2,0,1:T(8,128)}, u32[]{:S(2)}) copy-start(f32[256,2,512]{2,0,1:T(8,128)} %constant.44.clone) | copy-start | bytes 3145732
  60.7 42.5 %all-to-all-start.1 = ((f32[256,2,512]{2,1,0:T(2,128)}), f32[256,2,512]{2,1,0:T(2,128)S(1)}, u32[]{:S(2)}, u32[]{:S(2)}) async-start(f32[256,2,512]{2,1,0:T(2,128)} %copy.43), calls=%async_computation.1 | async-start | bytes 2097152 | tf_op jit(solution)/shard_map/all_to_all | solution.py:196
  73.3 4.1 %copy-start.11 = (bf16[2,128,512]{2,1,0:T(8,128)(2,1)S(1)}, bf16[2,128,512]{2,1,0:T(8,128)(2,1)}, u32[]{:S(2)}) copy-start(bf16[2,128,512]{2,1,0:T(8,128)(2,1)} %get-tuple-element.7) | copy-start | bytes 786436
  73.4 4.1 %copy-start.12 = (bf16[2,128,512]{2,1,0:T(8,128)(2,1)S(1)}, bf16[2,128,512]{2,1,0:T(8,128)(2,1)}, u32[]{:S(2)}) copy-start(bf16[2,128,512]{2,1,0:T(8,128)(2,1)} %get-tuple-element.5) | copy-start | bytes 786436
  73.4 4.1 %copy-start.13 = (bf16[2,128,512]{2,1,0:T(8,128)(2,1)S(1)}, bf16[2,128,512]{2,1,0:T(8,128)(2,1)}, u32[]{:S(2)}) copy-start(bf16[2,128,512]{2,1,0:T(8,128)(2,1)} %get-tuple-element.3) | copy-start | bytes 786436
  103.9 2.6 %copy-start.16 = (f32[16,256]{1,0:T(8,128)S(1)}, f32[16,256]{1,0:T(8,128)}, u32[]{:S(2)}) copy-start(f32[16,256]{1,0:T(8,128)} %constant.42.clone) | copy-start | bytes 49156
  104.3 2.4 %copy-start.18 = (f32[32,32]{1,0:T(8,128)S(1)}, f32[32,32]{1,0:T(8,128)}, u32[]{:S(2)}) copy-start(f32[32,32]{1,0:T(8,128)} %constant.46.clone) | copy-start | bytes 12292

commit v9 on v8

--- a/solution.py
+++ b/solution.py
@@ -123,17 +123,8 @@
     all_x, all_y = slice(0, rows_x), slice(0, rows_y)
     x_before = lax.ppermute(masked_part(slice(rows_x - 3, rows_x), all_y), "gx", up_x)
     x_after = lax.ppermute(masked_part(slice(0, 3), all_y), "gx", down_x)
-
-    def lanes_x(part):
-        return jnp.swapaxes(part, 2, 3).reshape(-1, rows_x)
-
-    def from_lanes_x(flat):
-        return jnp.swapaxes(flat.reshape(state.shape[0], levels, 3, rows_x), 2, 3)
-
-    y_before = from_lanes_x(
-        lax.ppermute(lanes_x(masked_part(all_x, slice(rows_y - 3, rows_y))), "gy", up_y)
-    )
-    y_after = from_lanes_x(lax.ppermute(lanes_x(masked_part(all_x, slice(0, 3))), "gy", down_y))
+    y_before = lax.ppermute(masked_part(all_x, slice(rows_y - 3, rows_y)), "gy", up_y)
+    y_after = lax.ppermute(masked_part(all_x, slice(0, 3)), "gy", down_y)
     pad_x = jnp.concatenate([x_before, masked, x_after], axis=2).astype(jnp.float32)
     pad_y = jnp.concatenate([y_before, masked, y_after], axis=3).astype(jnp.float32)
     center = masked.astype(jnp.float32)
@@ -201,7 +192,7 @@
     scale = 1.0 / math.sqrt(total_x * total_y)
     wa, t2c, t2s, wb = x_tables(n_s, n_i, scale)
     stage_a = lax.dot_general(
-        moved.reshape(2 * n_s, rows_m), const(wa), (((0,), (0,)), ((), ())), precision=PREC
+        moved, const(wa.reshape(n_s, 2, 2 * n_s)), (((0, 1), (0, 1)), ((), ())), precision=PREC
     )
     batch = levels * n_p
     stage_a = stage_a.reshape(batch, n_i, 2 * n_s)

time: 110 us -> 104 us (0.945)
  waiting for transfers between devices: 30.3 us -> 34.9 us
  starting transfers between devices: 29.7 us -> 25.4 us
  other arithmetic: 19.3 us -> 16.4 us
  local copies, waits for them, and re-layouts: 12.5 us -> 9.75 us
  matrix products: 5.26 us -> 4.13 us
    ppermute x2, waiting for transfers between devices: 0.01 us -> 4.86 us  [the longest x1 4.85 us: body(): lax.ppermute(masked_part(all_x, slice(rows_y - 3, rows_y)), 'gy', up_y)]
    ppermute x1, starting transfers between devices: 4.42 us -> 1.94 us  [body(): u_after = lax.ppermute(flow_u[:, :1, :], 'gx', down_x)]
    convert_element_type x1, other arithmetic: 2.2 us -> 0.35 us  [body(): jnp.concatenate([x_before, masked, x_after], axis=2).astype(jnp.float32)]
    transpose x4 -> x0, local copies, waits for them, and re-layouts: 1.39 us -> none  [the longest x2 1.1 us: from_lanes_x(): return jnp.swapaxes(flat.reshape(state.shape[0], levels, 3, rows_x), 2, 3)]
    convert_element_type x1, other arithmetic: 1.44 us -> 0.21 us  [body(): center = masked.astype(jnp.float32)]
    transpose x1 -> x0, other arithmetic: 1.18 us -> none  [lanes_x(): return jnp.swapaxes(part, 2, 3).reshape(-1, rows_x)]
    mul x1 -> x2, other arithmetic: 0.92 us -> 2.1 us  [masked_part(): return state[:, :, xs, ys] * wet[None]]
    dot_general x1, matrix products: 2.23 us -> 1.11 us  [body(): lax.dot_general(moved, const(wa.reshape(n_s, 2, 2 * n_s)), (((0, 1), (0,...]
  transfers between devices with their start and end apart: 9 -> 9, of which waited for: 3 -> 4; matrix products, arithmetic and copies ran while one was open for 13% -> 12% of each run, Pallas kernels for 0% -> 0%
where the time goes in v9:
time: 104 us; the launch traced here: 103 us
  waiting for transfers between devices  34.9 us (34%)
  starting transfers between devices  25.4 us (24%)
  other arithmetic  16.4 us (16%)
  blocking collectives  11.7 us (11%)
  local copies, waits for them, and re-layouts  9.75 us (9%)
  matrix products  4.13 us (4%)
    all_to_all x1, waiting for transfers between devices, body(): lax.all_to_all(spectrum_y, ('gx', 'gy'), split_axis=0, concat_axis=0, til...  24.4 us
    all_to_all x1, blocking collectives, body(): lax.all_to_all(sent, 'gy', split_axis=0, concat_axis=0, tiled=True)  11.7 us
    all_to_all x1, starting transfers between devices, body(): lax.all_to_all(spectrum_y, ('gx', 'gy'), split_axis=0, concat_axis=0, til...  10.8 us
    ppermute x1, starting transfers between devices, body(): y_after = lax.ppermute(masked_part(all_x, slice(0, 3)), 'gy', down_y)  6 us
    ppermute x1, waiting for transfers between devices, body(): v_before = lax.ppermute(flow_v[:, :, rows_y - 1:], 'gy', up_y)  5.48 us
    another operation x2, other arithmetic, body(): tendency = jnp.stack(pieces)  5.4 us
    add x3, other arithmetic, body(): flows.append(center[component] + DT * rounded[component])  5.01 us
    ppermute x1, waiting for transfers between devices, body(): lax.ppermute(masked_part(all_x, slice(rows_y - 3, rows_y)), 'gy', up_y)  4.85 us
  transfers between devices with their start and end apart: 9, of which 4 were waited for; matrix products, arithmetic and copies ran while one was open for 12% of the time, Pallas kernels for 0%

profile of v9, /device:TPU:1, one launch (start us, length us, event | category | flops | bytes accessed | tf_op | source)
XLA Modules:
  0.0 103.3 jit_solution(16703461964713125702)
XLA Ops:
  0.6 0.0 copy-start.3
  0.6 1.0 %fusion.130 = (s32[128,3]{1,0:T(8,128)S(1)}, s32[128,3]{1,0:T(8,128)S(1)}) fusion(s32[128,512]{1,0:T(8,128)} %param.12), kind=kLoop, calls=%fused_computation.203 | loop fusion | bytes 6144 | tf_op jit(solution)/shard_map/slice | solution.py:120
  1.7 1.2 %slice_multiply_fusion.1 = (bf16[4,2,128,3]{3,2,1,0:T(8,128)(2,1)S(1)}, bf16[4,2,128,3]{3,2,1,0:T(8,128)(2,1)S(1)}) fusion(bf16[4,2,128,512]{3,2,1,0:T(8,128)(2,1)} %param.11, bf16[2,128,3]{2,1,0:T(8,128)(2,1)S(1)} %get-tuple-element.40, bf16[2,128,3]{2,1,0:T(8,128)(2,1)S(1)} %get-tuple-element.41), kind=kLoop, calls=%fused_computation.182 | loop fusion | flops 6144 | bytes 27648 | tf_op jit(solution)/shard_map/mul | solution.py:121
  2.9 6.0 %collective-permute-start.3 = (bf16[4,2,128,3]{3,2,1,0:T(8,128)(2,1)S(1)}, bf16[4,2,128,3]{3,2,1,0:T(8,128)(2,1)S(1)}, u32[]{:S(2)}, u32[]{:S(2)}) collective-permute-start(bf16[4,2,128,3]{3,2,1,0:T(8,128)(2,1)S(1)} %get-tuple-element.25), channel_id=1, source_target_pairs={{1,0},{2,1},{3,2},{4,3},{5,4},{6,5},{7,6},{0,7},{9,8},{10,9},{11,1... | collective-permute-start | bytes 18440 | tf_op jit(solution)/shard_map/ppermute | solution.py:127
  8.9 0.0 collective-permute-start.2
  8.9 0.7 fusion.129
  9.7 0.9 slice_multiply_fusion.3
  10.6 1.0 %collective-permute-start.1 = (bf16[4,2,3,512]{3,2,1,0:T(4,128)(2,1)S(1)}, bf16[4,2,3,512]{3,2,1,0:T(4,128)(2,1)S(1)}, u32[]{:S(2)}, u32[]{:S(2)}) collective-permute-start(bf16[4,2,3,512]{3,2,1,0:T(4,128)(2,1)S(1)} %get-tuple-element.23), channel_id=1, source_target_pairs={{8,0},{16,8},{24,16},{32,24},{40,32},{48,40},{56,48},{64,56},{72,6... | collective-permute-start | bytes 73736 | tf_op jit(solution)/shard_map/ppermute | solution.py:125
  11.6 0.8 collective-permute-start
  12.4 1.0 convert_convert_fusion
  13.4 0.0 copy-done.3
  13.4 0.2 fusion.123
  13.7 1.2 %slice_bitcast_fusion.18 = (f32[1,128,512]{2,1,0:T(8,128)S(1)}, f32[1,128,512]{2,1,0:T(8,128)}, f32[1,128,512]{2,1,0:T(8,128)}, f32[1,128,512]{2,1,0:T(8,128)S(1...) fusion(f32[4,2,128,512]{3,2,1,0:T(8,128)S(1)} %get-tuple-element.8), kind=kLoop, calls=%fused_computation.176 | loop fusion | bytes 4194304 | tf_op jit(solution)/shard_map/slice | solution.py:25
  14.9 0.0 collective-permute-done.3
  14.9 4.9 %collective-permute-done.2 = bf16[4,2,128,3]{3,2,1,0:T(8,128)(2,1)S(1)} collective-permute-done((bf16[4,2,128,3]{3,2,1,0:T(8,128)(2,1)S(1)}, bf16[4,2,128,3]{3,2,1,0:T(8,128)(2,1)S(1)}, u32[]{:S(2)}, u32[]{:S(2)}) %collective-permute-start.2) | collective-permute-done | bytes 6176 | tf_op jit(solution)/shard_map/ppermute | solution.py:126
  19.7 0.7 maximum_convert_fusion
  20.4 0.0 copy-start.2
  20.4 0.0 collective-permute-done.1
  20.4 0.0 collective-permute-done
  20.4 0.3 maximum_convert_fusion.1
  20.8 0.8 copy-done.2
  21.6 1.7 %multiply_add_fusion.4 = (f32[2,128,512]{2,1,0:T(8,128)S(1)}, bf16[2,128,512]{2,1,0:T(8,128)(2,1)}) fusion(f32[4,2,128,512]{3,2,1,0:T(8,128)S(1)} %get-tuple-element.8, f32[4,2,128,518]{3,2,1,0:T(8,128)S(1)} %maximum_convert_fusion, f32[4,2,134,512]{3,2,1,0:T(8,128)S(1)} %maximum_convert_fusion.1, f32[1,128,512]{2,1,0:T(8,128)S(1)} %get-tuple-element.17, ...), kind=kLoop, calls=%fused_computation.164 | loop fusion | flops 5242880 | bytes 9437184 | tf_op jit(solution)/shard_map/add | solution.py:148
  23.2 0.1 fusion.128
  23.3 1.6 %multiply_add_fusion.3 = (f32[2,128,512]{2,1,0:T(8,128)S(1)}, bf16[2,128,512]{2,1,0:T(8,128)(2,1)}) fusion(f32[4,2,128,512]{3,2,1,0:T(8,128)S(1)} %get-tuple-element.8, f32[4,2,128,518]{3,2,1,0:T(8,128)S(1)} %maximum_convert_fusion, f32[4,2,134,512]{3,2,1,0:T(8,128)S(1)} %maximum_convert_fusion.1, f32[1,128,512]{2,1,0:T(8,128)S(1)} %get-tuple-element.15, ...), kind=kLoop, calls=%fused_computation.163 | loop fusion | flops 5242880 | bytes 9437184 | tf_op jit(solution)/shard_map/add | solution.py:148
  25.0 0.1 fusion.125
  25.1 0.2 fusion.126
  25.3 1.9 %collective-permute-start.4 = (f32[2,1,512]{2,1,0:T(1,128)S(1)}, f32[2,1,512]{2,1,0:T(1,128)S(1)}, u32[]{:S(2)}, u32[]{:S(2)}) collective-permute-start(f32[2,1,512]{2,1,0:T(1,128)S(1)} %get-tuple-element.33), channel_id=1, source_target_pairs={{8,0},{16,8},{24,16},{32,24},{40,32},{48,40},{56,48},{64,56},{72,6... | collective-permute-start | bytes 12296 | tf_op jit(solution)/shard_map/ppermute | solution.py:151
  27.2 0.0 collective-permute-start.5
  27.2 4.8 %collective-permute-start.6 = (f32[2,128,1]{2,1,0:T(8,128)S(1)}, f32[2,128,1]{2,1,0:T(8,128)S(1)}, u32[]{:S(2)}, u32[]{:S(2)}) collective-permute-start(f32[2,128,1]{2,1,0:T(8,128)S(1)} %get-tuple-element.29), channel_id=1, source_target_pairs={{1,0},{2,1},{3,2},{4,3},{5,4},{6,5},{7,6},{0,7},{9,8},{10,9},{11,1... | collective-permute-start | bytes 3080 | tf_op jit(solution)/shard_map/ppermute | solution.py:153
  32.1 0.0 collective-permute-start.7
  32.1 1.7 %multiply_add_fusion.2 = (f32[2,128,512]{2,1,0:T(8,128)S(1)}, bf16[2,128,512]{2,1,0:T(8,128)(2,1)}) fusion(f32[4,2,128,512]{3,2,1,0:T(8,128)S(1)} %get-tuple-element.8, f32[4,2,128,518]{3,2,1,0:T(8,128)S(1)} %maximum_convert_fusion, f32[4,2,134,512]{3,2,1,0:T(8,128)S(1)} %maximum_convert_fusion.1, f32[1,128,512]{2,1,0:T(8,128)S(1)} %get-tuple-element.13, ...), kind=kLoop, calls=%fused_computation.162 | loop fusion | flops 5505024 | bytes 9961472 | tf_op jit(solution)/shard_map/add | solution.py:148
  33.8 0.2 collective-permute-done.6
  34.0 5.5 %collective-permute-done.7 = f32[2,128,1]{2,1,0:T(8,128)S(1)} collective-permute-done((f32[2,128,1]{2,1,0:T(8,128)S(1)}, f32[2,128,1]{2,1,0:T(8,128)S(1)}, u32[]{:S(2)}, u32[]{:S(2)}) %collective-permute-start.7) | collective-permute-done | bytes 1056 | tf_op jit(solution)/shard_map/ppermute | solution.py:152
  39.5 0.0 collective-permute-done.4
  39.5 0.0 collective-permute-done.5
  39.5 0.3 fusion.102
  39.8 0.0 copy-start.9
  39.9 0.3 reshape.136
  40.2 0.0 copy-start.10
  40.2 0.1 copy.24
  40.3 11.7 %all_to_all.10 = f32[8,64,256]{2,1,0:T(8,128)S(1)} all-to-all(f32[8,64,256]{2,1,0:T(8,128)S(1)} %bitcast.307), channel_id=1, replica_groups=mesh['gx'=32,'gy'=8] {'gy'}, dimensions={0} | all-to-all | bytes 1048576 | tf_op jit(solution)/shard_map/all_to_all | solution.py:167
  52.0 1.4 %fusion.110 = f32[32,2,16,256]{3,0,2,1:T(8,128)S(1)} fusion(f32[32,16,1,1]{0,1,3,2:T(8,128)} %constant.67, f32[16,2,16,256]{3,2,1,0:T(8,128)S(1)} %bitcast.305), kind=kOutput, calls=%fused_computation.156 | convolution fusion | flops 25165824 | bytes 1574912 | tf_op jit(solution)/shard_map/dot_general | solution.py:170
  53.4 0.0 copy-start.5
  53.4 0.2 multiply_add_fusion.1
  53.6 0.3 copy.27
  53.9 0.3 copy.26
  54.2 0.4 copy-done.5
  54.7 1.0 fusion
  55.7 1.8 %copy.28 = f32[256,2,512]{2,1,0:T(2,128)} copy(f32[256,2,512]{2,0,1:T(8,128)S(1)} %fusion) | data formatting | bytes 2097152 | tf_op jit(solution)/shard_map/dot_general | solution.py:184
  57.5 10.8 %all-to-all-start.1 = ((f32[256,2,512]{2,1,0:T(2,128)}), f32[256,2,512]{2,1,0:T(2,128)S(1)}, u32[]{:S(2)}, u32[]{:S(2)}) async-start(f32[256,2,512]{2,1,0:T(2,128)} %copy.28), calls=%async_computation.1 | async-start | bytes 2097152 | tf_op jit(solution)/shard_map/all_to_all | solution.py:187
  68.3 1.0 convert_element_type.80
  69.3 4.3 %fusion.113 = bf16[1,2,128,512]{3,2,1,0:T(8,128)(2,1)S(1)} fusion(f32[128,512]{1,0:T(8,128)S(1)} %convert_element_type.80, f32[4,2,128,512]{3,2,1,0:T(8,128)} %copy-done.1, f32[4,2,128,518]{3,2,1,0:T(8,128)} %copy-done, f32[4,2,134,512]{3,2,1,0:T(8,128)S(1)} %maximum_convert_fusion.1, f32[1,128,512]{2,1,0:T(8,128)} %get-tuple-element.11, ...), kind=kLoop, calls=%fused_computation.183 | loop fusion | flops 5242880 | bytes 9699328 | tf_op jit(solution)/shard_map/stack | solution.py:144
  73.6 0.0 copy-start.4
  73.6 0.0 copy-done.6
  73.6 0.0 copy-done.7
  73.6 0.0 copy-done.8
  73.6 0.0 copy-start.11
  73.7 1.1 %pad_maximum_fusion = bf16[4,2,128,512]{3,2,1,0:T(8,128)(2,1)} fusion(bf16[1,2,128,512]{3,2,1,0:T(8,128)(2,1)S(1)} %fusion.113, bf16[1,2,128,512]{3,2,1,0:T(8,128)(2,1)S(1)} %bitcast.312, bf16[1,2,128,512]{3,2,1,0:T(8,128)(2,1)S(1)} %bitcast.311, bf16[1,2,128,512]{3,2,1,0:T(8,128)(2,1)S(1)} %bitcast.310), kind=kLoop, calls=%fused_computation.2 | loop fusion | flops 1572864 | bytes 2097152 | tf_op jit(solution)/shard_map/stack | solution.py:144
  74.8 24.4 %all-to-all-done.1 = f32[256,2,512]{2,1,0:T(2,128)S(1)} async-done(((f32[256,2,512]{2,1,0:T(2,128)}), f32[256,2,512]{2,1,0:T(2,128)S(1)}, u32[]{:S(2)}, u32[]{:S(2)}) %all-to-all-start.1) | async-done | bytes 1048608 | tf_op jit(solution)/shard_map/all_to_all | solution.py:187
  99.1 1.1 %fusion.7 = f32[512,512,1]{1,0,2:T(8,128)S(1)} fusion(f32[256,2,512]{2,0,1:T(8,128)S(1)} %copy-done.4, f32[256,2,512]{2,1,0:T(2,128)S(1)} %all-to-all-done.1), kind=kOutput, calls=%fused_computation.11 | convolution fusion | flops 805306368 | bytes 3145728 | tf_op jit(solution)/shard_map/dot_general | solution.py:194
  100.2 0.2 multiply_add_fusion
  100.4 0.6 fusion.3
  101.0 0.7 reshape.155
  101.7 1.6 %copy.32 = f32[2,2,16,4096]{3,2,1,0:T(8,128)} copy(f32[2,2,16,4096]{3,0,1,2:T(2,128)S(1)} %reshape.155) | data formatting | bytes 2097152 | tf_op jit(solution)/shard_map/reshape | solution.py:211
  (17 shorter events, 0.1 us)
Async XLA Ops:
  0.6 12.8 %copy-start.3 = (bf16[4,2,128,512]{3,2,1,0:T(8,128)(2,1)S(1)}, bf16[4,2,128,512]{3,2,1,0:T(8,128)(2,1)}, u32[]{:S(2)}) copy-start(bf16[4,2,128,512]{3,2,1,0:T(8,128)(2,1)} %param.11) | copy-start | bytes 3145732
  2.9 12.0 %collective-permute-start.3 = (bf16[4,2,128,3]{3,2,1,0:T(8,128)(2,1)S(1)}, bf16[4,2,128,3]{3,2,1,0:T(8,128)(2,1)S(1)}, u32[]{:S(2)}, u32[]{:S(2)}) collective-permute-start(bf16[4,2,128,3]{3,2,1,0:T(8,128)(2,1)S(1)} %get-tuple-element.25), channel_id=1, source_target_pairs={{1,0},{2,1},{3,2},{4,3},{5,4},{6,5},{7,6},{0,7},{9,8},{10,9},{11,1... | collective-permute-start | bytes 18440 | tf_op jit(solution)/shard_map/ppermute | solution.py:127
  8.9 10.8 %collective-permute-start.2 = (bf16[4,2,128,3]{3,2,1,0:T(8,128)(2,1)S(1)}, bf16[4,2,128,3]{3,2,1,0:T(8,128)(2,1)S(1)}, u32[]{:S(2)}, u32[]{:S(2)}) collective-permute-start(bf16[4,2,128,3]{3,2,1,0:T(8,128)(2,1)S(1)} %get-tuple-element.24), channel_id=1, source_target_pairs={{0,1},{1,2},{2,3},{3,4},{4,5},{5,6},{6,7},{7,0},{8,9},{9,10},{10,1... | collective-permute-start | bytes 18440 | tf_op jit(solution)/shard_map/ppermute | solution.py:126
  10.6 9.8 %collective-permute-start.1 = (bf16[4,2,3,512]{3,2,1,0:T(4,128)(2,1)S(1)}, bf16[4,2,3,512]{3,2,1,0:T(4,128)(2,1)S(1)}, u32[]{:S(2)}, u32[]{:S(2)}) collective-permute-start(bf16[4,2,3,512]{3,2,1,0:T(4,128)(2,1)S(1)} %get-tuple-element.23), channel_id=1, source_target_pairs={{8,0},{16,8},{24,16},{32,24},{40,32},{48,40},{56,48},{64,56},{72,6... | collective-permute-start | bytes 73736 | tf_op jit(solution)/shard_map/ppermute | solution.py:125
  11.6 8.8 %collective-permute-start = (bf16[4,2,3,512]{3,2,1,0:T(4,128)(2,1)S(1)}, bf16[4,2,3,512]{3,2,1,0:T(4,128)(2,1)S(1)}, u32[]{:S(2)}, u32[]{:S(2)}) collective-permute-start(bf16[4,2,3,512]{3,2,1,0:T(4,128)(2,1)S(1)} %get-tuple-element.22), channel_id=1, source_target_pairs={{0,8},{8,16},{16,24},{24,32},{32,40},{40,48},{48,56},{56,64},{64,7... | collective-permute-start | bytes 73736 | tf_op jit(solution)/shard_map/ppermute | solution.py:124
  13.6 18.4 %copy-start.1 = (f32[4,2,128,512]{3,2,1,0:T(8,128)}, f32[4,2,128,512]{3,2,1,0:T(8,128)S(1)}, u32[]{:S(2)}) copy-start(f32[4,2,128,512]{3,2,1,0:T(8,128)S(1)} %get-tuple-element.8) | copy-start | bytes 6291460
  20.4 11.7 %copy-start = (f32[4,2,128,518]{3,2,1,0:T(8,128)}, f32[4,2,128,518]{3,2,1,0:T(8,128)S(1)}, u32[]{:S(2)}) copy-start(f32[4,2,128,518]{3,2,1,0:T(8,128)S(1)} %maximum_convert_fusion) | copy-start | bytes 6365188
  20.4 1.1 %copy-start.2 = (s32[128,512]{1,0:T(8,128)S(1)}, s32[128,512]{1,0:T(8,128)}, u32[]{:S(2)}) copy-start(s32[128,512]{1,0:T(8,128)} %param.12) | copy-start | bytes 786436
  25.3 14.2 %collective-permute-start.4 = (f32[2,1,512]{2,1,0:T(1,128)S(1)}, f32[2,1,512]{2,1,0:T(1,128)S(1)}, u32[]{:S(2)}, u32[]{:S(2)}) collective-permute-start(f32[2,1,512]{2,1,0:T(1,128)S(1)} %get-tuple-element.33), channel_id=1, source_target_pairs={{8,0},{16,8},{24,16},{32,24},{40,32},{48,40},{56,48},{64,56},{72,6... | collective-permute-start | bytes 12296 | tf_op jit(solution)/shard_map/ppermute | solution.py:151
  27.2 12.3 %collective-permute-start.5 = (f32[2,1,512]{2,1,0:T(1,128)S(1)}, f32[2,1,512]{2,1,0:T(1,128)S(1)}, u32[]{:S(2)}, u32[]{:S(2)}) collective-permute-start(f32[2,1,512]{2,1,0:T(1,128)S(1)} %get-tuple-element.32), channel_id=1, source_target_pairs={{0,8},{8,16},{16,24},{24,32},{32,40},{40,48},{48,56},{56,64},{64,7... | collective-permute-start | bytes 12296 | tf_op jit(solution)/shard_map/ppermute | solution.py:150
  27.2 6.8 %collective-permute-start.6 = (f32[2,128,1]{2,1,0:T(8,128)S(1)}, f32[2,128,1]{2,1,0:T(8,128)S(1)}, u32[]{:S(2)}, u32[]{:S(2)}) collective-permute-start(f32[2,128,1]{2,1,0:T(8,128)S(1)} %get-tuple-element.29), channel_id=1, source_target_pairs={{1,0},{2,1},{3,2},{4,3},{5,4},{6,5},{7,6},{0,7},{9,8},{10,9},{11,1... | collective-permute-start | bytes 3080 | tf_op jit(solution)/shard_map/ppermute | solution.py:153
  32.1 7.4 %collective-permute-start.7 = (f32[2,128,1]{2,1,0:T(8,128)S(1)}, f32[2,128,1]{2,1,0:T(8,128)S(1)}, u32[]{:S(2)}, u32[]{:S(2)}) collective-permute-start(f32[2,128,1]{2,1,0:T(8,128)S(1)} %get-tuple-element.28), channel_id=1, source_target_pairs={{0,1},{1,2},{2,3},{3,4},{4,5},{5,6},{6,7},{7,0},{8,9},{9,10},{10,1... | collective-permute-start | bytes 3080 | tf_op jit(solution)/shard_map/ppermute | solution.py:152
  39.8 13.6 %copy-start.9 = (f32[16,256]{1,0:T(8,128)S(1)}, f32[16,256]{1,0:T(8,128)}, u32[]{:S(2)}) copy-start(f32[16,256]{1,0:T(8,128)} %constant.43.clone) | copy-start | bytes 49156
  40.2 13.2 %copy-start.10 = (f32[16,256]{1,0:T(8,128)S(1)}, f32[16,256]{1,0:T(8,128)}, u32[]{:S(2)}) copy-start(f32[16,256]{1,0:T(8,128)} %constant.42.clone) | copy-start | bytes 49156
  53.4 1.2 %copy-start.5 = (f32[256,2,512]{2,0,1:T(8,128)S(1)}, f32[256,2,512]{2,0,1:T(8,128)}, u32[]{:S(2)}) copy-start(f32[256,2,512]{2,0,1:T(8,128)} %constant.44.clone) | copy-start | bytes 3145732
  57.5 41.6 %all-to-all-start.1 = ((f32[256,2,512]{2,1,0:T(2,128)}), f32[256,2,512]{2,1,0:T(2,128)S(1)}, u32[]{:S(2)}, u32[]{:S(2)}) async-start(f32[256,2,512]{2,1,0:T(2,128)} %copy.28), calls=%async_computation.1 | async-start | bytes 2097152 | tf_op jit(solution)/shard_map/all_to_all | solution.py:187
  69.3 4.3 %copy-start.6 = (bf16[2,128,512]{2,1,0:T(8,128)(2,1)S(1)}, bf16[2,128,512]{2,1,0:T(8,128)(2,1)}, u32[]{:S(2)}) copy-start(bf16[2,128,512]{2,1,0:T(8,128)(2,1)} %get-tuple-element.7) | copy-start | bytes 786436
  69.3 4.3 %copy-start.7 = (bf16[2,128,512]{2,1,0:T(8,128)(2,1)S(1)}, bf16[2,128,512]{2,1,0:T(8,128)(2,1)}, u32[]{:S(2)}) copy-start(bf16[2,128,512]{2,1,0:T(8,128)(2,1)} %get-tuple-element.5) | copy-start | bytes 786436
  69.3 4.3 %copy-start.8 = (bf16[2,128,512]{2,1,0:T(8,128)(2,1)S(1)}, bf16[2,128,512]{2,1,0:T(8,128)(2,1)}, u32[]{:S(2)}) copy-start(bf16[2,128,512]{2,1,0:T(8,128)(2,1)} %get-tuple-element.3) | copy-start | bytes 786436
  73.6 25.5 %copy-start.4 = (f32[256,2,512]{2,0,1:T(8,128)S(1)}, f32[256,2,512]{2,0,1:T(8,128)}, u32[]{:S(2)}) copy-start(f32[256,2,512]{2,0,1:T(8,128)} %constant.45.clone) | copy-start | bytes 3145732
  73.6 26.6 %copy-start.11 = (f32[16,256]{1,0:T(8,128)S(1)}, f32[16,256]{1,0:T(8,128)}, u32[]{:S(2)}) copy-start(f32[16,256]{1,0:T(8,128)} %constant.42.clone) | copy-start | bytes 49156
  74.8 25.7 %copy-start.12 = (f32[32,32]{1,0:T(8,128)S(1)}, f32[32,32]{1,0:T(8,128)}, u32[]{:S(2)}) copy-start(f32[32,32]{1,0:T(8,128)} %constant.46.clone) | copy-start | bytes 12292

commit v10 on v9

--- a/solution.py
+++ b/solution.py
@@ -165,15 +165,15 @@
     sent = diverge.reshape(levels, count_y, piece_x, split_y, n_q).transpose(1, 3, 0, 2, 4)
     sent = sent.reshape(count_y, split_y * levels * piece_x, n_q)
     columns = lax.all_to_all(sent, "gy", split_axis=0, concat_axis=0, tiled=True)
-    columns = columns.reshape(n_p, levels, piece_x, n_q)
+    columns = columns.reshape(n_p, levels * piece_x, n_q)
     w1, t1c, t1s, w2 = y_tables(n_p, n_q)
     stage1 = lax.dot_general(
         const(w1), columns, (((1,), (0,)), ((), ())), precision=PREC
     )
     real1 = stage1[:n_p]
     imag1 = stage1[n_p:]
-    tc = const(t1c)[:, None, None, :]
-    ts = const(t1s)[:, None, None, :]
+    tc = const(t1c)[:, None, :]
+    ts = const(t1s)[:, None, :]
     real_t = real1 * tc + imag1 * ts
     imag_t = imag1 * tc - real1 * ts
     rows_m = levels * n_p * piece_x

time: 104 us -> 104 us (level)
  no operation moved by 1% of the time
where the time goes in v10:
time: 104 us; the launch traced here: 103 us
  waiting for transfers between devices  34.9 us (34%)
  starting transfers between devices  25.4 us (24%)
  other arithmetic  16.4 us (16%)
  blocking collectives  11.7 us (11%)
  local copies, waits for them, and re-layouts  9.76 us (9%)
  matrix products  4.13 us (4%)
    all_to_all x1, waiting for transfers between devices, body(): lax.all_to_all(spectrum_y, ('gx', 'gy'), split_axis=0, concat_axis=0, til...  24.4 us
    all_to_all x1, blocking collectives, body(): lax.all_to_all(sent, 'gy', split_axis=0, concat_axis=0, tiled=True)  11.7 us
    all_to_all x1, starting transfers between devices, body(): lax.all_to_all(spectrum_y, ('gx', 'gy'), split_axis=0, concat_axis=0, til...  10.8 us
    ppermute x1, starting transfers between devices, body(): y_after = lax.ppermute(masked_part(all_x, slice(0, 3)), 'gy', down_y)  6 us
    ppermute x1, waiting for transfers between devices, body(): v_before = lax.ppermute(flow_v[:, :, rows_y - 1:], 'gy', up_y)  5.48 us
    another operation x2, other arithmetic, body(): tendency = jnp.stack(pieces)  5.4 us
    add x3, other arithmetic, body(): flows.append(center[component] + DT * rounded[component])  5.01 us
    ppermute x1, waiting for transfers between devices, body(): lax.ppermute(masked_part(all_x, slice(rows_y - 3, rows_y)), 'gy', up_y)  4.85 us
  transfers between devices with their start and end apart: 9, of which 4 were waited for; matrix products, arithmetic and copies ran while one was open for 12% of the time, Pallas kernels for 0%

profile of v10, /device:TPU:1, one launch (start us, length us, event | category | flops | bytes accessed | tf_op | source)
XLA Modules:
  0.0 103.3 jit_solution(7344599622496956429)
XLA Ops:
  0.6 0.0 copy-start.3
  0.6 1.0 %fusion.130 = (s32[128,3]{1,0:T(8,128)S(1)}, s32[128,3]{1,0:T(8,128)S(1)}) fusion(s32[128,512]{1,0:T(8,128)} %param.12), kind=kLoop, calls=%fused_computation.203 | loop fusion | bytes 6144 | tf_op jit(solution)/shard_map/slice | solution.py:120
  1.7 1.2 %slice_multiply_fusion.1 = (bf16[4,2,128,3]{3,2,1,0:T(8,128)(2,1)S(1)}, bf16[4,2,128,3]{3,2,1,0:T(8,128)(2,1)S(1)}) fusion(bf16[4,2,128,512]{3,2,1,0:T(8,128)(2,1)} %param.11, bf16[2,128,3]{2,1,0:T(8,128)(2,1)S(1)} %get-tuple-element.40, bf16[2,128,3]{2,1,0:T(8,128)(2,1)S(1)} %get-tuple-element.41), kind=kLoop, calls=%fused_computation.182 | loop fusion | flops 6144 | bytes 27648 | tf_op jit(solution)/shard_map/mul | solution.py:121
  2.9 6.0 %collective-permute-start.3 = (bf16[4,2,128,3]{3,2,1,0:T(8,128)(2,1)S(1)}, bf16[4,2,128,3]{3,2,1,0:T(8,128)(2,1)S(1)}, u32[]{:S(2)}, u32[]{:S(2)}) collective-permute-start(bf16[4,2,128,3]{3,2,1,0:T(8,128)(2,1)S(1)} %get-tuple-element.25), channel_id=1, source_target_pairs={{1,0},{2,1},{3,2},{4,3},{5,4},{6,5},{7,6},{0,7},{9,8},{10,9},{11,1... | collective-permute-start | bytes 18440 | tf_op jit(solution)/shard_map/ppermute | solution.py:127
  8.9 0.0 collective-permute-start.2
  8.9 0.7 fusion.129
  9.7 0.9 slice_multiply_fusion.3
  10.6 1.0 %collective-permute-start.1 = (bf16[4,2,3,512]{3,2,1,0:T(4,128)(2,1)S(1)}, bf16[4,2,3,512]{3,2,1,0:T(4,128)(2,1)S(1)}, u32[]{:S(2)}, u32[]{:S(2)}) collective-permute-start(bf16[4,2,3,512]{3,2,1,0:T(4,128)(2,1)S(1)} %get-tuple-element.23), channel_id=1, source_target_pairs={{8,0},{16,8},{24,16},{32,24},{40,32},{48,40},{56,48},{64,56},{72,6... | collective-permute-start | bytes 73736 | tf_op jit(solution)/shard_map/ppermute | solution.py:125
  11.6 0.8 collective-permute-start
  12.4 1.0 convert_convert_fusion
  13.4 0.0 copy-done.3
  13.4 0.2 fusion.123
  13.7 1.2 %slice_bitcast_fusion.18 = (f32[1,128,512]{2,1,0:T(8,128)S(1)}, f32[1,128,512]{2,1,0:T(8,128)}, f32[1,128,512]{2,1,0:T(8,128)}, f32[1,128,512]{2,1,0:T(8,128)S(1...) fusion(f32[4,2,128,512]{3,2,1,0:T(8,128)S(1)} %get-tuple-element.8), kind=kLoop, calls=%fused_computation.176 | loop fusion | bytes 4194304 | tf_op jit(solution)/shard_map/slice | solution.py:25
  14.9 0.0 collective-permute-done.3
  14.9 4.9 %collective-permute-done.2 = bf16[4,2,128,3]{3,2,1,0:T(8,128)(2,1)S(1)} collective-permute-done((bf16[4,2,128,3]{3,2,1,0:T(8,128)(2,1)S(1)}, bf16[4,2,128,3]{3,2,1,0:T(8,128)(2,1)S(1)}, u32[]{:S(2)}, u32[]{:S(2)}) %collective-permute-start.2) | collective-permute-done | bytes 6176 | tf_op jit(solution)/shard_map/ppermute | solution.py:126
  19.7 0.7 maximum_convert_fusion
  20.4 0.0 copy-start.2
  20.4 0.0 collective-permute-done.1
  20.4 0.0 collective-permute-done
  20.4 0.3 maximum_convert_fusion.1
  20.8 0.8 copy-done.2
  21.6 1.7 %multiply_add_fusion.4 = (f32[2,128,512]{2,1,0:T(8,128)S(1)}, bf16[2,128,512]{2,1,0:T(8,128)(2,1)}) fusion(f32[4,2,128,512]{3,2,1,0:T(8,128)S(1)} %get-tuple-element.8, f32[4,2,128,518]{3,2,1,0:T(8,128)S(1)} %maximum_convert_fusion, f32[4,2,134,512]{3,2,1,0:T(8,128)S(1)} %maximum_convert_fusion.1, f32[1,128,512]{2,1,0:T(8,128)S(1)} %get-tuple-element.17, ...), kind=kLoop, calls=%fused_computation.164 | loop fusion | flops 5242880 | bytes 9437184 | tf_op jit(solution)/shard_map/add | solution.py:148
  23.2 0.1 fusion.128
  23.3 1.6 %multiply_add_fusion.3 = (f32[2,128,512]{2,1,0:T(8,128)S(1)}, bf16[2,128,512]{2,1,0:T(8,128)(2,1)}) fusion(f32[4,2,128,512]{3,2,1,0:T(8,128)S(1)} %get-tuple-element.8, f32[4,2,128,518]{3,2,1,0:T(8,128)S(1)} %maximum_convert_fusion, f32[4,2,134,512]{3,2,1,0:T(8,128)S(1)} %maximum_convert_fusion.1, f32[1,128,512]{2,1,0:T(8,128)S(1)} %get-tuple-element.15, ...), kind=kLoop, calls=%fused_computation.163 | loop fusion | flops 5242880 | bytes 9437184 | tf_op jit(solution)/shard_map/add | solution.py:148
  25.0 0.1 fusion.125
  25.1 0.2 fusion.126
  25.3 1.9 %collective-permute-start.4 = (f32[2,1,512]{2,1,0:T(1,128)S(1)}, f32[2,1,512]{2,1,0:T(1,128)S(1)}, u32[]{:S(2)}, u32[]{:S(2)}) collective-permute-start(f32[2,1,512]{2,1,0:T(1,128)S(1)} %get-tuple-element.33), channel_id=1, source_target_pairs={{8,0},{16,8},{24,16},{32,24},{40,32},{48,40},{56,48},{64,56},{72,6... | collective-permute-start | bytes 12296 | tf_op jit(solution)/shard_map/ppermute | solution.py:151
  27.2 0.0 collective-permute-start.5
  27.2 4.8 %collective-permute-start.6 = (f32[2,128,1]{2,1,0:T(8,128)S(1)}, f32[2,128,1]{2,1,0:T(8,128)S(1)}, u32[]{:S(2)}, u32[]{:S(2)}) collective-permute-start(f32[2,128,1]{2,1,0:T(8,128)S(1)} %get-tuple-element.29), channel_id=1, source_target_pairs={{1,0},{2,1},{3,2},{4,3},{5,4},{6,5},{7,6},{0,7},{9,8},{10,9},{11,1... | collective-permute-start | bytes 3080 | tf_op jit(solution)/shard_map/ppermute | solution.py:153
  32.1 0.0 collective-permute-start.7
  32.1 1.7 %multiply_add_fusion.2 = (f32[2,128,512]{2,1,0:T(8,128)S(1)}, bf16[2,128,512]{2,1,0:T(8,128)(2,1)}) fusion(f32[4,2,128,512]{3,2,1,0:T(8,128)S(1)} %get-tuple-element.8, f32[4,2,128,518]{3,2,1,0:T(8,128)S(1)} %maximum_convert_fusion, f32[4,2,134,512]{3,2,1,0:T(8,128)S(1)} %maximum_convert_fusion.1, f32[1,128,512]{2,1,0:T(8,128)S(1)} %get-tuple-element.13, ...), kind=kLoop, calls=%fused_computation.162 | loop fusion | flops 5505024 | bytes 9961472 | tf_op jit(solution)/shard_map/add | solution.py:148
  33.8 0.2 collective-permute-done.6
  34.0 5.5 %collective-permute-done.7 = f32[2,128,1]{2,1,0:T(8,128)S(1)} collective-permute-done((f32[2,128,1]{2,1,0:T(8,128)S(1)}, f32[2,128,1]{2,1,0:T(8,128)S(1)}, u32[]{:S(2)}, u32[]{:S(2)}) %collective-permute-start.7) | collective-permute-done | bytes 1056 | tf_op jit(solution)/shard_map/ppermute | solution.py:152
  39.5 0.0 collective-permute-done.4
  39.5 0.0 collective-permute-done.5
  39.5 0.3 fusion.102
  39.8 0.0 copy-start.9
  39.9 0.3 reshape.136
  40.2 0.0 copy-start.10
  40.2 0.1 copy.24
  40.3 11.7 %all_to_all.10 = f32[8,64,256]{2,1,0:T(8,128)S(1)} all-to-all(f32[8,64,256]{2,1,0:T(8,128)S(1)} %bitcast.305), channel_id=1, replica_groups=mesh['gx'=32,'gy'=8] {'gy'}, dimensions={0} | all-to-all | bytes 1048576 | tf_op jit(solution)/shard_map/all_to_all | solution.py:167
  52.0 1.4 %fusion.110 = f32[32,32,256]{2,0,1:T(8,128)S(1)} fusion(f32[32,16,1]{0,1,2:T(8,128)} %constant.67, f32[16,32,256]{2,1,0:T(8,128)S(1)} %bitcast.303), kind=kOutput, calls=%fused_computation.156 | convolution fusion | flops 25165824 | bytes 1574912 | tf_op jit(solution)/shard_map/dot_general | solution.py:170
  53.4 0.0 copy-start.5
  53.4 0.2 multiply_add_fusion.1
  53.6 0.3 copy.27
  53.9 0.3 copy.26
  54.2 0.4 copy-done.5
  54.7 1.0 fusion
  55.7 1.8 %copy.28 = f32[256,2,512]{2,1,0:T(2,128)} copy(f32[256,2,512]{2,0,1:T(8,128)S(1)} %fusion) | data formatting | bytes 2097152 | tf_op jit(solution)/shard_map/dot_general | solution.py:184
  57.5 10.8 %all-to-all-start.1 = ((f32[256,2,512]{2,1,0:T(2,128)}), f32[256,2,512]{2,1,0:T(2,128)S(1)}, u32[]{:S(2)}, u32[]{:S(2)}) async-start(f32[256,2,512]{2,1,0:T(2,128)} %copy.28), calls=%async_computation.1 | async-start | bytes 2097152 | tf_op jit(solution)/shard_map/all_to_all | solution.py:187
  68.3 1.0 convert_element_type.80
  69.3 4.3 %fusion.113 = bf16[1,2,128,512]{3,2,1,0:T(8,128)(2,1)S(1)} fusion(f32[128,512]{1,0:T(8,128)S(1)} %convert_element_type.80, f32[4,2,128,512]{3,2,1,0:T(8,128)} %copy-done.1, f32[4,2,128,518]{3,2,1,0:T(8,128)} %copy-done, f32[4,2,134,512]{3,2,1,0:T(8,128)S(1)} %maximum_convert_fusion.1, f32[1,128,512]{2,1,0:T(8,128)} %get-tuple-element.11, ...), kind=kLoop, calls=%fused_computation.183 | loop fusion | flops 5242880 | bytes 9699328 | tf_op jit(solution)/shard_map/stack | solution.py:144
  73.6 0.0 copy-start.4
  73.6 0.0 copy-done.6
  73.6 0.0 copy-done.7
  73.6 0.0 copy-done.8
  73.6 0.0 copy-start.11
  73.7 1.1 %pad_maximum_fusion = bf16[4,2,128,512]{3,2,1,0:T(8,128)(2,1)} fusion(bf16[1,2,128,512]{3,2,1,0:T(8,128)(2,1)S(1)} %fusion.113, bf16[1,2,128,512]{3,2,1,0:T(8,128)(2,1)S(1)} %bitcast.310, bf16[1,2,128,512]{3,2,1,0:T(8,128)(2,1)S(1)} %bitcast.309, bf16[1,2,128,512]{3,2,1,0:T(8,128)(2,1)S(1)} %bitcast.308), kind=kLoop, calls=%fused_computation.2 | loop fusion | flops 1572864 | bytes 2097152 | tf_op jit(solution)/shard_map/stack | solution.py:144
  74.8 24.4 %all-to-all-done.1 = f32[256,2,512]{2,1,0:T(2,128)S(1)} async-done(((f32[256,2,512]{2,1,0:T(2,128)}), f32[256,2,512]{2,1,0:T(2,128)S(1)}, u32[]{:S(2)}, u32[]{:S(2)}) %all-to-all-start.1) | async-done | bytes 1048608 | tf_op jit(solution)/shard_map/all_to_all | solution.py:187
  99.1 1.1 %fusion.7 = f32[512,512,1]{1,0,2:T(8,128)S(1)} fusion(f32[256,2,512]{2,0,1:T(8,128)S(1)} %copy-done.4, f32[256,2,512]{2,1,0:T(2,128)S(1)} %all-to-all-done.1), kind=kOutput, calls=%fused_computation.11 | convolution fusion | flops 805306368 | bytes 3145728 | tf_op jit(solution)/shard_map/dot_general | solution.py:194
  100.2 0.2 multiply_add_fusion
  100.4 0.6 fusion.3
  101.0 0.7 reshape.155
  101.7 1.6 %copy.31 = f32[2,2,16,4096]{3,2,1,0:T(8,128)} copy(f32[2,2,16,4096]{3,0,1,2:T(2,128)S(1)} %reshape.155) | data formatting | bytes 2097152 | tf_op jit(solution)/shard_map/reshape | solution.py:211
  (17 shorter events, 0.1 us)
Async XLA Ops:
  0.6 12.8 %copy-start.3 = (bf16[4,2,128,512]{3,2,1,0:T(8,128)(2,1)S(1)}, bf16[4,2,128,512]{3,2,1,0:T(8,128)(2,1)}, u32[]{:S(2)}) copy-start(bf16[4,2,128,512]{3,2,1,0:T(8,128)(2,1)} %param.11) | copy-start | bytes 3145732
  2.9 12.0 %collective-permute-start.3 = (bf16[4,2,128,3]{3,2,1,0:T(8,128)(2,1)S(1)}, bf16[4,2,128,3]{3,2,1,0:T(8,128)(2,1)S(1)}, u32[]{:S(2)}, u32[]{:S(2)}) collective-permute-start(bf16[4,2,128,3]{3,2,1,0:T(8,128)(2,1)S(1)} %get-tuple-element.25), channel_id=1, source_target_pairs={{1,0},{2,1},{3,2},{4,3},{5,4},{6,5},{7,6},{0,7},{9,8},{10,9},{11,1... | collective-permute-start | bytes 18440 | tf_op jit(solution)/shard_map/ppermute | solution.py:127
  8.9 10.8 %collective-permute-start.2 = (bf16[4,2,128,3]{3,2,1,0:T(8,128)(2,1)S(1)}, bf16[4,2,128,3]{3,2,1,0:T(8,128)(2,1)S(1)}, u32[]{:S(2)}, u32[]{:S(2)}) collective-permute-start(bf16[4,2,128,3]{3,2,1,0:T(8,128)(2,1)S(1)} %get-tuple-element.24), channel_id=1, source_target_pairs={{0,1},{1,2},{2,3},{3,4},{4,5},{5,6},{6,7},{7,0},{8,9},{9,10},{10,1... | collective-permute-start | bytes 18440 | tf_op jit(solution)/shard_map/ppermute | solution.py:126
  10.6 9.8 %collective-permute-start.1 = (bf16[4,2,3,512]{3,2,1,0:T(4,128)(2,1)S(1)}, bf16[4,2,3,512]{3,2,1,0:T(4,128)(2,1)S(1)}, u32[]{:S(2)}, u32[]{:S(2)}) collective-permute-start(bf16[4,2,3,512]{3,2,1,0:T(4,128)(2,1)S(1)} %get-tuple-element.23), channel_id=1, source_target_pairs={{8,0},{16,8},{24,16},{32,24},{40,32},{48,40},{56,48},{64,56},{72,6... | collective-permute-start | bytes 73736 | tf_op jit(solution)/shard_map/ppermute | solution.py:125
  11.6 8.8 %collective-permute-start = (bf16[4,2,3,512]{3,2,1,0:T(4,128)(2,1)S(1)}, bf16[4,2,3,512]{3,2,1,0:T(4,128)(2,1)S(1)}, u32[]{:S(2)}, u32[]{:S(2)}) collective-permute-start(bf16[4,2,3,512]{3,2,1,0:T(4,128)(2,1)S(1)} %get-tuple-element.22), channel_id=1, source_target_pairs={{0,8},{8,16},{16,24},{24,32},{32,40},{40,48},{48,56},{56,64},{64,7... | collective-permute-start | bytes 73736 | tf_op jit(solution)/shard_map/ppermute | solution.py:124
  13.6 18.4 %copy-start.1 = (f32[4,2,128,512]{3,2,1,0:T(8,128)}, f32[4,2,128,512]{3,2,1,0:T(8,128)S(1)}, u32[]{:S(2)}) copy-start(f32[4,2,128,512]{3,2,1,0:T(8,128)S(1)} %get-tuple-element.8) | copy-start | bytes 6291460
  20.4 11.7 %copy-start = (f32[4,2,128,518]{3,2,1,0:T(8,128)}, f32[4,2,128,518]{3,2,1,0:T(8,128)S(1)}, u32[]{:S(2)}) copy-start(f32[4,2,128,518]{3,2,1,0:T(8,128)S(1)} %maximum_convert_fusion) | copy-start | bytes 6365188
  20.4 1.1 %copy-start.2 = (s32[128,512]{1,0:T(8,128)S(1)}, s32[128,512]{1,0:T(8,128)}, u32[]{:S(2)}) copy-start(s32[128,512]{1,0:T(8,128)} %param.12) | copy-start | bytes 786436
  25.3 14.2 %collective-permute-start.4 = (f32[2,1,512]{2,1,0:T(1,128)S(1)}, f32[2,1,512]{2,1,0:T(1,128)S(1)}, u32[]{:S(2)}, u32[]{:S(2)}) collective-permute-start(f32[2,1,512]{2,1,0:T(1,128)S(1)} %get-tuple-element.33), channel_id=1, source_target_pairs={{8,0},{16,8},{24,16},{32,24},{40,32},{48,40},{56,48},{64,56},{72,6... | collective-permute-start | bytes 12296 | tf_op jit(solution)/shard_map/ppermute | solution.py:151
  27.2 12.3 %collective-permute-start.5 = (f32[2,1,512]{2,1,0:T(1,128)S(1)}, f32[2,1,512]{2,1,0:T(1,128)S(1)}, u32[]{:S(2)}, u32[]{:S(2)}) collective-permute-start(f32[2,1,512]{2,1,0:T(1,128)S(1)} %get-tuple-element.32), channel_id=1, source_target_pairs={{0,8},{8,16},{16,24},{24,32},{32,40},{40,48},{48,56},{56,64},{64,7... | collective-permute-start | bytes 12296 | tf_op jit(solution)/shard_map/ppermute | solution.py:150
  27.2 6.8 %collective-permute-start.6 = (f32[2,128,1]{2,1,0:T(8,128)S(1)}, f32[2,128,1]{2,1,0:T(8,128)S(1)}, u32[]{:S(2)}, u32[]{:S(2)}) collective-permute-start(f32[2,128,1]{2,1,0:T(8,128)S(1)} %get-tuple-element.29), channel_id=1, source_target_pairs={{1,0},{2,1},{3,2},{4,3},{5,4},{6,5},{7,6},{0,7},{9,8},{10,9},{11,1... | collective-permute-start | bytes 3080 | tf_op jit(solution)/shard_map/ppermute | solution.py:153
  32.1 7.4 %collective-permute-start.7 = (f32[2,128,1]{2,1,0:T(8,128)S(1)}, f32[2,128,1]{2,1,0:T(8,128)S(1)}, u32[]{:S(2)}, u32[]{:S(2)}) collective-permute-start(f32[2,128,1]{2,1,0:T(8,128)S(1)} %get-tuple-element.28), channel_id=1, source_target_pairs={{0,1},{1,2},{2,3},{3,4},{4,5},{5,6},{6,7},{7,0},{8,9},{9,10},{10,1... | collective-permute-start | bytes 3080 | tf_op jit(solution)/shard_map/ppermute | solution.py:152
  39.8 13.6 %copy-start.9 = (f32[16,256]{1,0:T(8,128)S(1)}, f32[16,256]{1,0:T(8,128)}, u32[]{:S(2)}) copy-start(f32[16,256]{1,0:T(8,128)} %constant.43.clone) | copy-start | bytes 49156
  40.2 13.2 %copy-start.10 = (f32[16,256]{1,0:T(8,128)S(1)}, f32[16,256]{1,0:T(8,128)}, u32[]{:S(2)}) copy-start(f32[16,256]{1,0:T(8,128)} %constant.42.clone) | copy-start | bytes 49156
  53.4 1.2 %copy-start.5 = (f32[256,2,512]{2,0,1:T(8,128)S(1)}, f32[256,2,512]{2,0,1:T(8,128)}, u32[]{:S(2)}) copy-start(f32[256,2,512]{2,0,1:T(8,128)} %constant.44.clone) | copy-start | bytes 3145732
  57.5 41.6 %all-to-all-start.1 = ((f32[256,2,512]{2,1,0:T(2,128)}), f32[256,2,512]{2,1,0:T(2,128)S(1)}, u32[]{:S(2)}, u32[]{:S(2)}) async-start(f32[256,2,512]{2,1,0:T(2,128)} %copy.28), calls=%async_computation.1 | async-start | bytes 2097152 | tf_op jit(solution)/shard_map/all_to_all | solution.py:187
  69.3 4.3 %copy-start.6 = (bf16[2,128,512]{2,1,0:T(8,128)(2,1)S(1)}, bf16[2,128,512]{2,1,0:T(8,128)(2,1)}, u32[]{:S(2)}) copy-start(bf16[2,128,512]{2,1,0:T(8,128)(2,1)} %get-tuple-element.7) | copy-start | bytes 786436
  69.3 4.3 %copy-start.7 = (bf16[2,128,512]{2,1,0:T(8,128)(2,1)S(1)}, bf16[2,128,512]{2,1,0:T(8,128)(2,1)}, u32[]{:S(2)}) copy-start(bf16[2,128,512]{2,1,0:T(8,128)(2,1)} %get-tuple-element.5) | copy-start | bytes 786436
  69.3 4.3 %copy-start.8 = (bf16[2,128,512]{2,1,0:T(8,128)(2,1)S(1)}, bf16[2,128,512]{2,1,0:T(8,128)(2,1)}, u32[]{:S(2)}) copy-start(bf16[2,128,512]{2,1,0:T(8,128)(2,1)} %get-tuple-element.3) | copy-start | bytes 786436
  73.6 25.5 %copy-start.4 = (f32[256,2,512]{2,0,1:T(8,128)S(1)}, f32[256,2,512]{2,0,1:T(8,128)}, u32[]{:S(2)}) copy-start(f32[256,2,512]{2,0,1:T(8,128)} %constant.45.clone) | copy-start | bytes 3145732
  73.6 26.6 %copy-start.11 = (f32[16,256]{1,0:T(8,128)S(1)}, f32[16,256]{1,0:T(8,128)}, u32[]{:S(2)}) copy-start(f32[16,256]{1,0:T(8,128)} %constant.42.clone) | copy-start | bytes 49156
  74.8 25.7 %copy-start.12 = (f32[32,32]{1,0:T(8,128)S(1)}, f32[32,32]{1,0:T(8,128)}, u32[]{:S(2)}) copy-start(f32[32,32]{1,0:T(8,128)} %constant.46.clone) | copy-start | bytes 12292
